TPU v7x, 256 devices: a whole 4x4x8 slice. The times are simulated.
256 devices in a mesh: shot: 32 (over x, y, z_lo), sp: 8 (over z_hi, core).
Axes of the slice: x: 4, y: 4, z: 8 (z_hi: 4, z_lo: 2; z = z_hi * 2 + z_lo), core: 2. Of those that a mesh axis runs over, the one named last changes fastest.
Arguments:
- shot_data: bfloat16 [2, 8, 12288, 4096], P(None, None, 'shot', 'sp'), may hold values from -6 to 6
- live_masks: int32 [12288, 4096], P('shot', 'sp'), may hold values 0 or 1
- spectra: bfloat16 [128, 2, 8, 1024, 256], P('shot', None, None, 'sp'), may hold values from -0.09375 to 0.09375
- plan: int32 [4, 8], replicated, may hold values from 0 to 31, as said below
Outputs:
- multiples: bfloat16 [12288, 2, 8, 256], P(('shot', 'sp'))
Inputs may be any that keep to these rules, and one draw needn't show every extreme that they name: `plan`: all 4 x 8 owners are distinct shot indices; 0 and the last index both occur.
All inputs are finite; a program needn't handle non-finite values. No bound on the sum of `live_masks` on one device may be relied on, other than what follows from the above.
Results may differ from a plain program's by a relative error of at most 0.001.
Values may be sent and summed in bfloat16 or wider, within the bound.
No kernel may reach another device: no remote copies, remote signals or barrier semaphores. Data moves between devices by JAX's collectives and lax.ppermute only.
A program may use at most 128 MiB of HBM per device.

v0:
```python
import jax
import jax.numpy as jnp
from jax import lax
from jax.sharding import PartitionSpec as P

STEPS = 4


def from_root(shard, axis, root):
    mine = lax.axis_index(axis) == root
    return lax.psum(jnp.where(mine, shard, jnp.zeros_like(shard)), axis)


def body(shot_data, live_masks, spectra, plan):
    width = spectra.shape[3]
    sp_index = lax.axis_index("sp")
    live = shot_data * live_masks.astype(shot_data.dtype)[None, None]
    totals = None
    for section in range(STEPS):
        owner = lax.dynamic_index_in_dim(plan[section], sp_index, 0, keepdims=False)
        recv = from_root(spectra[section], "shot", owner)
        window = live[:, :, :, section * width : (section + 1) * width]
        real_part = jnp.einsum(
            "fsk,fkr->sfr", window[0], recv[0], preferred_element_type=jnp.float32
        ) - jnp.einsum("fsk,fkr->sfr", window[1], recv[1], preferred_element_type=jnp.float32)
        imag_part = jnp.einsum(
            "fsk,fkr->sfr", window[0], recv[1], preferred_element_type=jnp.float32
        ) + jnp.einsum("fsk,fkr->sfr", window[1], recv[0], preferred_element_type=jnp.float32)
        piece = jnp.stack([real_part, imag_part], axis=1)
        totals = piece if totals is None else totals + piece
    return lax.psum_scatter(totals, "sp", scatter_dimension=0, tiled=True).astype(jnp.bfloat16)


def solution(mesh):
    in_specs = (
        P(None, None, "shot", "sp"),
        P("shot", "sp"),
        P("shot", None, None, "sp", None),
        P(),
    )
    out_specs = P(("shot", "sp"), None, None, None)
    return jax.shard_map(body, mesh=mesh, in_specs=in_specs, out_specs=out_specs, check_vma=False)
```

profile of v0, /device:TPU:6, one launch (start us, length us, event | category | flops | bytes accessed | tf_op | source)
XLA Modules:
  0.0 483.5 jit_solution(7400817069628201796)
XLA Ops:
  6.5 0.8 fusion.11
  7.4 0.6 constant_dynamic-slice_fusion
  9.3 0.6 constant_dynamic-slice_fusion.2
  11.2 3.5 fusion.10
  14.7 1.3 copy.18
  16.0 0.7 copy.17
  16.6 0.7 copy.16
  17.3 1.6 copy.15
  18.9 1.1 select_bitcast_fusion
  20.0 1.1 select_bitcast_fusion.1
  21.1 1.1 select_bitcast_fusion.2
  22.2 1.1 select_bitcast_fusion.3
  23.4 6.3 %broadcast_multiply_fusion = bf16[2,8,384,512]{3,2,1,0:T(8,128)(2,1)} fusion(bf16[2,8,384,512]{3,2,1,0:T(8,128)(2,1)} %param.4, bf16[384,512]{1,0:T(8,128)(2,1)S(1)} %convert_element_type.6), kind=kLoop, calls=%fused_computation.11 | loop fusion | flops 3145728 | bytes 12976128 | tf_op jit(solution)/shard_map/mul | solution.py:17
  29.7 328.4 %all-reduce.3.cloned.1.call-done = (bf16[2,8,128,256]{2,3,1,0:T(8,128)(2,1)}, bf16[2,8,128,256]{2,3,1,0:T(8,128)(2,1)}, bf16[2,8,128,256]{2,3,1,0:T(8,128)(2,1)}, bf16[2,8,128,256]{2,3,1,0:T(8,128)(2,1)}) async-done(((bf16[2,8,128,256]{2,3,1,0:T(8,128)(2,1)}, bf16[2,8,128,256]{2,3,1,0:T(8,128)(2,1)}, bf16[2,8,128,256]{2,3,1,0:T(8,128)(2,1)}, bf16[2,8,128,256]{2,3,1,0:T(8,128)(2,1)}), ...) | async-done | bytes 4194320 | tf_op jit(solution)/shard_map/psum | solution.py:11
  358.1 2.0 fusion.8
  360.1 2.5 fusion.9
  366.8 0.6 add_bitcast_fusion.1
  368.5 0.6 subtract_bitcast_fusion
  369.1 0.6 subtract_bitcast_fusion.1
  370.3 2.3 subtract_bitcast_fusion.3
  372.6 4.8 fusion.1
  377.4 6.7 %copy.14 = f32[384,2,8,256]{3,2,1,0:T(8,128)} copy(f32[384,2,8,256]{0,3,2,1:T(8,128)} %fusion.1) | data formatting | bytes 12582912 | tf_op jit(solution)/shard_map/add | solution.py:30
  384.1 90.6 %reduce-scatter.2.cloned.1.call-done = f32[48,2,8,256]{3,2,1,0:T(8,128)} async-done(((f32[384,2,8,256]{3,2,1,0:T(8,128)}), f32[48,2,8,256]{3,2,1,0:T(8,128)}) %reduce-scatter.2.cloned.1.call-update) | async-done | bytes 786448 | tf_op jit(solution)/shard_map/reduce_scatter | solution.py:31
  474.7 1.9 convert_element_type.7
  (27 shorter events, 6.0 us)
Async XLA Ops:
  6.5 351.5 %all-reduce.3.cloned.1.call-start = ((), (), s32[]{:S(2)}) async-start(), calls=%async_computation.2 | async-start | bytes 8388608 | tf_op jit(solution)/shard_map/psum | solution.py:11
  21.1 2.2 copy-start.5
  23.3 451.5 %reduce-scatter.2.cloned.1.call-start = ((), (), s32[]{:S(2)}) async-start(), calls=%async_computation.1 | async-start | bytes 7077888 | tf_op jit(solution)/shard_map/reduce_scatter | solution.py:31
  358.1 2.0 copy-start.4
  358.1 4.5 copy-start
  358.1 4.5 copy-start.3
  362.6 1.2 copy-start.2
  363.8 1.2 copy-start.1
Sparse Core Ops, SparseCore 0:
  23.4 334.6 all-reduce.2
  384.2 90.4 reduce-scatter.1
where the time goes:
time: 484 us
  waiting for transfers between devices  419 us (87%)
  other arithmetic  17.4 us (4%)
  local copies, waits for them, and re-layouts  16.7 us (3%)
  between operations  16.1 us (3%)
  matrix products  14.2 us (3%)
    psum x1, waiting for transfers between devices, from_root(): return lax.psum(jnp.where(mine, shard, jnp.zeros_like(shard)), axis)  328 us
    reduce_scatter x1, waiting for transfers between devices, body(): lax.psum_scatter(totals, 'sp', scatter_dimension=0, tiled=True)  90.6 us
  transfers between devices with their start and end apart: 2, of which 2 were waited for; matrix products, arithmetic and copies ran while one was open for 1% of the time, Pallas kernels for 0%

commit v1 on v0

v1 whole, which is shorter than its diff:
```python
import jax
import jax.numpy as jnp
from jax import lax
from jax.sharding import Mesh, PartitionSpec as P

STEPS = 4
SHOT = ("x", "y", "zl")
SP = ("zh", "c")


def gather_receivers(spectra, plan):
    n_shot = lax.psum(1, SHOT)
    sp_index = lax.axis_index(SP)
    shot_index = lax.axis_index(SHOT)
    column = lax.dynamic_index_in_dim(plan, sp_index, 1, keepdims=False)
    mine = column == shot_index
    owned_step = jnp.argmax(mine)
    block = lax.dynamic_index_in_dim(spectra, owned_step, 0, keepdims=False)
    parts, freq, kb, recv = block.shape
    split = n_shot // (parts * freq)
    pieces = block.reshape(parts * freq * split, kb // split, recv)
    got = lax.all_to_all(pieces, SHOT, 0, 0, tiled=True)
    chosen = jnp.take(got, column, axis=0)
    full = lax.all_gather(chosen, SHOT, axis=0, tiled=False)
    full = full.reshape(parts, freq, split, STEPS, kb // split, recv)
    full = jnp.transpose(full, (3, 0, 1, 2, 4, 5)).reshape(STEPS, parts, freq, kb, recv)
    return full


def body(shot_data, live_masks, spectra, plan):
    width = spectra.shape[3]
    live = shot_data * live_masks.astype(shot_data.dtype)[None, None]
    recv_all = gather_receivers(spectra, plan)
    totals = None
    for section in range(STEPS):
        recv = recv_all[section]
        window = live[:, :, :, section * width : (section + 1) * width]
        real_part = jnp.einsum(
            "fsk,fkr->sfr", window[0], recv[0], preferred_element_type=jnp.float32
        ) - jnp.einsum("fsk,fkr->sfr", window[1], recv[1], preferred_element_type=jnp.float32)
        imag_part = jnp.einsum(
            "fsk,fkr->sfr", window[0], recv[1], preferred_element_type=jnp.float32
        ) + jnp.einsum("fsk,fkr->sfr", window[1], recv[0], preferred_element_type=jnp.float32)
        piece = jnp.stack([real_part, imag_part], axis=1)
        totals = piece if totals is None else totals + piece
    return lax.psum_scatter(totals, SP, scatter_dimension=0, tiled=True).astype(jnp.bfloat16)


def solution(mesh):
    n_shot = mesh.shape["shot"]
    n_sp = mesh.shape["sp"]
    devices = mesh.devices.reshape(n_shot // 8, 4, 2, n_sp // 2, 2)
    fine = Mesh(devices, ("x", "y", "zl", "zh", "c"))
    in_specs = (
        P(None, None, SHOT, SP),
        P(SHOT, SP),
        P(SHOT, None, None, SP, None),
        P(),
    )
    out_specs = P(SHOT + SP, None, None, None)
    return jax.shard_map(body, mesh=fine, in_specs=in_specs, out_specs=out_specs, check_vma=False)
```

time: 484 us -> 320 us (0.66)
  waiting for transfers between devices: 419 us -> 257 us
  starting transfers between devices: 0.04 us -> 9.04 us
    psum x1 -> x0, waiting for transfers between devices: 328 us -> none  [from_root(): return lax.psum(jnp.where(mine, shard, jnp.zeros_like(shard)), axis)]
    all_gather x0 -> x1, waiting for transfers between devices: none -> 151 us  [gather_receivers(): full = lax.all_gather(chosen, SHOT, axis=0, tiled=False)]
    all_to_all x0 -> x1, waiting for transfers between devices: none -> 15.3 us  [gather_receivers(): got = lax.all_to_all(pieces, SHOT, 0, 0, tiled=True)]
    all_to_all x0 -> x1, starting transfers between devices: none -> 8.96 us  [gather_receivers(): got = lax.all_to_all(pieces, SHOT, 0, 0, tiled=True)]
  transfers between devices with their start and end apart: 2 -> 3, of which waited for: 2 -> 3; matrix products, arithmetic and copies ran while one was open for 1% -> 2% of each run, Pallas kernels for 0% -> 0%
where the time goes in v1:
time: 320 us
  waiting for transfers between devices  257 us (80%)
  between operations  15.6 us (5%)
  other arithmetic  14.2 us (4%)
  local copies, waits for them, and re-layouts  13.6 us (4%)
  matrix products  9.95 us (3%)
  starting transfers between devices  9.04 us (3%)
    all_gather x1, waiting for transfers between devices, gather_receivers(): full = lax.all_gather(chosen, SHOT, axis=0, tiled=False)  151 us
    reduce_scatter x1, waiting for transfers between devices, body(): lax.psum_scatter(totals, SP, scatter_dimension=0, tiled=True)  90.5 us
    all_to_all x1, waiting for transfers between devices, gather_receivers(): got = lax.all_to_all(pieces, SHOT, 0, 0, tiled=True)  15.3 us
    all_to_all x1, starting transfers between devices, gather_receivers(): got = lax.all_to_all(pieces, SHOT, 0, 0, tiled=True)  8.96 us
    add x1, local copies, waits for them, and re-layouts, body(): totals = piece if totals is None else totals + piece  6.71 us
  transfers between devices with their start and end apart: 3, of which 3 were waited for; matrix products, arithmetic and copies ran while one was open for 2% of the time, Pallas kernels for 0%

profile of v1, /device:TPU:6, one launch (start us, length us, event | category | flops | bytes accessed | tf_op | source)
XLA Modules:
  0.0 319.7 jit_solution(10253785052834005150)
XLA Ops:
  6.5 1.0 and_reduce_fusion
  7.5 0.7 iota_reduce_fusion
  10.3 2.3 constant_dynamic-slice_fusion
  12.6 9.0 %all-to-all-start = ((bf16[32,64,256]{2,1,0:T(8,128)(2,1)}), bf16[32,64,256]{2,1,0:T(8,128)(2,1)S(1)}, u32[]{:S(2)}, u32[]{:S(2)}) async-start(bf16[32,64,256]{2,1,0:T(8,128)(2,1)} %bitcast), calls=%async_computation | async-start | bytes 2097152 | tf_op jit(solution)/shard_map/all_to_all | solution.py:22
  21.9 15.3 %all-to-all-done = bf16[32,64,256]{2,1,0:T(8,128)(2,1)S(1)} async-done(((bf16[32,64,256]{2,1,0:T(8,128)(2,1)}), bf16[32,64,256]{2,1,0:T(8,128)(2,1)S(1)}, u32[]{:S(2)}, u32[]{:S(2)}) %all-to-all-start) | async-done | bytes 1048608 | tf_op jit(solution)/shard_map/all_to_all | solution.py:22
  37.8 0.7 bitcast_select_fusion
  38.6 6.3 %broadcast_multiply_fusion = bf16[2,8,384,512]{3,2,1,0:T(8,128)(2,1)} fusion(bf16[2,8,384,512]{3,2,1,0:T(8,128)(2,1)} %param.4, bf16[384,512]{1,0:T(8,128)(2,1)S(1)} %convert_element_type.6), kind=kLoop, calls=%fused_computation.12 | loop fusion | flops 3145728 | bytes 12976128 | tf_op jit(solution)/shard_map/mul | solution.py:32
  44.9 151.5 %all-gather.2.cloned.1.call-done = bf16[32,4,64,256]{3,2,1,0:T(8,128)(2,1)} async-done(((bf16[1,4,64,256]{3,2,1,0:T(8,128)(2,1)}), bf16[32,4,64,256]{3,2,1,0:T(8,128)(2,1)}) %all-gather.2.cloned.1.call-update) | async-done | bytes 4194320 | tf_op jit(solution)/shard_map/all_gather | solution.py:24
  196.4 2.9 fusion.11
  199.3 1.2 copy-done
  201.7 0.6 add_bitcast_fusion
  202.3 0.6 subtract_bitcast_fusion
  203.0 0.6 fusion.6
  203.6 0.6 fusion.7
  204.2 0.6 add_bitcast_fusion.1
  204.9 0.6 subtract_bitcast_fusion.1
  206.7 0.6 add_bitcast_fusion.2
  207.4 0.6 subtract_bitcast_fusion.2
  209.2 0.6 add_bitcast_fusion.3
  209.9 0.6 subtract_bitcast_fusion.3
  210.5 3.3 %fusion.1 = f32[384,2,8,256]{0,3,2,1:T(8,128)} fusion(f32[384,1,8,256]{0,3,2,1:T(8,128)S(1)} %add_bitcast_fusion.3, f32[384,1,8,256]{0,3,2,1:T(8,128)S(1)} %subtract_bitcast_fusion.3, f32[384,1,8,256]{0,3,2,1:T(8,128)S(1)} %add_bitcast_fusion.2, f32[384,1,8,256]{0,3,2,1:T(8,128)S(1)} %subtract_bitcast_fusion.2, f32[384,1,8,256]{0,3,2,1:T(8,128)S(1)} %add_bitcast_fusion.1, ...), kind=kLoop, calls=%fused_computation.3 | loop fusion | flops 11010048 | bytes 31457280 | tf_op jit(solution)/shard_map/add | solution.py:45
  213.8 6.7 %copy.39 = f32[384,2,8,256]{3,2,1,0:T(8,128)} copy(f32[384,2,8,256]{0,3,2,1:T(8,128)} %fusion.1) | data formatting | bytes 12582912 | tf_op jit(solution)/shard_map/add | solution.py:45
  220.5 90.5 %reduce-scatter.2.cloned.1.call-done = f32[48,2,8,256]{3,2,1,0:T(8,128)} async-done(((f32[384,2,8,256]{3,2,1,0:T(8,128)}), f32[48,2,8,256]{3,2,1,0:T(8,128)}) %reduce-scatter.2.cloned.1.call-update) | async-done | bytes 786448 | tf_op jit(solution)/shard_map/reduce_scatter | solution.py:46
  311.0 1.9 convert_element_type.7
  (19 shorter events, 4.6 us)
Async XLA Ops:
  6.5 15.1 %copy-start.2 = (s32[4,8]{1,0:T(4,128)S(1)}, s32[4,8]{1,0:T(4,128)}, u32[]{:S(2)}) copy-start(s32[4,8]{1,0:T(4,128)} %param.7) | copy-start | bytes 388
  6.5 32.0 %copy-start.1 = (s32[384,512]{1,0:T(8,128)S(1)}, s32[384,512]{1,0:T(8,128)}, u32[]{:S(2)}) copy-start(s32[384,512]{1,0:T(8,128)} %param.5) | copy-start | bytes 2359300
  12.6 24.6 %all-to-all-start = ((bf16[32,64,256]{2,1,0:T(8,128)(2,1)}), bf16[32,64,256]{2,1,0:T(8,128)(2,1)S(1)}, u32[]{:S(2)}, u32[]{:S(2)}) async-start(bf16[32,64,256]{2,1,0:T(8,128)(2,1)} %bitcast), calls=%async_computation | async-start | bytes 2097152 | tf_op jit(solution)/shard_map/all_to_all | solution.py:22
  21.6 174.8 %all-gather.2.cloned.1.call-start = ((), (), s32[]{:S(2)}) async-start(), calls=%async_computation.2 | async-start | bytes 4325376 | tf_op jit(solution)/shard_map/all_gather | solution.py:24
  38.5 272.5 %reduce-scatter.2.cloned.1.call-start = ((), (), s32[]{:S(2)}) async-start(), calls=%async_computation.3 | async-start | bytes 7077888 | tf_op jit(solution)/shard_map/reduce_scatter | solution.py:46
  196.4 4.1 %copy-start = (bf16[2,8,384,512]{3,2,1,0:T(8,128)(2,1)S(1)}, bf16[2,8,384,512]{3,2,1,0:T(8,128)(2,1)}, u32[]{:S(2)}) copy-start(bf16[2,8,384,512]{3,2,1,0:T(8,128)(2,1)} %broadcast_multiply_fusion) | copy-start | bytes 18874372
Sparse Core Ops, SparseCore 0:
  38.6 157.7 all-gather.1
  220.6 90.2 reduce-scatter.1

commit v2 on v1

--- a/solution.py
+++ b/solution.py
@@ -21,9 +21,12 @@
     pieces = block.reshape(parts * freq * split, kb // split, recv)
     got = lax.all_to_all(pieces, SHOT, 0, 0, tiled=True)
     chosen = jnp.take(got, column, axis=0)
-    full = lax.all_gather(chosen, SHOT, axis=0, tiled=False)
-    full = full.reshape(parts, freq, split, STEPS, kb // split, recv)
-    full = jnp.transpose(full, (3, 0, 1, 2, 4, 5)).reshape(STEPS, parts, freq, kb, recv)
+    full = lax.all_gather(chosen, "zl", axis=0, tiled=False)
+    full = lax.all_gather(full, "x", axis=0, tiled=False)
+    full = lax.all_gather(full, "y", axis=0, tiled=False)
+    n_y, n_x, n_zl = full.shape[:3]
+    full = full.reshape(n_y, parts, n_x // parts, n_zl, STEPS, kb // split, recv)
+    full = jnp.transpose(full, (4, 1, 2, 0, 3, 5, 6)).reshape(STEPS, parts, freq, kb, recv)
     return full
 
 
@@ -43,7 +46,14 @@
         ) + jnp.einsum("fsk,fkr->sfr", window[1], recv[0], preferred_element_type=jnp.float32)
         piece = jnp.stack([real_part, imag_part], axis=1)
         totals = piece if totals is None else totals + piece
-    return lax.psum_scatter(totals, SP, scatter_dimension=0, tiled=True).astype(jnp.bfloat16)
+    n_zh = lax.psum(1, "zh")
+    n_c = lax.psum(1, "c")
+    rows = totals.shape[0]
+    totals = totals.reshape(n_zh, n_c, rows // (n_zh * n_c), *totals.shape[1:])
+    totals = jnp.swapaxes(totals, 0, 1).reshape(rows, *totals.shape[3:])
+    totals = lax.psum_scatter(totals, "c", scatter_dimension=0, tiled=True)
+    totals = lax.psum_scatter(totals, "zh", scatter_dimension=0, tiled=True)
+    return totals.astype(jnp.bfloat16)
 
 
 def solution(mesh):

time: 320 us -> 306 us (0.956)
  waiting for transfers between devices: 257 us -> 181 us
  matrix products: 9.95 us -> 40.2 us
  local copies, waits for them, and re-layouts: 13.6 us -> 34.1 us
  blocking collectives: 0 us -> 5.74 us
  other arithmetic: 14.2 us -> 19.5 us
    all_gather x1 -> x2, waiting for transfers between devices: 151 us -> 73.5 us  [the longest x1 47.8 us: gather_receivers(): full = lax.all_gather(full, 'y', axis=0, tiled=False)]
    dot_general x4, matrix products: 2.47 us -> 13.7 us  [body(): jnp.einsum('fsk,fkr->sfr', window[0], recv[0], preferred_element_type=jnp...]
    sub x0 -> x4, local copies, waits for them, and re-layouts: none -> 9.58 us  [body(): jnp.einsum('fsk,fkr->sfr', window[0], recv[0], preferred_element_type=jnp...]
    transpose x0 -> x1, other arithmetic: none -> 9.22 us  [body(): totals = jnp.swapaxes(totals, 0, 1).reshape(rows, *totals.shape[3:])]
    dot_general x4, matrix products: 2.53 us -> 11.7 us  [body(): jnp.einsum('fsk,fkr->sfr', window[1], recv[1], preferred_element_type=jnp...]
    all_gather x0 -> x1, blocking collectives: none -> 5.74 us  [gather_receivers(): full = lax.all_gather(chosen, 'zl', axis=0, tiled=False)]
    dot_general x4, matrix products: 2.47 us -> 7.64 us  [body(): jnp.einsum('fsk,fkr->sfr', window[0], recv[1], preferred_element_type=jnp...]
    dot_general x4, matrix products: 2.49 us -> 7.08 us  [body(): jnp.einsum('fsk,fkr->sfr', window[1], recv[0], preferred_element_type=jnp...]
  transfers between devices with their start and end apart: 3 -> 5, of which waited for: 3 -> 5; matrix products, arithmetic and copies ran while one was open for 2% -> 2% of each run, Pallas kernels for 0% -> 0%
where the time goes in v2:
time: 306 us; the launch traced here: 305 us
  waiting for transfers between devices  181 us (59%)
  matrix products  40.2 us (13%)
  local copies, waits for them, and re-layouts  34.1 us (11%)
  other arithmetic  19.5 us (6%)
  between operations  15.4 us (5%)
  starting transfers between devices  9.13 us (3%)
  blocking collectives  5.74 us (2%)
    reduce_scatter x1, waiting for transfers between devices, body(): totals = lax.psum_scatter(totals, 'zh', scatter_dimension=0, tiled=True)  71.3 us
    all_gather x1, waiting for transfers between devices, gather_receivers(): full = lax.all_gather(full, 'y', axis=0, tiled=False)  47.8 us
    all_gather x1, waiting for transfers between devices, gather_receivers(): full = lax.all_gather(full, 'x', axis=0, tiled=False)  25.8 us
    reduce_scatter x1, waiting for transfers between devices, body(): totals = lax.psum_scatter(totals, 'c', scatter_dimension=0, tiled=True)  20.7 us
    all_to_all x1, waiting for transfers between devices, gather_receivers(): got = lax.all_to_all(pieces, SHOT, 0, 0, tiled=True)  15.3 us
    dot_general x4, matrix products, body(): jnp.einsum('fsk,fkr->sfr', window[0], recv[0], preferred_element_type=jnp...  13.7 us
    dot_general x4, matrix products, body(): jnp.einsum('fsk,fkr->sfr', window[1], recv[1], preferred_element_type=jnp...  11.7 us
    add x4, local copies, waits for them, and re-layouts, body(): jnp.einsum('fsk,fkr->sfr', window[0], recv[1], preferred_element_type=jnp...  9.95 us
  transfers between devices with their start and end apart: 5, of which 5 were waited for; matrix products, arithmetic and copies ran while one was open for 2% of the time, Pallas kernels for 0%

profile of v2, /device:TPU:6, one launch (start us, length us, event | category | flops | bytes accessed | tf_op | source)
XLA Modules:
  0.0 304.9 jit_solution(1736064832038613201)
XLA Ops:
  12.7 9.0 %all-to-all-start = ((bf16[32,64,256]{2,1,0:T(8,128)(2,1)}), bf16[32,64,256]{2,1,0:T(8,128)(2,1)S(1)}, u32[]{:S(2)}, u32[]{:S(2)}) async-start(bf16[32,64,256]{2,1,0:T(8,128)(2,1)} %bitcast), calls=%async_computation | async-start | bytes 2097152 | tf_op jit(solution)/shard_map/all_to_all | solution.py:22
  21.9 15.3 %all-to-all-done = bf16[32,64,256]{2,1,0:T(8,128)(2,1)S(1)} async-done(((bf16[32,64,256]{2,1,0:T(8,128)(2,1)}), bf16[32,64,256]{2,1,0:T(8,128)(2,1)S(1)}, u32[]{:S(2)}, u32[]{:S(2)}) %all-to-all-start) | async-done | bytes 1048608 | tf_op jit(solution)/shard_map/all_to_all | solution.py:22
  37.9 5.7 %all_gather.16 = bf16[2,4,64,256]{3,2,1,0:T(8,128)(2,1)} all-gather(bf16[1,4,64,256]{3,2,1,0:T(8,128)(2,1)S(1)} %bitcast_select_fusion), channel_id=1, replica_groups=mesh['x'=4,'y'=4,'zl'=2,'zh'=4,'c'=2] {'zl'}, dimensions={0}, use_global_device_ids=true | all-gather | bytes 393216 | tf_op jit(solution)/shard_map/all_gather | solution.py:24
  43.7 25.8 %all-gather.5.cloned.1.call-done = bf16[8,4,64,256]{3,2,1,0:T(8,128)(2,1)} async-done(((bf16[2,4,64,256]{3,2,1,0:T(8,128)(2,1)}), bf16[8,4,64,256]{3,2,1,0:T(8,128)(2,1)}) %all-gather.5.cloned.1.call-update) | async-done | bytes 1048592 | tf_op jit(solution)/shard_map/all_gather | solution.py:25
  69.6 6.3 %broadcast_multiply_fusion = bf16[2,8,384,512]{3,2,1,0:T(8,128)(2,1)} fusion(bf16[2,8,384,512]{3,2,1,0:T(8,128)(2,1)} %param.4, bf16[384,512]{1,0:T(8,128)(2,1)S(1)} %convert_element_type.6), kind=kLoop, calls=%fused_computation.13 | loop fusion | flops 3145728 | bytes 12976128 | tf_op jit(solution)/shard_map/mul | solution.py:35
  75.9 47.8 %all-gather.7.cloned.1.call-done = bf16[16,2,4,64,256]{4,3,2,1,0:T(8,128)(2,1)} async-done(((bf16[4,2,4,64,256]{4,3,2,1,0:T(8,128)(2,1)}), bf16[16,2,4,64,256]{4,3,2,1,0:T(8,128)(2,1)}) %all-gather.7.cloned.1.call-update) | async-done | bytes 4194320 | tf_op jit(solution)/shard_map/all_gather | solution.py:26
  123.7 2.7 fusion.12
  133.6 3.4 %fusion.10 = f32[8,256,384]{2,1,0:T(8,128)} fusion(bf16[8,128,256]{2,1,0:T(8,128)(2,1)S(1)} %bitcast.113, bf16[2,8,384,512]{3,2,1,0:T(8,128)(2,1)} %broadcast_multiply_fusion), kind=kOutput, calls=%fused_computation.29 | convolution fusion | flops 201326592 | bytes 4456448 | tf_op jit(solution)/shard_map/fsk,fkr->sfr/dot_general | solution.py:41
  138.7 2.6 copy.102
  141.3 2.9 subtract_bitcast_fusion
  148.6 3.4 %fusion.8 = f32[8,256,384]{2,1,0:T(8,128)} fusion(bf16[8,128,256]{2,1,0:T(8,128)(2,1)S(1)} %bitcast.109, bf16[2,8,384,512]{3,2,1,0:T(8,128)(2,1)} %broadcast_multiply_fusion), kind=kOutput, calls=%fused_computation.27 | convolution fusion | flops 201326592 | bytes 4456448 | tf_op jit(solution)/shard_map/fsk,fkr->sfr/dot_general | solution.py:41
  153.8 2.4 copy.94
  156.3 2.9 subtract_bitcast_fusion.1
  163.6 3.4 %fusion.6 = f32[8,256,384]{2,1,0:T(8,128)} fusion(bf16[8,128,256]{2,1,0:T(8,128)(2,1)S(1)} %bitcast.105, bf16[2,8,384,512]{3,2,1,0:T(8,128)(2,1)} %broadcast_multiply_fusion), kind=kOutput, calls=%fused_computation.25 | convolution fusion | flops 201326592 | bytes 4456448 | tf_op jit(solution)/shard_map/fsk,fkr->sfr/dot_general | solution.py:41
  168.8 2.4 copy.86
  171.2 2.9 subtract_bitcast_fusion.2
  174.1 2.4 copy.83
  178.5 3.5 %fusion.4 = f32[8,256,384]{2,1,0:T(8,128)} fusion(bf16[8,128,256]{2,1,0:T(8,128)(2,1)S(1)} %bitcast.103, bf16[2,8,384,512]{3,2,1,0:T(8,128)(2,1)} %broadcast_multiply_fusion), kind=kOutput, calls=%fused_computation.23 | convolution fusion | flops 201326592 | bytes 4456448 | tf_op jit(solution)/shard_map/fsk,fkr->sfr/dot_general | solution.py:41
  183.8 2.5 copy.78
  186.3 2.9 subtract_bitcast_fusion.3
  191.6 9.2 %fusion.2 = f32[2,4,48,2,8,256]{5,4,2,0,1,3:T(8,128)S(1)} fusion(f32[4,2,48,1,8,256]{5,4,2,1,0,3:T(8,128)} %bitcast.97, f32[4,2,48,1,8,256]{5,4,2,1,0,3:T(8,128)} %bitcast.98, f32[4,2,48,1,8,256]{5,4,2,1,0,3:T(8,128)} %bitcast.95, f32[4,2,48,1,8,256]{5,4,2,1,0,3:T(8,128)} %bitcast.96, f32[4,2,48,1,8,256]{5,4,2,1,0,3:T(8,128)} %bitcast.93, ...), kind=kLoop, calls=%fused_computation.4 | loop fusion | flops 11010048 | bytes 31457280 | tf_op jit(solution)/shard_map/transpose | solution.py:53
  200.9 3.5 %copy.103 = f32[2,4,48,2,8,256]{5,4,3,2,1,0:T(8,128)} copy(f32[2,4,48,2,8,256]{5,4,2,0,1,3:T(8,128)S(1)} %fusion.2) | data formatting | bytes 12582912 | tf_op jit(solution)/shard_map/transpose | solution.py:53
  204.5 20.7 %reduce-scatter.3.cloned.1.call-done = f32[192,2,8,256]{3,2,1,0:T(8,128)} async-done(((f32[384,2,8,256]{3,2,1,0:T(8,128)}), f32[192,2,8,256]{3,2,1,0:T(8,128)}) %reduce-scatter.3.cloned.1.call-update) | async-done | bytes 3145744 | tf_op jit(solution)/shard_map/reduce_scatter | solution.py:54
  225.2 71.3 %reduce-scatter.5.cloned.1.call-done = f32[48,2,8,256]{3,2,1,0:T(8,128)} async-done(((f32[192,2,8,256]{3,2,1,0:T(8,128)}), f32[48,2,8,256]{3,2,1,0:T(8,128)}) %reduce-scatter.5.cloned.1.call-update) | async-done | bytes 786448 | tf_op jit(solution)/shard_map/reduce_scatter | solution.py:55
  (48 shorter events, 34.4 us)
Async XLA Ops:
  6.5 15.2 %copy-start.5 = (s32[4,8]{1,0:T(4,128)S(1)}, s32[4,8]{1,0:T(4,128)}, u32[]{:S(2)}) copy-start(s32[4,8]{1,0:T(4,128)} %param.7) | copy-start | bytes 388
  10.3 59.3 %copy-start.4 = (s32[384,512]{1,0:T(8,128)S(1)}, s32[384,512]{1,0:T(8,128)}, u32[]{:S(2)}) copy-start(s32[384,512]{1,0:T(8,128)} %param.5) | copy-start | bytes 2359300
  12.7 24.6 %all-to-all-start = ((bf16[32,64,256]{2,1,0:T(8,128)(2,1)}), bf16[32,64,256]{2,1,0:T(8,128)(2,1)S(1)}, u32[]{:S(2)}, u32[]{:S(2)}) async-start(bf16[32,64,256]{2,1,0:T(8,128)(2,1)} %bitcast), calls=%async_computation | async-start | bytes 2097152 | tf_op jit(solution)/shard_map/all_to_all | solution.py:22
  21.7 47.8 %all-gather.5.cloned.1.call-start = ((), (), s32[]{:S(2)}) async-start(), calls=%async_computation.5 | async-start | bytes 1310720 | tf_op jit(solution)/shard_map/all_gather | solution.py:25
  43.7 80.0 %all-gather.7.cloned.1.call-start = ((), (), s32[]{:S(2)}) async-start(), calls=%async_computation.6 | async-start | bytes 5242880 | tf_op jit(solution)/shard_map/all_gather | solution.py:26
  69.5 155.6 %reduce-scatter.3.cloned.1.call-start = ((), (), s32[]{:S(2)}) async-start(), calls=%async_computation.3 | async-start | bytes 9437184 | tf_op jit(solution)/shard_map/reduce_scatter | solution.py:54
  126.5 5.3 %copy-start.3 = (bf16[1,1,2,4,2,64,256]{6,5,4,3,2,1,0:T(8,128)(2,1)}, bf16[1,1,2,4,2,64,256]{6,5,4,3,2,1,0:T(8,128)(2,1)S(1)}, u32[]{:S(2)}) copy-start(bf16[1,1,2,4,2,64,256]{6,5,4,3,2,1,0:T(8,128)(2,1)S(1)} %copy.97) | copy-start | bytes 1572868
  146.7 2.0 copy-start.2
  161.6 2.0 copy-start.1
  176.6 2.0 copy-start
  204.4 92.1 %reduce-scatter.5.cloned.1.call-start = ((), (), s32[]{:S(2)}) async-start(), calls=%async_computation.4 | async-start | bytes 3932160 | tf_op jit(solution)/shard_map/reduce_scatter | solution.py:55
Sparse Core Ops, SparseCore 0:
  43.8 25.6 all-gather.4
  71.3 52.3 all-gather.6
  204.5 20.5 reduce-scatter.2
  227.6 68.8 reduce-scatter.4

commit v3 on v2

--- a/solution.py
+++ b/solution.py
@@ -31,29 +31,22 @@
 
 
 def body(shot_data, live_masks, spectra, plan):
-    width = spectra.shape[3]
     live = shot_data * live_masks.astype(shot_data.dtype)[None, None]
     recv_all = gather_receivers(spectra, plan)
-    totals = None
-    for section in range(STEPS):
-        recv = recv_all[section]
-        window = live[:, :, :, section * width : (section + 1) * width]
-        real_part = jnp.einsum(
-            "fsk,fkr->sfr", window[0], recv[0], preferred_element_type=jnp.float32
-        ) - jnp.einsum("fsk,fkr->sfr", window[1], recv[1], preferred_element_type=jnp.float32)
-        imag_part = jnp.einsum(
-            "fsk,fkr->sfr", window[0], recv[1], preferred_element_type=jnp.float32
-        ) + jnp.einsum("fsk,fkr->sfr", window[1], recv[0], preferred_element_type=jnp.float32)
-        piece = jnp.stack([real_part, imag_part], axis=1)
-        totals = piece if totals is None else totals + piece
-    n_zh = lax.psum(1, "zh")
-    n_c = lax.psum(1, "c")
-    rows = totals.shape[0]
-    totals = totals.reshape(n_zh, n_c, rows // (n_zh * n_c), *totals.shape[1:])
-    totals = jnp.swapaxes(totals, 0, 1).reshape(rows, *totals.shape[3:])
-    totals = lax.psum_scatter(totals, "c", scatter_dimension=0, tiled=True)
-    totals = lax.psum_scatter(totals, "zh", scatter_dimension=0, tiled=True)
-    return totals.astype(jnp.bfloat16)
+    steps, parts, freq, kb, recv = recv_all.shape
+    stacked = jnp.transpose(recv_all, (1, 2, 0, 3, 4)).reshape(parts, freq, steps * kb, recv)
+    real_in, imag_in = stacked[0], stacked[1]
+    weights = jnp.stack(
+        [jnp.stack([real_in, imag_in], axis=2), jnp.stack([-imag_in, real_in], axis=2)], axis=0
+    ).reshape(parts, freq, steps * kb, 2 * recv)
+    out = lax.dot_general(
+        live, weights, (((0, 3), (0, 2)), ((1,), (1,))), preferred_element_type=jnp.float32
+    )
+    out = jnp.transpose(out, (1, 0, 2))
+    out = lax.psum_scatter(out, SP, scatter_dimension=0, tiled=True)
+    rows = out.shape[0]
+    out = out.reshape(rows, freq, 2, recv).astype(jnp.bfloat16)
+    return jnp.transpose(out, (0, 2, 1, 3))
 
 
 def solution(mesh):

time: 306 us -> 262 us (0.86)
  matrix products: 40.2 us -> 11.3 us
  other arithmetic: 19.5 us -> 5.83 us
  waiting for transfers between devices: 181 us -> 176 us
  local copies, waits for them, and re-layouts: 34.1 us -> 37.8 us
    another operation x0 -> x4, local copies, waits for them, and re-layouts: none -> 30.1 us  [the longest x2 15.2 us: body(): jnp.stack([jnp.stack([real_in, imag_in], axis=2), jnp.stack([-imag_in, re...]
    dot_general x16 -> x1, matrix products: 40.2 us -> 11.3 us  [body(): lax.dot_general(live, weights, (((0, 3), (0, 2)), ((1,), (1,))), preferre...]
    reduce_scatter x2 -> x1, waiting for transfers between devices: 92 us -> 81.1 us  [body(): out = lax.psum_scatter(out, SP, scatter_dimension=0, tiled=True)]
    add x4 -> x0, local copies, waits for them, and re-layouts: 9.95 us -> none  [body(): jnp.einsum('fsk,fkr->sfr', window[0], recv[1], preferred_element_type=jnp...]
    sub x4 -> x0, local copies, waits for them, and re-layouts: 9.58 us -> none  [body(): jnp.einsum('fsk,fkr->sfr', window[0], recv[0], preferred_element_type=jnp...]
    transpose x1 -> x0, other arithmetic: 9.22 us -> none  [body(): totals = jnp.swapaxes(totals, 0, 1).reshape(rows, *totals.shape[3:])]
    slice x9 -> x3, local copies, waits for them, and re-layouts: 8.1 us -> 0.91 us  [body(): real_in, imag_in = (stacked[0], stacked[1])]
    all_gather x1, waiting for transfers between devices: 47.8 us -> 54 us  [gather_receivers(): full = lax.all_gather(full, 'y', axis=0, tiled=False)]
  transfers between devices with their start and end apart: 5 -> 4, of which waited for: 5 -> 4; matrix products, arithmetic and copies ran while one was open for 2% -> 0% of each run, Pallas kernels for 0% -> 0%
where the time goes in v3:
time: 262 us; the launch traced here: 261 us
  waiting for transfers between devices  176 us (67%)
  local copies, waits for them, and re-layouts  37.8 us (14%)
  between operations  15.3 us (6%)
  matrix products  11.3 us (4%)
  starting transfers between devices  9.08 us (3%)
  other arithmetic  5.83 us (2%)
  blocking collectives  5.74 us (2%)
    reduce_scatter x1, waiting for transfers between devices, body(): out = lax.psum_scatter(out, SP, scatter_dimension=0, tiled=True)  81.1 us
    all_gather x1, waiting for transfers between devices, gather_receivers(): full = lax.all_gather(full, 'y', axis=0, tiled=False)  54 us
    all_gather x1, waiting for transfers between devices, gather_receivers(): full = lax.all_gather(full, 'x', axis=0, tiled=False)  25.8 us
    all_to_all x1, waiting for transfers between devices, gather_receivers(): got = lax.all_to_all(pieces, SHOT, 0, 0, tiled=True)  15.3 us
    another operation x2, local copies, waits for them, and re-layouts, body(): jnp.stack([jnp.stack([real_in, imag_in], axis=2), jnp.stack([-imag_in, re...  15.2 us
    dot_general x1, matrix products, body(): lax.dot_general(live, weights, (((0, 3), (0, 2)), ((1,), (1,))), preferre...  11.3 us
    all_to_all x1, starting transfers between devices, gather_receivers(): got = lax.all_to_all(pieces, SHOT, 0, 0, tiled=True)  8.96 us
    another operation x1, local copies, waits for them, and re-layouts, body(): jnp.stack([-imag_in, real_in], axis=2)  8.48 us
  transfers between devices with their start and end apart: 4, of which 4 were waited for; matrix products, arithmetic and copies ran while one was open for 0% of the time, Pallas kernels for 0%

profile of v3, /device:TPU:6, one launch (start us, length us, event | category | flops | bytes accessed | tf_op | source)
XLA Modules:
  0.0 261.3 jit_solution(1779671477610059696)
XLA Ops:
  6.5 1.0 and_reduce_fusion
  7.5 0.7 iota_reduce_fusion
  10.3 2.3 constant_dynamic-slice_fusion
  12.6 9.0 %all-to-all-start = ((bf16[32,64,256]{2,1,0:T(8,128)(2,1)}), bf16[32,64,256]{2,1,0:T(8,128)(2,1)S(1)}, u32[]{:S(2)}, u32[]{:S(2)}) async-start(bf16[32,64,256]{2,1,0:T(8,128)(2,1)} %bitcast), calls=%async_computation | async-start | bytes 2097152 | tf_op jit(solution)/shard_map/all_to_all | solution.py:22
  21.7 0.2 fusion.11
  21.9 15.3 %all-to-all-done = bf16[32,64,256]{2,1,0:T(8,128)(2,1)S(1)} async-done(((bf16[32,64,256]{2,1,0:T(8,128)(2,1)}), bf16[32,64,256]{2,1,0:T(8,128)(2,1)S(1)}, u32[]{:S(2)}, u32[]{:S(2)}) %all-to-all-start) | async-done | bytes 1048608 | tf_op jit(solution)/shard_map/all_to_all | solution.py:22
  37.2 0.6 gather_fusion
  37.8 5.7 %all_gather.16 = bf16[2,4,64,256]{3,2,1,0:T(8,128)(2,1)} all-gather(bf16[1,4,64,256]{3,2,1,0:T(8,128)(2,1)S(1)} %bitcast_select_fusion), channel_id=1, replica_groups=mesh['x'=4,'y'=4,'zl'=2,'zh'=4,'c'=2] {'zl'}, dimensions={0}, use_global_device_ids=true | all-gather | bytes 393216 | tf_op jit(solution)/shard_map/all_gather | solution.py:24
  43.7 25.8 %all-gather.5.cloned.1.call-done = bf16[8,4,64,256]{3,2,1,0:T(8,128)(2,1)} async-done(((bf16[2,4,64,256]{3,2,1,0:T(8,128)(2,1)}), bf16[8,4,64,256]{3,2,1,0:T(8,128)(2,1)}) %all-gather.5.cloned.1.call-update) | async-done | bytes 1048592 | tf_op jit(solution)/shard_map/all_gather | solution.py:25
  69.6 54.0 %all-gather.7.cloned.1.call-done = bf16[16,2,4,64,256]{4,3,2,1,0:T(8,128)(2,1)} async-done(((bf16[4,2,4,64,256]{4,3,2,1,0:T(8,128)(2,1)}), bf16[16,2,4,64,256]{4,3,2,1,0:T(8,128)(2,1)}) %all-gather.7.cloned.1.call-update) | async-done | bytes 4194320 | tf_op jit(solution)/shard_map/all_gather | solution.py:26
  123.6 2.7 %copy.17 = bf16[4,2,2,4,2,64,256]{6,5,4,3,2,1,0:T(8,128)(2,1)S(1)} copy(bf16[4,2,2,4,2,64,256]{6,5,0,4,2,1,3:T(8,128)(2,1)} %bitcast.25) | data formatting | bytes 8388608 | tf_op jit(solution)/shard_map/transpose | solution.py:29
  126.3 0.5 fusion.13
  126.8 0.2 copy.19
  127.0 0.3 bitcast_negate_fusion
  127.3 0.2 copy.18
  127.5 2.3 pad_maximum_fusion
  129.8 6.4 %copy.20 = bf16[8,512,2,256]{3,2,1,0:T(2,128)(2,1)} copy(bf16[8,512,2,256]{3,1,0,2:T(8,128)(2,1)S(1)} %get-tuple-element.11) | data formatting | bytes 8388608 | tf_op jit(solution)/shard_map/stack | solution.py:40
  136.2 7.6 %stack.17 = bf16[1,8,512,512]{3,2,1,0:T(8,128)(2,1)} reshape(bf16[8,512,2,256]{3,2,1,0:T(2,128)(2,1)} %copy.20) | data formatting | bytes 8388608 | tf_op jit(solution)/shard_map/stack | solution.py:39
  143.8 8.5 %copy.21 = bf16[8,512,2,256]{3,2,1,0:T(2,128)(2,1)} copy(bf16[8,512,2,256]{3,1,0,2:T(8,128)(2,1)} %get-tuple-element.12) | data formatting | bytes 8388608 | tf_op jit(solution)/shard_map/stack | solution.py:40
  152.3 7.6 %stack.19 = bf16[1,8,512,512]{3,2,1,0:T(8,128)(2,1)} reshape(bf16[8,512,2,256]{3,2,1,0:T(2,128)(2,1)} %copy.21) | data formatting | bytes 8388608 | tf_op jit(solution)/shard_map/stack | solution.py:39
  159.9 11.3 %fusion.6 = f32[384,8,512]{2,0,1:T(8,128)} fusion(bf16[1,8,512,512]{3,2,1,0:T(8,128)(2,1)} %stack.19, bf16[1,8,512,512]{3,2,1,0:T(8,128)(2,1)} %stack.17, bf16[2,8,384,512]{3,2,1,0:T(8,128)(2,1)} %param.4, bf16[384,512]{1,0:T(8,128)(2,1)S(1)} %convert_element_type.9), kind=kOutput, calls=%fused_computation.9 | convolution fusion | flops 3228565504 | bytes 21364736 | tf_op jit(solution)/shard_map/dot_general | solution.py:42
  171.3 81.1 %reduce-scatter.2.cloned.1.call-done = f32[48,8,512]{2,0,1:T(8,128)} async-done(((f32[384,8,512]{2,0,1:T(8,128)}), f32[48,8,512]{2,0,1:T(8,128)}) %reduce-scatter.2.cloned.1.call-update) | async-done | bytes 786448 | tf_op jit(solution)/shard_map/reduce_scatter | solution.py:46
  252.3 1.2 convert_element_type.10
  253.6 1.2 copy.24
  (14 shorter events, 0.4 us)
Async XLA Ops:
  6.5 15.1 %copy-start.1 = (s32[4,8]{1,0:T(4,128)S(1)}, s32[4,8]{1,0:T(4,128)}, u32[]{:S(2)}) copy-start(s32[4,8]{1,0:T(4,128)} %param.7) | copy-start | bytes 388
  6.5 63.0 %copy-start = (s32[384,512]{1,0:T(8,128)S(1)}, s32[384,512]{1,0:T(8,128)}, u32[]{:S(2)}) copy-start(s32[384,512]{1,0:T(8,128)} %param.5) | copy-start | bytes 2359300
  12.6 24.6 %all-to-all-start = ((bf16[32,64,256]{2,1,0:T(8,128)(2,1)}), bf16[32,64,256]{2,1,0:T(8,128)(2,1)S(1)}, u32[]{:S(2)}, u32[]{:S(2)}) async-start(bf16[32,64,256]{2,1,0:T(8,128)(2,1)} %bitcast), calls=%async_computation | async-start | bytes 2097152 | tf_op jit(solution)/shard_map/all_to_all | solution.py:22
  21.6 47.8 %all-gather.5.cloned.1.call-start = ((), (), s32[]{:S(2)}) async-start(), calls=%async_computation.3 | async-start | bytes 1310720 | tf_op jit(solution)/shard_map/all_gather | solution.py:25
  43.6 80.0 %all-gather.7.cloned.1.call-start = ((), (), s32[]{:S(2)}) async-start(), calls=%async_computation.4 | async-start | bytes 5242880 | tf_op jit(solution)/shard_map/all_gather | solution.py:26
  69.4 182.9 %reduce-scatter.2.cloned.1.call-start = ((), (), s32[]{:S(2)}) async-start(), calls=%async_computation.2 | async-start | bytes 7077888 | tf_op jit(solution)/shard_map/reduce_scatter | solution.py:46
Sparse Core Ops, SparseCore 0:
  43.7 25.6 all-gather.4
  71.2 52.3 all-gather.6
  171.4 80.9 reduce-scatter.1

commit v4 on v3

--- a/solution.py
+++ b/solution.py
@@ -26,19 +26,20 @@
     full = lax.all_gather(full, "y", axis=0, tiled=False)
     n_y, n_x, n_zl = full.shape[:3]
     full = full.reshape(n_y, parts, n_x // parts, n_zl, STEPS, kb // split, recv)
-    full = jnp.transpose(full, (4, 1, 2, 0, 3, 5, 6)).reshape(STEPS, parts, freq, kb, recv)
-    return full
+
+    def part_of(p):
+        return jnp.transpose(full[:, p], (1, 0, 3, 2, 4, 5)).reshape(freq, STEPS * kb, recv)
+
+    return part_of(0), part_of(1)
 
 
 def body(shot_data, live_masks, spectra, plan):
     live = shot_data * live_masks.astype(shot_data.dtype)[None, None]
-    recv_all = gather_receivers(spectra, plan)
-    steps, parts, freq, kb, recv = recv_all.shape
-    stacked = jnp.transpose(recv_all, (1, 2, 0, 3, 4)).reshape(parts, freq, steps * kb, recv)
-    real_in, imag_in = stacked[0], stacked[1]
+    real_in, imag_in = gather_receivers(spectra, plan)
+    freq, _, recv = real_in.shape
     weights = jnp.stack(
-        [jnp.stack([real_in, imag_in], axis=2), jnp.stack([-imag_in, real_in], axis=2)], axis=0
-    ).reshape(parts, freq, steps * kb, 2 * recv)
+        [jnp.concatenate([real_in, imag_in], axis=-1), jnp.concatenate([-imag_in, real_in], axis=-1)], axis=0
+    )
     out = lax.dot_general(
         live, weights, (((0, 3), (0, 2)), ((1,), (1,))), preferred_element_type=jnp.float32
     )

time: 262 us -> 227 us (0.87)
  local copies, waits for them, and re-layouts: 37.8 us -> 7.21 us
    another operation x4 -> x0, local copies, waits for them, and re-layouts: 30.1 us -> none  [the longest x2 15.2 us: body(): jnp.stack([jnp.stack([real_in, imag_in], axis=2), jnp.stack([-imag_in, re...]
where the time goes in v4:
time: 227 us
  waiting for transfers between devices  176 us (78%)
  between operations  15.3 us (7%)
  starting transfers between devices  9.08 us (4%)
  matrix products  8.86 us (4%)
  local copies, waits for them, and re-layouts  7.21 us (3%)
  blocking collectives  5.74 us (3%)
  other arithmetic  4.41 us (2%)
    reduce_scatter x1, waiting for transfers between devices, body(): out = lax.psum_scatter(out, SP, scatter_dimension=0, tiled=True)  81.1 us
    all_gather x1, waiting for transfers between devices, gather_receivers(): full = lax.all_gather(full, 'y', axis=0, tiled=False)  54 us
    all_gather x1, waiting for transfers between devices, gather_receivers(): full = lax.all_gather(full, 'x', axis=0, tiled=False)  25.8 us
    all_to_all x1, waiting for transfers between devices, gather_receivers(): got = lax.all_to_all(pieces, SHOT, 0, 0, tiled=True)  15.3 us
    all_to_all x1, starting transfers between devices, gather_receivers(): got = lax.all_to_all(pieces, SHOT, 0, 0, tiled=True)  8.96 us
    dot_general x1, matrix products, body(): lax.dot_general(live, weights, (((0, 3), (0, 2)), ((1,), (1,))), preferre...  8.86 us
    all_gather x1, blocking collectives, gather_receivers(): full = lax.all_gather(chosen, 'zl', axis=0, tiled=False)  5.74 us
  transfers between devices with their start and end apart: 4, of which 4 were waited for; matrix products, arithmetic and copies ran while one was open for 0% of the time, Pallas kernels for 0%

profile of v4, /device:TPU:6, one launch (start us, length us, event | category | flops | bytes accessed | tf_op | source)
XLA Modules:
  0.0 226.8 jit_solution(7056602300058204902)
XLA Ops:
  6.5 1.0 and_reduce_fusion
  7.5 0.7 iota_reduce_fusion
  10.3 2.3 %constant_dynamic-slice_fusion = bf16[1,2,8,128,256]{4,3,2,1,0:T(8,128)(2,1)} fusion(bf16[4,2,8,128,256]{4,3,2,1,0:T(8,128)(2,1)} %param.6, s32[]{:T(128)S(6)} %select_n.32), kind=kLoop, calls=%fused_computation.20 | loop fusion | bytes 2097156 | tf_op jit(solution)/shard_map/jit(dynamic_index_in_dim)/dynamic_slice | solution.py:18
  12.6 9.0 %all-to-all-start = ((bf16[32,64,256]{2,1,0:T(8,128)(2,1)}), bf16[32,64,256]{2,1,0:T(8,128)(2,1)S(1)}, u32[]{:S(2)}, u32[]{:S(2)}) async-start(bf16[32,64,256]{2,1,0:T(8,128)(2,1)} %bitcast), calls=%async_computation | async-start | bytes 2097152 | tf_op jit(solution)/shard_map/all_to_all | solution.py:22
  21.6 0.0 all-gather.5.cloned.1.call-start
  21.7 0.2 fusion.11
  21.9 15.3 %all-to-all-done = bf16[32,64,256]{2,1,0:T(8,128)(2,1)S(1)} async-done(((bf16[32,64,256]{2,1,0:T(8,128)(2,1)}), bf16[32,64,256]{2,1,0:T(8,128)(2,1)S(1)}, u32[]{:S(2)}, u32[]{:S(2)}) %all-to-all-start) | async-done | bytes 1048608 | tf_op jit(solution)/shard_map/all_to_all | solution.py:22
  37.2 0.6 gather_fusion
  37.8 0.1 bitcast_select_fusion
  37.8 5.7 %all_gather.16 = bf16[2,4,64,256]{3,2,1,0:T(8,128)(2,1)} all-gather(bf16[1,4,64,256]{3,2,1,0:T(8,128)(2,1)S(1)} %bitcast_select_fusion), channel_id=1, replica_groups=mesh['x'=4,'y'=4,'zl'=2,'zh'=4,'c'=2] {'zl'}, dimensions={0}, use_global_device_ids=true | all-gather | bytes 393216 | tf_op jit(solution)/shard_map/all_gather | solution.py:24
  43.6 0.0 all-gather.7.cloned.1.call-start
  43.7 25.8 %all-gather.5.cloned.1.call-done = bf16[8,4,64,256]{3,2,1,0:T(8,128)(2,1)} async-done(((bf16[2,4,64,256]{3,2,1,0:T(8,128)(2,1)}), bf16[8,4,64,256]{3,2,1,0:T(8,128)(2,1)}) %all-gather.5.cloned.1.call-update) | async-done | bytes 1048592 | tf_op jit(solution)/shard_map/all_gather | solution.py:25
  69.5 0.1 convert_element_type.9
  69.6 54.0 %all-gather.7.cloned.1.call-done = bf16[16,2,4,64,256]{4,3,2,1,0:T(8,128)(2,1)} async-done(((bf16[4,2,4,64,256]{4,3,2,1,0:T(8,128)(2,1)}), bf16[16,2,4,64,256]{4,3,2,1,0:T(8,128)(2,1)}) %all-gather.7.cloned.1.call-update) | async-done | bytes 4194320 | tf_op jit(solution)/shard_map/all_gather | solution.py:26
  123.6 2.6 %slice_bitcast_fusion = (bf16[2,4,4,2,64,256]{5,4,2,3,0,1:T(8,128)(2,1)S(1)}, bf16[2,4,4,2,64,256]{5,4,2,3,0,1:T(8,128)(2,1)S(1)}) fusion(bf16[4,2,2,2,4,64,256]{6,5,4,3,2,1,0:T(8,128)(2,1)} %bitcast.31), kind=kLoop, calls=%fused_computation.10 | loop fusion | bytes 8388608 | tf_op jit(solution)/shard_map/transpose | solution.py:31
  126.2 0.2 copy.14
  126.4 0.4 neg.3
  126.9 0.2 copy.13
  127.1 0.8 maximum_bitcast_fusion
  127.9 8.9 %fusion.6 = f32[384,8,512]{2,0,1:T(8,128)} fusion(bf16[1,8,512,512]{3,2,1,0:T(8,128)(2,1)S(1)} %get-tuple-element.12, bf16[1,8,512,512]{3,2,1,0:T(8,128)(2,1)S(1)} %get-tuple-element.11, bf16[2,8,384,512]{3,2,1,0:T(8,128)(2,1)} %param.4, bf16[384,512]{1,0:T(8,128)(2,1)S(1)} %convert_element_type.9), kind=kOutput, calls=%fused_computation.9 | convolution fusion | flops 3228565504 | bytes 21364736 | tf_op jit(solution)/shard_map/dot_general | solution.py:43
  136.8 81.1 %reduce-scatter.2.cloned.1.call-done = f32[48,8,512]{2,0,1:T(8,128)} async-done(((f32[384,8,512]{2,0,1:T(8,128)}), f32[48,8,512]{2,0,1:T(8,128)}) %reduce-scatter.2.cloned.1.call-update) | async-done | bytes 786448 | tf_op jit(solution)/shard_map/reduce_scatter | solution.py:47
  217.8 1.2 convert_element_type.10
  219.0 0.1 convert_element_type.11
  219.1 1.2 copy.17
  (9 shorter events, 0.1 us)
Async XLA Ops:
  6.5 15.1 %copy-start.1 = (s32[4,8]{1,0:T(4,128)S(1)}, s32[4,8]{1,0:T(4,128)}, u32[]{:S(2)}) copy-start(s32[4,8]{1,0:T(4,128)} %param.7) | copy-start | bytes 388
  6.5 63.0 %copy-start = (s32[384,512]{1,0:T(8,128)S(1)}, s32[384,512]{1,0:T(8,128)}, u32[]{:S(2)}) copy-start(s32[384,512]{1,0:T(8,128)} %param.5) | copy-start | bytes 2359300
  12.6 24.6 %all-to-all-start = ((bf16[32,64,256]{2,1,0:T(8,128)(2,1)}), bf16[32,64,256]{2,1,0:T(8,128)(2,1)S(1)}, u32[]{:S(2)}, u32[]{:S(2)}) async-start(bf16[32,64,256]{2,1,0:T(8,128)(2,1)} %bitcast), calls=%async_computation | async-start | bytes 2097152 | tf_op jit(solution)/shard_map/all_to_all | solution.py:22
  21.6 47.8 %all-gather.5.cloned.1.call-start = ((), (), s32[]{:S(2)}) async-start(), calls=%async_computation.3 | async-start | bytes 1310720 | tf_op jit(solution)/shard_map/all_gather | solution.py:25
  43.6 80.0 %all-gather.7.cloned.1.call-start = ((), (), s32[]{:S(2)}) async-start(), calls=%async_computation.4 | async-start | bytes 5242880 | tf_op jit(solution)/shard_map/all_gather | solution.py:26
  69.4 148.4 %reduce-scatter.2.cloned.1.call-start = ((), (), s32[]{:S(2)}) async-start(), calls=%async_computation.2 | async-start | bytes 7077888 | tf_op jit(solution)/shard_map/reduce_scatter | solution.py:47
Sparse Core Ops, SparseCore 0:
  43.7 25.6 all-gather.4
  71.2 52.3 all-gather.6
  136.9 80.9 reduce-scatter.1

commit v5 on v4

--- a/solution.py
+++ b/solution.py
@@ -33,6 +33,36 @@
     return part_of(0), part_of(1)
 
 
+def reduce_rows(out):
+    n_zh = lax.psum(1, "zh")
+    n_c = lax.psum(1, "c")
+    zh = lax.axis_index("zh")
+    c = lax.axis_index("c")
+    rows = out.shape[0]
+    blk = rows // (n_zh * n_c)
+    x = out.reshape(n_zh, n_c, blk, *out.shape[1:])
+    send = lax.dynamic_index_in_dim(x, n_c - 1 - c, 1, keepdims=False)
+    keep = lax.dynamic_index_in_dim(x, c, 1, keepdims=False)
+    got = lax.ppermute(send, "c", [(i, n_c - 1 - i) for i in range(n_c)])
+    partial = keep + got
+    half = blk // 2
+    lo, hi = partial[:, :half], partial[:, half:]
+    fwd = [(i, (i + 1) % n_zh) for i in range(n_zh)]
+    bwd = [(i, (i - 1) % n_zh) for i in range(n_zh)]
+
+    def chunk(a, index):
+        return lax.dynamic_index_in_dim(a, index % n_zh, 0, keepdims=False)
+
+    acc_lo = chunk(lo, zh + 2 * n_zh - 1)
+    acc_hi = chunk(hi, zh + 1)
+    for step in range(n_zh - 1):
+        got_lo = lax.ppermute(acc_lo, "zh", fwd)
+        got_hi = lax.ppermute(acc_hi, "zh", bwd)
+        acc_lo = got_lo + chunk(lo, zh + 2 * n_zh - step - 2)
+        acc_hi = got_hi + chunk(hi, zh + step + 2)
+    return jnp.concatenate([acc_lo, acc_hi], axis=0)
+
+
 def body(shot_data, live_masks, spectra, plan):
     live = shot_data * live_masks.astype(shot_data.dtype)[None, None]
     real_in, imag_in = gather_receivers(spectra, plan)
@@ -44,7 +74,7 @@
         live, weights, (((0, 3), (0, 2)), ((1,), (1,))), preferred_element_type=jnp.float32
     )
     out = jnp.transpose(out, (1, 0, 2))
-    out = lax.psum_scatter(out, SP, scatter_dimension=0, tiled=True)
+    out = reduce_rows(out)
     rows = out.shape[0]
     out = out.reshape(rows, freq, 2, recv).astype(jnp.bfloat16)
     return jnp.transpose(out, (0, 2, 1, 3))

time: 227 us -> 232 us (1.022)
  waiting for transfers between devices: 176 us -> 147 us
  starting transfers between devices: 9.08 us -> 26.2 us
  other arithmetic: 4.41 us -> 16.4 us
  local copies, waits for them, and re-layouts: 7.21 us -> 12.4 us
    reduce_scatter x1 -> x0, waiting for transfers between devices: 81.1 us -> none  [body(): out = lax.psum_scatter(out, SP, scatter_dimension=0, tiled=True)]
    ppermute x0 -> x7, waiting for transfers between devices: none -> 51.9 us  [the longest x3 37.1 us: reduce_rows(): got_lo = lax.ppermute(acc_lo, 'zh', fwd)]
    ppermute x0 -> x7, starting transfers between devices: none -> 17.1 us  [the longest x3 11.7 us: reduce_rows(): got_lo = lax.ppermute(acc_lo, 'zh', fwd)]
    add x0 -> x5, other arithmetic: none -> 10.5 us  [the longest x1 4.06 us: reduce_rows(): partial = keep + got]
    unnamed x4 -> x5, local copies, waits for them, and re-layouts: 0.01 us -> 3.48 us
  transfers between devices with their start and end apart: 4 -> 10, of which waited for: 4 -> 10; matrix products, arithmetic and copies ran while one was open for 0% -> 3% of each run, Pallas kernels for 0% -> 0%
where the time goes in v5:
time: 232 us; the launch traced here: 231 us
  waiting for transfers between devices  147 us (63%)
  starting transfers between devices  26.2 us (11%)
  other arithmetic  16.4 us (7%)
  between operations  15.5 us (7%)
  local copies, waits for them, and re-layouts  12.4 us (5%)
  matrix products  7.42 us (3%)
  blocking collectives  5.74 us (2%)
    all_gather x1, waiting for transfers between devices, gather_receivers(): full = lax.all_gather(full, 'y', axis=0, tiled=False)  54.1 us
    ppermute x3, waiting for transfers between devices, reduce_rows(): got_lo = lax.ppermute(acc_lo, 'zh', fwd)  37.1 us
    all_gather x1, waiting for transfers between devices, gather_receivers(): full = lax.all_gather(full, 'x', axis=0, tiled=False)  25.8 us
    all_to_all x1, waiting for transfers between devices, gather_receivers(): got = lax.all_to_all(pieces, SHOT, 0, 0, tiled=True)  15.3 us
    ppermute x3, starting transfers between devices, reduce_rows(): got_lo = lax.ppermute(acc_lo, 'zh', fwd)  11.7 us
    all_to_all x1, starting transfers between devices, gather_receivers(): got = lax.all_to_all(pieces, SHOT, 0, 0, tiled=True)  8.96 us
    ppermute x3, waiting for transfers between devices, reduce_rows(): got_hi = lax.ppermute(acc_hi, 'zh', bwd)  8.79 us
    dot_general x1, matrix products, body(): lax.dot_general(live, weights, (((0, 3), (0, 2)), ((1,), (1,))), preferre...  7.42 us
  transfers between devices with their start and end apart: 10, of which 10 were waited for; matrix products, arithmetic and copies ran while one was open for 3% of the time, Pallas kernels for 0%

profile of v5, /device:TPU:6, one launch (start us, length us, event | category | flops | bytes accessed | tf_op | source)
XLA Modules:
  0.0 230.7 jit_solution(12154943423017060959)
XLA Ops:
  10.1 2.3 constant_dynamic-slice_fusion.2
  12.4 9.0 %all-to-all-start = ((bf16[32,64,256]{2,1,0:T(8,128)(2,1)}), bf16[32,64,256]{2,1,0:T(8,128)(2,1)S(1)}, u32[]{:S(2)}, u32[]{:S(2)}) async-start(bf16[32,64,256]{2,1,0:T(8,128)(2,1)} %bitcast), calls=%async_computation | async-start | bytes 2097152 | tf_op jit(solution)/shard_map/all_to_all | solution.py:22
  21.7 15.3 %all-to-all-done = bf16[32,64,256]{2,1,0:T(8,128)(2,1)S(1)} async-done(((bf16[32,64,256]{2,1,0:T(8,128)(2,1)}), bf16[32,64,256]{2,1,0:T(8,128)(2,1)S(1)}, u32[]{:S(2)}, u32[]{:S(2)}) %all-to-all-start) | async-done | bytes 1048608 | tf_op jit(solution)/shard_map/all_to_all | solution.py:22
  37.6 5.7 %all_gather.16 = bf16[2,4,64,256]{3,2,1,0:T(8,128)(2,1)} all-gather(bf16[1,4,64,256]{3,2,1,0:T(8,128)(2,1)S(1)} %bitcast_select_fusion), channel_id=1, replica_groups=mesh['x'=4,'y'=4,'zl'=2,'zh'=4,'c'=2] {'zl'}, dimensions={0}, use_global_device_ids=true | all-gather | bytes 393216 | tf_op jit(solution)/shard_map/all_gather | solution.py:24
  43.5 25.8 %all-gather.5.cloned.1.call-done = bf16[8,4,64,256]{3,2,1,0:T(8,128)(2,1)} async-done(((bf16[2,4,64,256]{3,2,1,0:T(8,128)(2,1)}), bf16[8,4,64,256]{3,2,1,0:T(8,128)(2,1)}) %all-gather.5.cloned.1.call-update) | async-done | bytes 1048592 | tf_op jit(solution)/shard_map/all_gather | solution.py:25
  69.3 54.1 %all-gather.7.cloned.1.call-done = bf16[16,2,4,64,256]{4,3,2,1,0:T(8,128)(2,1)} async-done(((bf16[4,2,4,64,256]{4,3,2,1,0:T(8,128)(2,1)}), bf16[16,2,4,64,256]{4,3,2,1,0:T(8,128)(2,1)}) %all-gather.7.cloned.1.call-update) | async-done | bytes 4194320 | tf_op jit(solution)/shard_map/all_gather | solution.py:26
  123.4 2.6 %slice_bitcast_fusion = (bf16[2,4,4,2,64,256]{5,4,2,3,0,1:T(8,128)(2,1)S(1)}, bf16[2,4,4,2,64,256]{5,4,2,3,0,1:T(8,128)(2,1)S(1)}) fusion(bf16[4,2,2,2,4,64,256]{6,5,4,3,2,1,0:T(8,128)(2,1)} %bitcast.56), kind=kLoop, calls=%fused_computation.12 | loop fusion | bytes 8388608 | tf_op jit(solution)/shard_map/transpose | solution.py:31
  126.9 2.3 %maximum_bitcast_fusion = (bf16[1,8,512,512]{3,2,1,0:T(8,128)(2,1)S(1)}, bf16[1,8,512,512]{3,2,1,0:T(8,128)(2,1)}) fusion(bf16[8,512,256]{2,1,0:T(8,128)(2,1)S(1)} %bitcast.53, bf16[8,512,256]{2,1,0:T(8,128)(2,1)S(1)} %bitcast.54, bf16[8,512,256]{2,1,0:T(8,128)(2,1)S(1)} %neg.3), kind=kLoop, calls=%fused_computation.6 | loop fusion | flops 16777216 | bytes 14680064 | tf_op jit(solution)/shard_map/stack | solution.py:70
  129.2 7.4 %fusion = f32[8,384,512,1]{2,1,0,3:T(8,128)S(1)} fusion(bf16[1,8,512,512]{3,2,1,0:T(8,128)(2,1)} %get-tuple-element.16, bf16[1,8,512,512]{3,2,1,0:T(8,128)(2,1)S(1)} %get-tuple-element.15, bf16[2,8,384,512]{3,2,1,0:T(8,128)(2,1)} %param.4, bf16[384,512]{1,0:T(8,128)(2,1)S(1)} %convert_element_type.7), kind=kOutput, calls=%fused_computation.1 | convolution fusion | flops 3228565504 | bytes 21364736 | tf_op jit(solution)/shard_map/dot_general | solution.py:73
  137.4 3.5 %copy.28 = f32[4,1,48,8,512]{4,3,2,0,1:T(8,128)} copy(f32[4,1,48,8,512]{4,2,1,0,3:T(8,128)S(1)} %get-tuple-element.10) | data formatting | bytes 6291456
  140.9 6.0 %collective-permute-done = f32[4,48,8,512]{3,2,1,0:T(8,128)} collective-permute-done((f32[4,48,8,512]{3,2,1,0:T(8,128)}, f32[4,48,8,512]{3,2,1,0:T(8,128)}, u32[]{:S(2)}, u32[]{:S(2)}) %collective-permute-start) | collective-permute-done | bytes 3145760 | tf_op jit(solution)/shard_map/ppermute | solution.py:46
  146.9 4.1 %fusion.5 = f32[4,48,8,512]{3,2,1,0:T(8,128)S(1)} fusion(f32[4,48,8,512]{3,2,1,0:T(8,128)} %collective-permute-done, f32[4,1,48,8,512]{4,2,1,0,3:T(8,128)S(1)} %get-tuple-element.9), kind=kLoop, calls=%fused_computation.10 | loop fusion | flops 786432 | bytes 9437184 | tf_op jit(solution)/shard_map/add | solution.py:47
  151.5 2.8 %collective-permute-start.1 = (f32[24,8,512]{2,1,0:T(8,128)S(1)}, f32[24,8,512]{2,1,0:T(8,128)}, u32[]{:S(2)}, u32[]{:S(2)}) collective-permute-start(f32[24,8,512]{2,1,0:T(8,128)S(1)} %dynamic-slice_bitcast_fusion.1), channel_id=1, source_target_pairs={{0,2},{2,4},{4,6},{6,0},{1,3},{3,5},{5,7},{7,1},{8,10},{10,12},{12... | collective-permute-start | bytes 1179656 | tf_op jit(solution)/shard_map/ppermute | solution.py:59
  156.7 13.8 %collective-permute-done.1 = f32[24,8,512]{2,1,0:T(8,128)} collective-permute-done((f32[24,8,512]{2,1,0:T(8,128)S(1)}, f32[24,8,512]{2,1,0:T(8,128)}, u32[]{:S(2)}, u32[]{:S(2)}) %collective-permute-start.1) | collective-permute-done | bytes 393248 | tf_op jit(solution)/shard_map/ppermute | solution.py:59
  171.6 4.6 %collective-permute-start.2 = (f32[24,8,512]{2,1,0:T(8,128)S(1)}, f32[24,8,512]{2,1,0:T(8,128)}, u32[]{:S(2)}, u32[]{:S(2)}) collective-permute-start(f32[24,8,512]{2,1,0:T(8,128)S(1)} %bitcast_add_fusion.5), channel_id=1, source_target_pairs={{0,2},{2,4},{4,6},{6,0},{1,3},{3,5},{5,7},{7,1},{8,10},{10,12},{12... | collective-permute-start | bytes 1179656 | tf_op jit(solution)/shard_map/ppermute | solution.py:59
  176.7 1.8 bitcast_add_fusion.2
  178.5 2.0 collective-permute-start.5
  180.5 12.4 %collective-permute-done.2 = f32[24,8,512]{2,1,0:T(8,128)} collective-permute-done((f32[24,8,512]{2,1,0:T(8,128)S(1)}, f32[24,8,512]{2,1,0:T(8,128)}, u32[]{:S(2)}, u32[]{:S(2)}) %collective-permute-start.2) | collective-permute-done | bytes 393248 | tf_op jit(solution)/shard_map/ppermute | solution.py:59
  192.9 1.8 bitcast_add_fusion.4
  194.7 4.3 %collective-permute-start.3 = (f32[24,8,512]{2,1,0:T(8,128)}, f32[24,8,512]{2,1,0:T(8,128)S(1)}, u32[]{:S(2)}, u32[]{:S(2)}) collective-permute-start(f32[24,8,512]{2,1,0:T(8,128)} %bitcast_add_fusion.4), channel_id=1, source_target_pairs={{0,2},{2,4},{4,6},{6,0},{1,3},{3,5},{5,7},{7,1},{8,10},{10,12},{12... | collective-permute-start | bytes 1179656 | tf_op jit(solution)/shard_map/ppermute | solution.py:59
  199.9 1.8 bitcast_add_fusion.1
  201.7 1.8 collective-permute-start.6
  203.5 10.9 %collective-permute-done.3 = f32[24,8,512]{2,1,0:T(8,128)S(1)} collective-permute-done((f32[24,8,512]{2,1,0:T(8,128)}, f32[24,8,512]{2,1,0:T(8,128)S(1)}, u32[]{:S(2)}, u32[]{:S(2)}) %collective-permute-start.3) | collective-permute-done | bytes 393248 | tf_op jit(solution)/shard_map/ppermute | solution.py:59
  214.4 7.4 %collective-permute-done.6 = f32[24,8,512]{2,1,0:T(8,128)} collective-permute-done((f32[24,8,512]{2,1,0:T(8,128)}, f32[24,8,512]{2,1,0:T(8,128)}, u32[]{:S(2)}, u32[]{:S(2)}) %collective-permute-start.6) | collective-permute-done | bytes 393248 | tf_op jit(solution)/shard_map/ppermute | solution.py:60
  (32 shorter events, 11.8 us)
Async XLA Ops:
  6.5 14.9 %copy-start.1 = (s32[4,8]{1,0:T(4,128)S(1)}, s32[4,8]{1,0:T(4,128)}, u32[]{:S(2)}) copy-start(s32[4,8]{1,0:T(4,128)} %param.7) | copy-start | bytes 388
  6.5 62.7 %copy-start = (s32[384,512]{1,0:T(8,128)S(1)}, s32[384,512]{1,0:T(8,128)}, u32[]{:S(2)}) copy-start(s32[384,512]{1,0:T(8,128)} %param.5) | copy-start | bytes 2359300
  12.4 24.6 %all-to-all-start = ((bf16[32,64,256]{2,1,0:T(8,128)(2,1)}), bf16[32,64,256]{2,1,0:T(8,128)(2,1)S(1)}, u32[]{:S(2)}, u32[]{:S(2)}) async-start(bf16[32,64,256]{2,1,0:T(8,128)(2,1)} %bitcast), calls=%async_computation | async-start | bytes 2097152 | tf_op jit(solution)/shard_map/all_to_all | solution.py:22
  21.4 47.8 %all-gather.5.cloned.1.call-start = ((), (), s32[]{:S(2)}) async-start(), calls=%async_computation.1 | async-start | bytes 1310720 | tf_op jit(solution)/shard_map/all_gather | solution.py:25
  43.4 80.0 %all-gather.7.cloned.1.call-start = ((), (), s32[]{:S(2)}) async-start(), calls=%async_computation.2 | async-start | bytes 5242880 | tf_op jit(solution)/shard_map/all_gather | solution.py:26
  140.9 6.0 %collective-permute-start = (f32[4,48,8,512]{3,2,1,0:T(8,128)}, f32[4,48,8,512]{3,2,1,0:T(8,128)}, u32[]{:S(2)}, u32[]{:S(2)}) collective-permute-start(f32[4,48,8,512]{3,2,1,0:T(8,128)} %bitcast.51), channel_id=1, source_target_pairs={{0,1},{1,0},{2,3},{3,2},{4,5},{5,4},{6,7},{7,6},{8,9},{9,8},{10,11... | collective-permute-start | bytes 9437192 | tf_op jit(solution)/shard_map/ppermute | solution.py:46
  151.5 19.0 %collective-permute-start.1 = (f32[24,8,512]{2,1,0:T(8,128)S(1)}, f32[24,8,512]{2,1,0:T(8,128)}, u32[]{:S(2)}, u32[]{:S(2)}) collective-permute-start(f32[24,8,512]{2,1,0:T(8,128)S(1)} %dynamic-slice_bitcast_fusion.1), channel_id=1, source_target_pairs={{0,2},{2,4},{4,6},{6,0},{1,3},{3,5},{5,7},{7,1},{8,10},{10,12},{12... | collective-permute-start | bytes 1179656 | tf_op jit(solution)/shard_map/ppermute | solution.py:59
  155.1 21.6 %collective-permute-start.4 = (f32[24,8,512]{2,1,0:T(8,128)}, f32[24,8,512]{2,1,0:T(8,128)}, u32[]{:S(2)}, u32[]{:S(2)}) collective-permute-start(f32[24,8,512]{2,1,0:T(8,128)} %dynamic-slice_bitcast_fusion), channel_id=1, source_target_pairs={{0,6},{2,0},{4,2},{6,4},{1,7},{3,1},{5,3},{7,5},{8,14},{10,8},{12,... | collective-permute-start | bytes 1179656 | tf_op jit(solution)/shard_map/ppermute | solution.py:60
  171.6 21.3 %collective-permute-start.2 = (f32[24,8,512]{2,1,0:T(8,128)S(1)}, f32[24,8,512]{2,1,0:T(8,128)}, u32[]{:S(2)}, u32[]{:S(2)}) collective-permute-start(f32[24,8,512]{2,1,0:T(8,128)S(1)} %bitcast_add_fusion.5), channel_id=1, source_target_pairs={{0,2},{2,4},{4,6},{6,0},{1,3},{3,5},{5,7},{7,1},{8,10},{10,12},{12... | collective-permute-start | bytes 1179656 | tf_op jit(solution)/shard_map/ppermute | solution.py:59
  178.5 21.4 %collective-permute-start.5 = (f32[24,8,512]{2,1,0:T(8,128)}, f32[24,8,512]{2,1,0:T(8,128)}, u32[]{:S(2)}, u32[]{:S(2)}) collective-permute-start(f32[24,8,512]{2,1,0:T(8,128)} %bitcast_add_fusion.2), channel_id=1, source_target_pairs={{0,6},{2,0},{4,2},{6,4},{1,7},{3,1},{5,3},{7,5},{8,14},{10,8},{12,... | collective-permute-start | bytes 1179656 | tf_op jit(solution)/shard_map/ppermute | solution.py:60
  194.7 19.6 %collective-permute-start.3 = (f32[24,8,512]{2,1,0:T(8,128)}, f32[24,8,512]{2,1,0:T(8,128)S(1)}, u32[]{:S(2)}, u32[]{:S(2)}) collective-permute-start(f32[24,8,512]{2,1,0:T(8,128)} %bitcast_add_fusion.4), channel_id=1, source_target_pairs={{0,2},{2,4},{4,6},{6,0},{1,3},{3,5},{5,7},{7,1},{8,10},{10,12},{12... | collective-permute-start | bytes 1179656 | tf_op jit(solution)/shard_map/ppermute | solution.py:59
  201.7 20.1 %collective-permute-start.6 = (f32[24,8,512]{2,1,0:T(8,128)}, f32[24,8,512]{2,1,0:T(8,128)}, u32[]{:S(2)}, u32[]{:S(2)}) collective-permute-start(f32[24,8,512]{2,1,0:T(8,128)} %bitcast_add_fusion.1), channel_id=1, source_target_pairs={{0,6},{2,0},{4,2},{6,4},{1,7},{3,1},{5,3},{7,5},{8,14},{10,8},{12,... | collective-permute-start | bytes 1179656 | tf_op jit(solution)/shard_map/ppermute | solution.py:60
Sparse Core Ops, SparseCore 0:
  43.5 25.6 all-gather.4
  71.0 52.3 all-gather.6

commit v6 on v4

--- a/solution.py
+++ b/solution.py
@@ -22,9 +22,9 @@
     got = lax.all_to_all(pieces, SHOT, 0, 0, tiled=True)
     chosen = jnp.take(got, column, axis=0)
     full = lax.all_gather(chosen, "zl", axis=0, tiled=False)
-    full = lax.all_gather(full, "x", axis=0, tiled=False)
-    full = lax.all_gather(full, "y", axis=0, tiled=False)
-    n_y, n_x, n_zl = full.shape[:3]
+    n_y, n_x, n_zl = lax.psum(1, "y"), lax.psum(1, "x"), full.shape[0]
+    full = lax.all_gather(full, ("y", "x"), axis=0, tiled=False)
+    full = full.reshape(n_y, n_x, *full.shape[1:])
     full = full.reshape(n_y, parts, n_x // parts, n_zl, STEPS, kb // split, recv)
 
     def part_of(p):

time: 227 us -> 204 us (0.90)
  waiting for transfers between devices: 176 us -> 152 us
    all_gather x2 -> x1, waiting for transfers between devices: 79.8 us -> 56.6 us  [gather_receivers(): full = lax.all_gather(full, ('y', 'x'), axis=0, tiled=False)]
  transfers between devices with their start and end apart: 4 -> 3, of which waited for: 4 -> 3; matrix products, arithmetic and copies ran while one was open for 0% -> 0% of each run, Pallas kernels for 0% -> 0%
where the time goes in v6:
time: 204 us; the launch traced here: 203 us
  waiting for transfers between devices  152 us (75%)
  between operations  15.6 us (8%)
  starting transfers between devices  9.04 us (4%)
  matrix products  8.87 us (4%)
  local copies, waits for them, and re-layouts  7.21 us (4%)
  blocking collectives  5.74 us (3%)
  other arithmetic  4.41 us (2%)
    reduce_scatter x1, waiting for transfers between devices, body(): out = lax.psum_scatter(out, SP, scatter_dimension=0, tiled=True)  80.5 us
    all_gather x1, waiting for transfers between devices, gather_receivers(): full = lax.all_gather(full, ('y', 'x'), axis=0, tiled=False)  56.6 us
    all_to_all x1, waiting for transfers between devices, gather_receivers(): got = lax.all_to_all(pieces, SHOT, 0, 0, tiled=True)  15.3 us
    all_to_all x1, starting transfers between devices, gather_receivers(): got = lax.all_to_all(pieces, SHOT, 0, 0, tiled=True)  8.96 us
    dot_general x1, matrix products, body(): lax.dot_general(live, weights, (((0, 3), (0, 2)), ((1,), (1,))), preferre...  8.87 us
    all_gather x1, blocking collectives, gather_receivers(): full = lax.all_gather(chosen, 'zl', axis=0, tiled=False)  5.74 us
  transfers between devices with their start and end apart: 3, of which 3 were waited for; matrix products, arithmetic and copies ran while one was open for 0% of the time, Pallas kernels for 0%

profile of v6, /device:TPU:6, one launch (start us, length us, event | category | flops | bytes accessed | tf_op | source)
XLA Modules:
  0.0 203.3 jit_solution(8306458426076461595)
XLA Ops:
  6.5 1.0 and_reduce_fusion
  7.5 0.7 iota_reduce_fusion
  10.3 2.3 %constant_dynamic-slice_fusion = bf16[1,2,8,128,256]{4,3,2,1,0:T(8,128)(2,1)} fusion(bf16[4,2,8,128,256]{4,3,2,1,0:T(8,128)(2,1)} %param.6, s32[]{:T(128)S(6)} %select_n.32), kind=kLoop, calls=%fused_computation.20 | loop fusion | bytes 2097156 | tf_op jit(solution)/shard_map/jit(dynamic_index_in_dim)/dynamic_slice | solution.py:18
  12.6 9.0 %all-to-all-start = ((bf16[32,64,256]{2,1,0:T(8,128)(2,1)}), bf16[32,64,256]{2,1,0:T(8,128)(2,1)S(1)}, u32[]{:S(2)}, u32[]{:S(2)}) async-start(bf16[32,64,256]{2,1,0:T(8,128)(2,1)} %bitcast), calls=%async_computation | async-start | bytes 2097152 | tf_op jit(solution)/shard_map/all_to_all | solution.py:22
  21.6 0.0 all-gather.3.cloned.1.call-start
  21.7 0.2 fusion.11
  21.9 15.3 %all-to-all-done = bf16[32,64,256]{2,1,0:T(8,128)(2,1)S(1)} async-done(((bf16[32,64,256]{2,1,0:T(8,128)(2,1)}), bf16[32,64,256]{2,1,0:T(8,128)(2,1)S(1)}, u32[]{:S(2)}, u32[]{:S(2)}) %all-to-all-start) | async-done | bytes 1048608 | tf_op jit(solution)/shard_map/all_to_all | solution.py:22
  37.2 0.6 gather_fusion
  37.8 0.1 bitcast_select_fusion
  37.8 5.7 %all_gather.10 = bf16[2,4,64,256]{3,2,1,0:T(8,128)(2,1)} all-gather(bf16[1,4,64,256]{3,2,1,0:T(8,128)(2,1)S(1)} %bitcast_select_fusion), channel_id=1, replica_groups=mesh['x'=4,'y'=4,'zl'=2,'zh'=4,'c'=2] {'zl'}, dimensions={0}, use_global_device_ids=true | all-gather | bytes 393216 | tf_op jit(solution)/shard_map/all_gather | solution.py:24
  43.6 0.0 all-gather.3.cloned.1.call-update
  43.6 0.0 reduce-scatter.2.cloned.1.call-start
  43.7 0.1 convert_element_type.9
  43.7 56.6 %all-gather.3.cloned.1.call-done = bf16[32,4,64,256]{3,2,1,0:T(8,128)(2,1)} async-done(((bf16[2,4,64,256]{3,2,1,0:T(8,128)(2,1)}), bf16[32,4,64,256]{3,2,1,0:T(8,128)(2,1)}) %all-gather.3.cloned.1.call-update) | async-done | bytes 4194320 | tf_op jit(solution)/shard_map/all_gather | solution.py:26
  100.4 2.6 %slice_bitcast_fusion = (bf16[2,4,4,2,64,256]{5,4,2,3,0,1:T(8,128)(2,1)S(1)}, bf16[2,4,4,2,64,256]{5,4,2,3,0,1:T(8,128)(2,1)S(1)}) fusion(bf16[4,2,2,2,4,64,256]{6,5,4,3,2,1,0:T(8,128)(2,1)} %bitcast.30), kind=kLoop, calls=%fused_computation.10 | loop fusion | bytes 8388608 | tf_op jit(solution)/shard_map/transpose | solution.py:31
  103.0 0.2 copy.14
  103.2 0.4 neg.3
  103.7 0.2 copy.13
  103.9 0.8 maximum_bitcast_fusion
  104.7 8.9 %fusion.6 = f32[384,8,512]{2,0,1:T(8,128)} fusion(bf16[1,8,512,512]{3,2,1,0:T(8,128)(2,1)S(1)} %get-tuple-element.12, bf16[1,8,512,512]{3,2,1,0:T(8,128)(2,1)S(1)} %get-tuple-element.11, bf16[2,8,384,512]{3,2,1,0:T(8,128)(2,1)} %param.4, bf16[384,512]{1,0:T(8,128)(2,1)S(1)} %convert_element_type.9), kind=kOutput, calls=%fused_computation.9 | convolution fusion | flops 3228565504 | bytes 21364736 | tf_op jit(solution)/shard_map/dot_general | solution.py:43
  113.6 80.5 %reduce-scatter.2.cloned.1.call-done = f32[48,8,512]{2,0,1:T(8,128)} async-done(((f32[384,8,512]{2,0,1:T(8,128)}), f32[48,8,512]{2,0,1:T(8,128)}) %reduce-scatter.2.cloned.1.call-update) | async-done | bytes 786448 | tf_op jit(solution)/shard_map/reduce_scatter | solution.py:47
  194.0 1.2 convert_element_type.10
  195.2 0.1 convert_element_type.11
  195.3 1.2 copy.17
  (6 shorter events, 0.0 us)
Async XLA Ops:
  6.5 15.1 %copy-start.1 = (s32[4,8]{1,0:T(4,128)S(1)}, s32[4,8]{1,0:T(4,128)}, u32[]{:S(2)}) copy-start(s32[4,8]{1,0:T(4,128)} %param.7) | copy-start | bytes 388
  6.5 37.1 %copy-start = (s32[384,512]{1,0:T(8,128)S(1)}, s32[384,512]{1,0:T(8,128)}, u32[]{:S(2)}) copy-start(s32[384,512]{1,0:T(8,128)} %param.5) | copy-start | bytes 2359300
  12.6 24.6 %all-to-all-start = ((bf16[32,64,256]{2,1,0:T(8,128)(2,1)}), bf16[32,64,256]{2,1,0:T(8,128)(2,1)S(1)}, u32[]{:S(2)}, u32[]{:S(2)}) async-start(bf16[32,64,256]{2,1,0:T(8,128)(2,1)} %bitcast), calls=%async_computation | async-start | bytes 2097152 | tf_op jit(solution)/shard_map/all_to_all | solution.py:22
  21.6 78.8 %all-gather.3.cloned.1.call-start = ((), (), s32[]{:S(2)}) async-start(), calls=%async_computation.3 | async-start | bytes 4456448 | tf_op jit(solution)/shard_map/all_gather | solution.py:26
  43.6 150.4 %reduce-scatter.2.cloned.1.call-start = ((), (), s32[]{:S(2)}) async-start(), calls=%async_computation.2 | async-start | bytes 7077888 | tf_op jit(solution)/shard_map/reduce_scatter | solution.py:47
Sparse Core Ops, SparseCore 0:
  43.7 56.5 all-gather.2
  113.7 80.2 reduce-scatter.1

commit v7 on v5

--- a/solution.py
+++ b/solution.py
@@ -8,27 +8,30 @@
 SP = ("zh", "c")
 
 
-def gather_receivers(spectra, plan):
+def gather_receivers(spectra, plan, group, n_groups, after=None):
     n_shot = lax.psum(1, SHOT)
     sp_index = lax.axis_index(SP)
     shot_index = lax.axis_index(SHOT)
     column = lax.dynamic_index_in_dim(plan, sp_index, 1, keepdims=False)
-    mine = column == shot_index
-    owned_step = jnp.argmax(mine)
+    owned_step = jnp.argmax(column == shot_index)
     block = lax.dynamic_index_in_dim(spectra, owned_step, 0, keepdims=False)
     parts, freq, kb, recv = block.shape
-    split = n_shot // (parts * freq)
-    pieces = block.reshape(parts * freq * split, kb // split, recv)
+    fg = freq // n_groups
+    block = block[:, group * fg : (group + 1) * fg]
+    quarters = n_shot // (parts * fg)
+    pieces = block.reshape(n_shot, kb // quarters, recv)
+    if after is not None:
+        pieces = pieces + (after[0, 0, 0] * 0).astype(pieces.dtype)
     got = lax.all_to_all(pieces, SHOT, 0, 0, tiled=True)
     chosen = jnp.take(got, column, axis=0)
     full = lax.all_gather(chosen, "zl", axis=0, tiled=False)
-    full = lax.all_gather(full, "x", axis=0, tiled=False)
-    full = lax.all_gather(full, "y", axis=0, tiled=False)
-    n_y, n_x, n_zl = full.shape[:3]
-    full = full.reshape(n_y, parts, n_x // parts, n_zl, STEPS, kb // split, recv)
+    n_y, n_x, n_zl = lax.psum(1, "y"), lax.psum(1, "x"), full.shape[0]
+    full = lax.all_gather(full, ("y", "x"), axis=0, tiled=False)
+    full = full.reshape(n_y, n_x, *full.shape[1:])
+    full = full.reshape(n_y // 2, 2, parts, n_x // parts, n_zl, STEPS, kb // quarters, recv)
 
     def part_of(p):
-        return jnp.transpose(full[:, p], (1, 0, 3, 2, 4, 5)).reshape(freq, STEPS * kb, recv)
+        return jnp.transpose(full[:, :, p], (2, 0, 4, 1, 3, 5, 6)).reshape(fg, STEPS * kb, recv)
 
     return part_of(0), part_of(1)
 
@@ -64,17 +67,29 @@
 
 
 def body(shot_data, live_masks, spectra, plan):
-    live = shot_data * live_masks.astype(shot_data.dtype)[None, None]
-    real_in, imag_in = gather_receivers(spectra, plan)
-    freq, _, recv = real_in.shape
-    weights = jnp.stack(
-        [jnp.concatenate([real_in, imag_in], axis=-1), jnp.concatenate([-imag_in, real_in], axis=-1)], axis=0
-    )
-    out = lax.dot_general(
-        live, weights, (((0, 3), (0, 2)), ((1,), (1,))), preferred_element_type=jnp.float32
-    )
-    out = jnp.transpose(out, (1, 0, 2))
-    out = reduce_rows(out)
+    mask = live_masks.astype(shot_data.dtype)[None, None]
+    freq = shot_data.shape[1]
+    n_groups = 2
+    fg = freq // n_groups
+    results = []
+    prev = None
+    for group in range(n_groups):
+        real_in, imag_in = gather_receivers(spectra, plan, group, n_groups, prev)
+        recv = real_in.shape[-1]
+        weights = jnp.stack(
+            [jnp.concatenate([real_in, imag_in], axis=-1), jnp.concatenate([-imag_in, real_in], axis=-1)], axis=0
+        )
+        if results:
+            both_halves = results[-1][0, 0, 0] + results[-1][-1, 0, 0]
+            weights = weights + (both_halves * 0).astype(weights.dtype)
+        live = shot_data[:, group * fg : (group + 1) * fg] * mask
+        out = lax.dot_general(
+            live, weights, (((0, 3), (0, 2)), ((1,), (1,))), preferred_element_type=jnp.float32
+        )
+        out = jnp.transpose(out, (1, 0, 2))
+        prev = out
+        results.append(reduce_rows(out))
+    out = jnp.concatenate(results, axis=1)
     rows = out.shape[0]
     out = out.reshape(rows, freq, 2, recv).astype(jnp.bfloat16)
     return jnp.transpose(out, (0, 2, 1, 3))

time: 232 us -> 225 us (0.970)
  waiting for transfers between devices: 147 us -> 130 us
  starting transfers between devices: 26.2 us -> 40.2 us
  other arithmetic: 16.4 us -> 5.35 us
  local copies, waits for them, and re-layouts: 12.4 us -> 16.9 us
  blocking collectives: 5.74 us -> 10.1 us
  matrix products: 7.42 us -> 3.73 us
    all_gather x2, waiting for transfers between devices: 79.8 us -> 51 us  [gather_receivers(): full = lax.all_gather(full, ('y', 'x'), axis=0, tiled=False)]
    ppermute x3 -> x6, waiting for transfers between devices: 8.79 us -> 27.9 us  [reduce_rows(): got_hi = lax.ppermute(acc_hi, 'zh', bwd)]
    ppermute x3 -> x6, waiting for transfers between devices: 37.1 us -> 25.2 us  [reduce_rows(): got_lo = lax.ppermute(acc_lo, 'zh', fwd)]
    ppermute x3 -> x6, starting transfers between devices: 5.41 us -> 13.2 us  [reduce_rows(): got_hi = lax.ppermute(acc_hi, 'zh', bwd)]
    all_to_all x1 -> x2, starting transfers between devices: 8.96 us -> 15.8 us  [gather_receivers(): got = lax.all_to_all(pieces, SHOT, 0, 0, tiled=True)]
    all_gather x1 -> x2, blocking collectives: 5.74 us -> 10.1 us  [gather_receivers(): full = lax.all_gather(chosen, 'zl', axis=0, tiled=False)]
    dot_general x1 -> x2, matrix products: 7.42 us -> 3.73 us  [body(): lax.dot_general(live, weights, (((0, 3), (0, 2)), ((1,), (1,))), preferre...]
    add x2 -> x4, other arithmetic: 3.59 us -> 0.11 us  [reduce_rows(): acc_hi = got_hi + chunk(hi, zh + step + 2)]
  transfers between devices with their start and end apart: 10 -> 18, of which waited for: 10 -> 17; matrix products, arithmetic and copies ran while one was open for 3% -> 3% of each run, Pallas kernels for 0% -> 0%
where the time goes in v7:
time: 225 us; the launch traced here: 223 us
  waiting for transfers between devices  130 us (58%)
  starting transfers between devices  40.2 us (18%)
  between operations  17.4 us (8%)
  local copies, waits for them, and re-layouts  16.9 us (8%)
  blocking collectives  10.1 us (4%)
  other arithmetic  5.35 us (2%)
  matrix products  3.73 us (2%)
    all_gather x2, waiting for transfers between devices, gather_receivers(): full = lax.all_gather(full, ('y', 'x'), axis=0, tiled=False)  51 us
    ppermute x6, waiting for transfers between devices, reduce_rows(): got_hi = lax.ppermute(acc_hi, 'zh', bwd)  27.9 us
    ppermute x6, waiting for transfers between devices, reduce_rows(): got_lo = lax.ppermute(acc_lo, 'zh', fwd)  25.2 us
    all_to_all x2, waiting for transfers between devices, gather_receivers(): got = lax.all_to_all(pieces, SHOT, 0, 0, tiled=True)  18.4 us
    all_to_all x2, starting transfers between devices, gather_receivers(): got = lax.all_to_all(pieces, SHOT, 0, 0, tiled=True)  15.8 us
    ppermute x6, starting transfers between devices, reduce_rows(): got_hi = lax.ppermute(acc_hi, 'zh', bwd)  13.2 us
    ppermute x6, starting transfers between devices, reduce_rows(): got_lo = lax.ppermute(acc_lo, 'zh', fwd)  10.9 us
    all_gather x2, blocking collectives, gather_receivers(): full = lax.all_gather(chosen, 'zl', axis=0, tiled=False)  10.1 us
  transfers between devices with their start and end apart: 18, of which 17 were waited for; matrix products, arithmetic and copies ran while one was open for 3% of the time, Pallas kernels for 0%

profile of v7, /device:TPU:6, one launch (start us, length us, event | category | flops | bytes accessed | tf_op | source)
XLA Modules:
  0.0 223.2 jit_solution(10673550949270507753)
XLA Ops:
  12.0 9.0 %all-to-all-start = ((bf16[32,32,256]{2,1,0:T(8,128)(2,1)}), bf16[32,32,256]{2,1,0:T(8,128)(2,1)S(1)}, u32[]{:S(2)}, u32[]{:S(2)}) async-start(bf16[32,32,256]{2,1,0:T(8,128)(2,1)} %bitcast.1), calls=%async_computation | async-start | bytes 1048576 | tf_op jit(solution)/shard_map/all_to_all | solution.py:25
  21.0 9.9 %all-to-all-done = bf16[32,32,256]{2,1,0:T(8,128)(2,1)S(1)} async-done(((bf16[32,32,256]{2,1,0:T(8,128)(2,1)}), bf16[32,32,256]{2,1,0:T(8,128)(2,1)S(1)}, u32[]{:S(2)}, u32[]{:S(2)}) %all-to-all-start) | async-done | bytes 524320 | tf_op jit(solution)/shard_map/all_to_all | solution.py:25
  31.6 5.0 %all-gather = bf16[8,32,256]{2,1,0:T(8,128)(2,1)} all-gather(bf16[4,32,256]{2,1,0:T(8,128)(2,1)S(1)} %broadcast_select_fusion.1), channel_id=2, replica_groups=mesh['x'=4,'y'=4,'zl'=2,'zh'=4,'c'=2] {'zl'}, dimensions={0}, use_global_device_ids=true | all-gather | bytes 196608 | tf_op jit(solution)/shard_map/all_gather | solution.py:27
  36.7 49.9 %all-gather.7.cloned.1.call-done = bf16[32,4,32,256]{3,2,1,0:T(8,128)(2,1)} async-done(((bf16[2,4,32,256]{3,2,1,0:T(8,128)(2,1)}), bf16[32,4,32,256]{3,2,1,0:T(8,128)(2,1)}) %all-gather.7.cloned.1.call-update) | async-done | bytes 2097168 | tf_op jit(solution)/shard_map/all_gather | solution.py:29
  94.5 6.9 %all-to-all-start.1 = ((bf16[32,32,256]{2,1,0:T(8,128)(2,1)}), bf16[32,32,256]{2,1,0:T(8,128)(2,1)S(1)}, u32[]{:S(2)}, u32[]{:S(2)}) async-start(bf16[32,32,256]{2,1,0:T(8,128)(2,1)} %bitcast.28), calls=%async_computation.1 | async-start | bytes 1048576 | tf_op jit(solution)/shard_map/all_to_all | solution.py:25
  101.4 8.5 %all-to-all-done.1 = bf16[32,32,256]{2,1,0:T(8,128)(2,1)S(1)} async-done(((bf16[32,32,256]{2,1,0:T(8,128)(2,1)}), bf16[32,32,256]{2,1,0:T(8,128)(2,1)S(1)}, u32[]{:S(2)}, u32[]{:S(2)}) %all-to-all-start.1) | async-done | bytes 524320 | tf_op jit(solution)/shard_map/all_to_all | solution.py:25
  110.6 5.0 %all-gather.2 = bf16[8,32,256]{2,1,0:T(8,128)(2,1)} all-gather(bf16[4,32,256]{2,1,0:T(8,128)(2,1)S(1)} %broadcast_select_fusion), channel_id=4, replica_groups=mesh['x'=4,'y'=4,'zl'=2,'zh'=4,'c'=2] {'zl'}, dimensions={0}, use_global_device_ids=true | all-gather | bytes 196608 | tf_op jit(solution)/shard_map/all_gather | solution.py:27
  115.7 2.2 %constant_dynamic-slice_fusion.3 = (f32[4,1,48,4,512]{4,2,1,0,3:T(8,128)S(1)}, f32[4,1,48,4,512]{4,2,1,0,3:T(8,128)S(1)}) fusion(f32[4,2,48,4,512]{4,2,1,0,3:T(8,128)} %bitcast.108, s32[]{:T(128)S(6)} %select_n.112, s32[]{:T(128)S(6)} %select_n.113), kind=kLoop, calls=%fused_computation.56 | loop fusion | bytes 6291464 | tf_op jit(solution)/shard_map/jit(dynamic_index_in_dim)/dynamic_slice | solution.py:48
  118.2 3.5 %collective-permute-done = f32[4,48,4,512]{3,1,2,0:T(8,128)} collective-permute-done((f32[4,48,4,512]{3,1,2,0:T(8,128)S(1)}, f32[4,48,4,512]{3,1,2,0:T(8,128)}, u32[]{:S(2)}, u32[]{:S(2)}) %collective-permute-start) | collective-permute-done | bytes 1572896 | tf_op jit(solution)/shard_map/ppermute | solution.py:49
  123.6 3.3 %collective-permute-start.4 = (f32[24,4,512]{2,0,1:T(8,128)S(1)}, f32[24,4,512]{2,0,1:T(8,128)S(1)}, u32[]{:S(2)}, u32[]{:S(2)}) collective-permute-start(f32[24,4,512]{2,0,1:T(8,128)S(1)} %dynamic-slice_bitcast_fusion.3), channel_id=1, source_target_pairs={{0,6},{2,0},{4,2},{6,4},{1,7},{3,1},{5,3},{7,5},{8,14},{10,8},{12,... | collective-permute-start | bytes 589832 | tf_op jit(solution)/shard_map/ppermute | solution.py:63
  127.0 8.7 %collective-permute-done.4 = f32[24,4,512]{2,0,1:T(8,128)S(1)} collective-permute-done((f32[24,4,512]{2,0,1:T(8,128)S(1)}, f32[24,4,512]{2,0,1:T(8,128)S(1)}, u32[]{:S(2)}, u32[]{:S(2)}) %collective-permute-start.4) | collective-permute-done | bytes 196640 | tf_op jit(solution)/shard_map/ppermute | solution.py:63
  135.8 3.8 %collective-permute-start.5 = (f32[24,4,512]{2,0,1:T(8,128)S(1)}, f32[24,4,512]{2,0,1:T(8,128)S(1)}, u32[]{:S(2)}, u32[]{:S(2)}) collective-permute-start(f32[24,4,512]{2,0,1:T(8,128)S(1)} %bitcast_add_fusion.10), channel_id=1, source_target_pairs={{0,6},{2,0},{4,2},{6,4},{1,7},{3,1},{5,3},{7,5},{8,14},{10,8},{12,... | collective-permute-start | bytes 589832 | tf_op jit(solution)/shard_map/ppermute | solution.py:63
  139.8 7.7 %collective-permute-done.5 = f32[24,4,512]{2,0,1:T(8,128)S(1)} collective-permute-done((f32[24,4,512]{2,0,1:T(8,128)S(1)}, f32[24,4,512]{2,0,1:T(8,128)S(1)}, u32[]{:S(2)}, u32[]{:S(2)}) %collective-permute-start.5) | collective-permute-done | bytes 196640 | tf_op jit(solution)/shard_map/ppermute | solution.py:63
  149.4 2.2 %collective-permute-done.2 = f32[24,4,512]{2,0,1:T(8,128)S(1)} collective-permute-done((f32[24,4,512]{2,0,1:T(8,128)S(1)}, f32[24,4,512]{2,0,1:T(8,128)S(1)}, u32[]{:S(2)}, u32[]{:S(2)}) %collective-permute-start.2) | collective-permute-done | bytes 196640 | tf_op jit(solution)/shard_map/ppermute | solution.py:62
  151.9 4.3 %collective-permute-done.6 = f32[24,4,512]{2,0,1:T(8,128)S(1)} collective-permute-done((f32[24,4,512]{2,0,1:T(8,128)S(1)}, f32[24,4,512]{2,0,1:T(8,128)S(1)}, u32[]{:S(2)}, u32[]{:S(2)}) %collective-permute-start.6) | collective-permute-done | bytes 196640 | tf_op jit(solution)/shard_map/ppermute | solution.py:63
  156.8 4.5 %collective-permute-done.3 = f32[24,4,512]{2,0,1:T(8,128)S(1)} collective-permute-done((f32[24,4,512]{2,0,1:T(8,128)S(1)}, f32[24,4,512]{2,0,1:T(8,128)S(1)}, u32[]{:S(2)}, u32[]{:S(2)}) %collective-permute-start.3) | collective-permute-done | bytes 196640 | tf_op jit(solution)/shard_map/ppermute | solution.py:62
  170.6 3.4 %collective-permute-done.7 = f32[4,48,4,512]{3,1,2,0:T(8,128)S(1)} collective-permute-done((f32[4,48,4,512]{3,1,2,0:T(8,128)S(1)}, f32[4,48,4,512]{3,1,2,0:T(8,128)S(1)}, u32[]{:S(2)}, u32[]{:S(2)}) %collective-permute-start.7) | collective-permute-done | bytes 1572896 | tf_op jit(solution)/shard_map/ppermute | solution.py:49
  174.6 2.6 %collective-permute-start.8 = (f32[24,4,512]{2,0,1:T(8,128)S(1)}, f32[24,4,512]{2,0,1:T(8,128)S(1)}, u32[]{:S(2)}, u32[]{:S(2)}) collective-permute-start(f32[24,4,512]{2,0,1:T(8,128)S(1)} %dynamic-slice_bitcast_fusion.2), channel_id=1, source_target_pairs={{0,2},{2,4},{4,6},{6,0},{1,3},{3,5},{5,7},{7,1},{8,10},{10,12},{12... | collective-permute-start | bytes 589832 | tf_op jit(solution)/shard_map/ppermute | solution.py:62
  178.9 7.0 %collective-permute-done.8 = f32[24,4,512]{2,0,1:T(8,128)S(1)} collective-permute-done((f32[24,4,512]{2,0,1:T(8,128)S(1)}, f32[24,4,512]{2,0,1:T(8,128)S(1)}, u32[]{:S(2)}, u32[]{:S(2)}) %collective-permute-start.8) | collective-permute-done | bytes 196640 | tf_op jit(solution)/shard_map/ppermute | solution.py:62
  185.9 3.8 %collective-permute-start.9 = (f32[24,4,512]{2,0,1:T(8,128)S(1)}, f32[24,4,512]{2,0,1:T(8,128)S(1)}, u32[]{:S(2)}, u32[]{:S(2)}) collective-permute-start(f32[24,4,512]{2,0,1:T(8,128)S(1)} %bitcast_add_fusion.7), channel_id=1, source_target_pairs={{0,2},{2,4},{4,6},{6,0},{1,3},{3,5},{5,7},{7,1},{8,10},{10,12},{12... | collective-permute-start | bytes 589832 | tf_op jit(solution)/shard_map/ppermute | solution.py:62
  192.3 6.0 %collective-permute-done.9 = f32[24,4,512]{2,0,1:T(8,128)S(1)} collective-permute-done((f32[24,4,512]{2,0,1:T(8,128)S(1)}, f32[24,4,512]{2,0,1:T(8,128)S(1)}, u32[]{:S(2)}, u32[]{:S(2)}) %collective-permute-start.9) | collective-permute-done | bytes 196640 | tf_op jit(solution)/shard_map/ppermute | solution.py:62
  198.3 3.8 %collective-permute-start.10 = (f32[24,4,512]{2,0,1:T(8,128)S(1)}, f32[24,4,512]{2,0,1:T(8,128)S(1)}, u32[]{:S(2)}, u32[]{:S(2)}) collective-permute-start(f32[24,4,512]{2,0,1:T(8,128)S(1)} %bitcast_add_fusion.6), channel_id=1, source_target_pairs={{0,2},{2,4},{4,6},{6,0},{1,3},{3,5},{5,7},{7,1},{8,10},{10,12},{12... | collective-permute-start | bytes 589832 | tf_op jit(solution)/shard_map/ppermute | solution.py:62
  203.4 5.5 %collective-permute-done.10 = f32[24,4,512]{2,0,1:T(8,128)S(1)} collective-permute-done((f32[24,4,512]{2,0,1:T(8,128)S(1)}, f32[24,4,512]{2,0,1:T(8,128)S(1)}, u32[]{:S(2)}, u32[]{:S(2)}) %collective-permute-start.10) | collective-permute-done | bytes 196640 | tf_op jit(solution)/shard_map/ppermute | solution.py:62
  208.9 6.1 %collective-permute-done.13 = f32[24,4,512]{2,0,1:T(8,128)S(1)} collective-permute-done((f32[24,4,512]{2,0,1:T(8,128)S(1)}, f32[24,4,512]{2,0,1:T(8,128)S(1)}, u32[]{:S(2)}, u32[]{:S(2)}) %collective-permute-start.13) | collective-permute-done | bytes 196640 | tf_op jit(solution)/shard_map/ppermute | solution.py:63
  (89 shorter events, 33.1 us)
Async XLA Ops:
  9.8 26.9 %copy-start.3 = (s32[384,512]{1,0:T(8,128)S(1)}, s32[384,512]{1,0:T(8,128)}, u32[]{:S(2)}) copy-start(s32[384,512]{1,0:T(8,128)} %param.7) | copy-start | bytes 2359300
  12.0 18.9 %all-to-all-start = ((bf16[32,32,256]{2,1,0:T(8,128)(2,1)}), bf16[32,32,256]{2,1,0:T(8,128)(2,1)S(1)}, u32[]{:S(2)}, u32[]{:S(2)}) async-start(bf16[32,32,256]{2,1,0:T(8,128)(2,1)} %bitcast.1), calls=%async_computation | async-start | bytes 1048576 | tf_op jit(solution)/shard_map/all_to_all | solution.py:25
  21.0 65.6 %all-gather.7.cloned.1.call-start = ((), (), s32[]{:S(2)}) async-start(), calls=%async_computation.2 | async-start | bytes 2228224 | tf_op jit(solution)/shard_map/all_gather | solution.py:29
  86.6 2.8 %slice-start = ((s8[6291456]{0:T(1024)(128)(4,1)}), s8[4194304]{0:T(1024)(128)(4,1)S(1)}, s32[]{:S(2)}) async-start(s8[6291456]{0:T(1024)(128)(4,1)} %bitcast.116), calls=%async_computation.4 | async-start | bytes 8388608
  88.8 1.7 slice-start.1
  92.4 2.1 copy-start.2
  94.5 15.5 %all-to-all-start.1 = ((bf16[32,32,256]{2,1,0:T(8,128)(2,1)}), bf16[32,32,256]{2,1,0:T(8,128)(2,1)S(1)}, u32[]{:S(2)}, u32[]{:S(2)}) async-start(bf16[32,32,256]{2,1,0:T(8,128)(2,1)} %bitcast.28), calls=%async_computation.1 | async-start | bytes 1048576 | tf_op jit(solution)/shard_map/all_to_all | solution.py:25
  101.4 62.8 %all-gather.9.cloned.1.call-start = ((), (), s32[]{:S(2)}) async-start(), calls=%async_computation.3 | async-start | bytes 2228224 | tf_op jit(solution)/shard_map/all_gather | solution.py:29
  118.0 3.6 %collective-permute-start = (f32[4,48,4,512]{3,1,2,0:T(8,128)S(1)}, f32[4,48,4,512]{3,1,2,0:T(8,128)}, u32[]{:S(2)}, u32[]{:S(2)}) collective-permute-start(f32[4,48,4,512]{3,1,2,0:T(8,128)S(1)} %bitcast.112), channel_id=1, source_target_pairs={{0,1},{1,0},{2,3},{3,2},{4,5},{5,4},{6,7},{7,6},{8,9},{9,8},{10,11... | collective-permute-start | bytes 4718600 | tf_op jit(solution)/shard_map/ppermute | solution.py:49
  123.6 12.1 %collective-permute-start.4 = (f32[24,4,512]{2,0,1:T(8,128)S(1)}, f32[24,4,512]{2,0,1:T(8,128)S(1)}, u32[]{:S(2)}, u32[]{:S(2)}) collective-permute-start(f32[24,4,512]{2,0,1:T(8,128)S(1)} %dynamic-slice_bitcast_fusion.3), channel_id=1, source_target_pairs={{0,6},{2,0},{4,2},{6,4},{1,7},{3,1},{5,3},{7,5},{8,14},{10,8},{12,... | collective-permute-start | bytes 589832 | tf_op jit(solution)/shard_map/ppermute | solution.py:63
  126.9 12.6 %collective-permute-start.1 = (f32[24,4,512]{2,0,1:T(8,128)S(1)}, f32[24,4,512]{2,0,1:T(8,128)S(1)}, u32[]{:S(2)}, u32[]{:S(2)}) collective-permute-start(f32[24,4,512]{2,0,1:T(8,128)S(1)} %dynamic-slice_bitcast_fusion.4), channel_id=1, source_target_pairs={{0,2},{2,4},{4,6},{6,0},{1,3},{3,5},{5,7},{7,1},{8,10},{10,12},{12... | collective-permute-start | bytes 589832 | tf_op jit(solution)/shard_map/ppermute | solution.py:62
  135.8 11.7 %collective-permute-start.5 = (f32[24,4,512]{2,0,1:T(8,128)S(1)}, f32[24,4,512]{2,0,1:T(8,128)S(1)}, u32[]{:S(2)}, u32[]{:S(2)}) collective-permute-start(f32[24,4,512]{2,0,1:T(8,128)S(1)} %bitcast_add_fusion.10), channel_id=1, source_target_pairs={{0,6},{2,0},{4,2},{6,4},{1,7},{3,1},{5,3},{7,5},{8,14},{10,8},{12,... | collective-permute-start | bytes 589832 | tf_op jit(solution)/shard_map/ppermute | solution.py:63
  139.6 12.0 %collective-permute-start.2 = (f32[24,4,512]{2,0,1:T(8,128)S(1)}, f32[24,4,512]{2,0,1:T(8,128)S(1)}, u32[]{:S(2)}, u32[]{:S(2)}) collective-permute-start(f32[24,4,512]{2,0,1:T(8,128)S(1)} %bitcast_add_fusion.13), channel_id=1, source_target_pairs={{0,2},{2,4},{4,6},{6,0},{1,3},{3,5},{5,7},{7,1},{8,10},{10,12},{12... | collective-permute-start | bytes 589832 | tf_op jit(solution)/shard_map/ppermute | solution.py:62
  147.5 8.7 %collective-permute-start.6 = (f32[24,4,512]{2,0,1:T(8,128)S(1)}, f32[24,4,512]{2,0,1:T(8,128)S(1)}, u32[]{:S(2)}, u32[]{:S(2)}) collective-permute-start(f32[24,4,512]{2,0,1:T(8,128)S(1)} %bitcast_add_fusion.9), channel_id=1, source_target_pairs={{0,6},{2,0},{4,2},{6,4},{1,7},{3,1},{5,3},{7,5},{8,14},{10,8},{12,... | collective-permute-start | bytes 589832 | tf_op jit(solution)/shard_map/ppermute | solution.py:63
  151.6 9.7 %collective-permute-start.3 = (f32[24,4,512]{2,0,1:T(8,128)S(1)}, f32[24,4,512]{2,0,1:T(8,128)S(1)}, u32[]{:S(2)}, u32[]{:S(2)}) collective-permute-start(f32[24,4,512]{2,0,1:T(8,128)S(1)} %bitcast_add_fusion.12), channel_id=1, source_target_pairs={{0,2},{2,4},{4,6},{6,0},{1,3},{3,5},{5,7},{7,1},{8,10},{10,12},{12... | collective-permute-start | bytes 589832 | tf_op jit(solution)/shard_map/ppermute | solution.py:62
  164.2 2.8 %slice-start.2 = ((s8[6291456]{0:T(1024)(128)(4,1)}), s8[4194304]{0:T(1024)(128)(4,1)S(1)}, s32[]{:S(2)}) async-start(s8[6291456]{0:T(1024)(128)(4,1)} %bitcast.118), calls=%async_computation.6 | async-start | bytes 8388608
  170.5 3.5 %collective-permute-start.7 = (f32[4,48,4,512]{3,1,2,0:T(8,128)S(1)}, f32[4,48,4,512]{3,1,2,0:T(8,128)S(1)}, u32[]{:S(2)}, u32[]{:S(2)}) collective-permute-start(f32[4,48,4,512]{3,1,2,0:T(8,128)S(1)} %bitcast.113), channel_id=1, source_target_pairs={{0,1},{1,0},{2,3},{3,2},{4,5},{5,4},{6,7},{7,6},{8,9},{9,8},{10,11... | collective-permute-start | bytes 4718600 | tf_op jit(solution)/shard_map/ppermute | solution.py:49
  174.6 11.3 %collective-permute-start.8 = (f32[24,4,512]{2,0,1:T(8,128)S(1)}, f32[24,4,512]{2,0,1:T(8,128)S(1)}, u32[]{:S(2)}, u32[]{:S(2)}) collective-permute-start(f32[24,4,512]{2,0,1:T(8,128)S(1)} %dynamic-slice_bitcast_fusion.2), channel_id=1, source_target_pairs={{0,2},{2,4},{4,6},{6,0},{1,3},{3,5},{5,7},{7,1},{8,10},{10,12},{12... | collective-permute-start | bytes 589832 | tf_op jit(solution)/shard_map/ppermute | solution.py:62
  177.2 13.0 %collective-permute-start.11 = (f32[24,4,512]{2,0,1:T(8,128)S(1)}, f32[24,4,512]{2,0,1:T(8,128)S(1)}, u32[]{:S(2)}, u32[]{:S(2)}) collective-permute-start(f32[24,4,512]{2,0,1:T(8,128)S(1)} %dynamic-slice_bitcast_fusion.1), channel_id=1, source_target_pairs={{0,6},{2,0},{4,2},{6,4},{1,7},{3,1},{5,3},{7,5},{8,14},{10,8},{12,... | collective-permute-start | bytes 589832 | tf_op jit(solution)/shard_map/ppermute | solution.py:63
  185.9 12.4 %collective-permute-start.9 = (f32[24,4,512]{2,0,1:T(8,128)S(1)}, f32[24,4,512]{2,0,1:T(8,128)S(1)}, u32[]{:S(2)}, u32[]{:S(2)}) collective-permute-start(f32[24,4,512]{2,0,1:T(8,128)S(1)} %bitcast_add_fusion.7), channel_id=1, source_target_pairs={{0,2},{2,4},{4,6},{6,0},{1,3},{3,5},{5,7},{7,1},{8,10},{10,12},{12... | collective-permute-start | bytes 589832 | tf_op jit(solution)/shard_map/ppermute | solution.py:62
  190.2 12.5 %collective-permute-start.12 = (f32[24,4,512]{2,0,1:T(8,128)S(1)}, f32[24,4,512]{2,0,1:T(8,128)S(1)}, u32[]{:S(2)}, u32[]{:S(2)}) collective-permute-start(f32[24,4,512]{2,0,1:T(8,128)S(1)} %bitcast_add_fusion.4), channel_id=1, source_target_pairs={{0,6},{2,0},{4,2},{6,4},{1,7},{3,1},{5,3},{7,5},{8,14},{10,8},{12,... | collective-permute-start | bytes 589832 | tf_op jit(solution)/shard_map/ppermute | solution.py:63
  198.2 18.2 %copy-start.1 = (s32[4,8]{1,0:T(4,128)S(1)}, s32[4,8]{1,0:T(4,128)}, u32[]{:S(2)}) copy-start(s32[4,8]{1,0:T(4,128)} %param.9) | copy-start | bytes 388
  198.3 10.6 %collective-permute-start.10 = (f32[24,4,512]{2,0,1:T(8,128)S(1)}, f32[24,4,512]{2,0,1:T(8,128)S(1)}, u32[]{:S(2)}, u32[]{:S(2)}) collective-permute-start(f32[24,4,512]{2,0,1:T(8,128)S(1)} %bitcast_add_fusion.6), channel_id=1, source_target_pairs={{0,2},{2,4},{4,6},{6,0},{1,3},{3,5},{5,7},{7,1},{8,10},{10,12},{12... | collective-permute-start | bytes 589832 | tf_op jit(solution)/shard_map/ppermute | solution.py:62
  202.7 12.3 %collective-permute-start.13 = (f32[24,4,512]{2,0,1:T(8,128)S(1)}, f32[24,4,512]{2,0,1:T(8,128)S(1)}, u32[]{:S(2)}, u32[]{:S(2)}) collective-permute-start(f32[24,4,512]{2,0,1:T(8,128)S(1)} %bitcast_add_fusion.3), channel_id=1, source_target_pairs={{0,6},{2,0},{4,2},{6,4},{1,7},{3,1},{5,3},{7,5},{8,14},{10,8},{12,... | collective-permute-start | bytes 589832 | tf_op jit(solution)/shard_map/ppermute | solution.py:63
  (2 other events, 2.4 us)
Sparse Core Ops, SparseCore 0:
  36.7 49.7 all-gather.6
  115.8 48.3 all-gather.8

commit v8 on v5

--- a/solution.py
+++ b/solution.py
@@ -22,9 +22,9 @@
     got = lax.all_to_all(pieces, SHOT, 0, 0, tiled=True)
     chosen = jnp.take(got, column, axis=0)
     full = lax.all_gather(chosen, "zl", axis=0, tiled=False)
-    full = lax.all_gather(full, "x", axis=0, tiled=False)
-    full = lax.all_gather(full, "y", axis=0, tiled=False)
-    n_y, n_x, n_zl = full.shape[:3]
+    n_y, n_x, n_zl = lax.psum(1, "y"), lax.psum(1, "x"), full.shape[0]
+    full = lax.all_gather(full, ("y", "x"), axis=0, tiled=False)
+    full = full.reshape(n_y, n_x, *full.shape[1:])
     full = full.reshape(n_y, parts, n_x // parts, n_zl, STEPS, kb // split, recv)
 
     def part_of(p):
@@ -74,7 +74,10 @@
         live, weights, (((0, 3), (0, 2)), ((1,), (1,))), preferred_element_type=jnp.float32
     )
     out = jnp.transpose(out, (1, 0, 2))
-    out = reduce_rows(out)
+    half = out.shape[1] // 2
+    by_scatter = lax.psum_scatter(out[:, :half], SP, scatter_dimension=0, tiled=True)
+    by_ring = reduce_rows(out[:, half:])
+    out = jnp.concatenate([by_scatter, by_ring], axis=1)
     rows = out.shape[0]
     out = out.reshape(rows, freq, 2, recv).astype(jnp.bfloat16)
     return jnp.transpose(out, (0, 2, 1, 3))

time: 232 us -> 200 us (0.86)
  waiting for transfers between devices: 147 us -> 123 us
  other arithmetic: 16.4 us -> 7.71 us
    all_gather x2 -> x1, waiting for transfers between devices: 79.8 us -> 56.6 us  [gather_receivers(): full = lax.all_gather(full, ('y', 'x'), axis=0, tiled=False)]
    reduce_scatter x0 -> x1, waiting for transfers between devices: none -> 8.66 us  [body(): lax.psum_scatter(out[:, :half], SP, scatter_dimension=0, tiled=True)]
    ppermute x3, waiting for transfers between devices: 37.1 us -> 28.6 us  [reduce_rows(): got_lo = lax.ppermute(acc_lo, 'zh', fwd)]
    ppermute x3, starting transfers between devices: 11.7 us -> 16.1 us  [reduce_rows(): got_lo = lax.ppermute(acc_lo, 'zh', fwd)]
    add x2, other arithmetic: 3.59 us -> 0.06 us  [reduce_rows(): acc_hi = got_hi + chunk(hi, zh + step + 2)]
    unnamed x5 -> x7, local copies, waits for them, and re-layouts: 3.48 us -> 0.13 us
    add x2, other arithmetic: 2.85 us -> 0.06 us  [reduce_rows(): acc_lo = got_lo + chunk(lo, zh + 2 * n_zh - step - 2)]
    slice x0 -> x1, local copies, waits for them, and re-layouts: none -> 2.66 us  [body(): out[:, :half]]
  transfers between devices with their start and end apart: 10 -> 10, of which waited for: 10 -> 9; matrix products, arithmetic and copies ran while one was open for 3% -> 2% of each run, Pallas kernels for 0% -> 0%
where the time goes in v8:
time: 200 us; the launch traced here: 199 us
  waiting for transfers between devices  123 us (62%)
  starting transfers between devices  28.3 us (14%)
  between operations  15.5 us (8%)
  local copies, waits for them, and re-layouts  11.7 us (6%)
  other arithmetic  7.71 us (4%)
  matrix products  7.42 us (4%)
  blocking collectives  5.74 us (3%)
    all_gather x1, waiting for transfers between devices, gather_receivers(): full = lax.all_gather(full, ('y', 'x'), axis=0, tiled=False)  56.6 us
    ppermute x3, waiting for transfers between devices, reduce_rows(): got_lo = lax.ppermute(acc_lo, 'zh', fwd)  28.6 us
    ppermute x3, starting transfers between devices, reduce_rows(): got_lo = lax.ppermute(acc_lo, 'zh', fwd)  16.1 us
    all_to_all x1, waiting for transfers between devices, gather_receivers(): got = lax.all_to_all(pieces, SHOT, 0, 0, tiled=True)  15.3 us
    ppermute x3, waiting for transfers between devices, reduce_rows(): got_hi = lax.ppermute(acc_hi, 'zh', bwd)  9.79 us
    all_to_all x1, starting transfers between devices, gather_receivers(): got = lax.all_to_all(pieces, SHOT, 0, 0, tiled=True)  8.96 us
    reduce_scatter x1, waiting for transfers between devices, body(): lax.psum_scatter(out[:, :half], SP, scatter_dimension=0, tiled=True)  8.66 us
    dot_general x1, matrix products, body(): lax.dot_general(live, weights, (((0, 3), (0, 2)), ((1,), (1,))), preferre...  7.42 us
  transfers between devices with their start and end apart: 10, of which 9 were waited for; matrix products, arithmetic and copies ran while one was open for 2% of the time, Pallas kernels for 0%

profile of v8, /device:TPU:6, one launch (start us, length us, event | category | flops | bytes accessed | tf_op | source)
XLA Modules:
  0.0 198.9 jit_solution(13144097624303251497)
XLA Ops:
  10.1 2.3 %constant_dynamic-slice_fusion.2 = bf16[1,2,8,128,256]{4,3,2,1,0:T(8,128)(2,1)} fusion(bf16[4,2,8,128,256]{4,3,2,1,0:T(8,128)(2,1)} %param.6, s32[]{:T(128)S(6)} %select_n.95), kind=kLoop, calls=%fused_computation.32 | loop fusion | bytes 2097156 | tf_op jit(solution)/shard_map/jit(dynamic_index_in_dim)/dynamic_slice | solution.py:18
  12.4 9.0 %all-to-all-start = ((bf16[32,64,256]{2,1,0:T(8,128)(2,1)}), bf16[32,64,256]{2,1,0:T(8,128)(2,1)S(1)}, u32[]{:S(2)}, u32[]{:S(2)}) async-start(bf16[32,64,256]{2,1,0:T(8,128)(2,1)} %bitcast), calls=%async_computation | async-start | bytes 2097152 | tf_op jit(solution)/shard_map/all_to_all | solution.py:22
  21.6 15.3 %all-to-all-done = bf16[32,64,256]{2,1,0:T(8,128)(2,1)S(1)} async-done(((bf16[32,64,256]{2,1,0:T(8,128)(2,1)}), bf16[32,64,256]{2,1,0:T(8,128)(2,1)S(1)}, u32[]{:S(2)}, u32[]{:S(2)}) %all-to-all-start) | async-done | bytes 1048608 | tf_op jit(solution)/shard_map/all_to_all | solution.py:22
  37.6 5.7 %all_gather.10 = bf16[2,4,64,256]{3,2,1,0:T(8,128)(2,1)} all-gather(bf16[1,4,64,256]{3,2,1,0:T(8,128)(2,1)S(1)} %bitcast_select_fusion), channel_id=1, replica_groups=mesh['x'=4,'y'=4,'zl'=2,'zh'=4,'c'=2] {'zl'}, dimensions={0}, use_global_device_ids=true | all-gather | bytes 393216 | tf_op jit(solution)/shard_map/all_gather | solution.py:24
  43.5 56.6 %all-gather.3.cloned.1.call-done = bf16[32,4,64,256]{3,2,1,0:T(8,128)(2,1)} async-done(((bf16[2,4,64,256]{3,2,1,0:T(8,128)(2,1)}), bf16[32,4,64,256]{3,2,1,0:T(8,128)(2,1)}) %all-gather.3.cloned.1.call-update) | async-done | bytes 4194320 | tf_op jit(solution)/shard_map/all_gather | solution.py:26
  100.1 2.6 %slice_bitcast_fusion = (bf16[2,4,4,2,64,256]{5,4,2,3,0,1:T(8,128)(2,1)S(1)}, bf16[2,4,4,2,64,256]{5,4,2,3,0,1:T(8,128)(2,1)S(1)}) fusion(bf16[4,2,2,2,4,64,256]{6,5,4,3,2,1,0:T(8,128)(2,1)} %bitcast.59), kind=kLoop, calls=%fused_computation.10 | loop fusion | bytes 8388608 | tf_op jit(solution)/shard_map/transpose | solution.py:31
  103.7 2.3 %maximum_bitcast_fusion = (bf16[1,8,512,512]{3,2,1,0:T(8,128)(2,1)S(1)}, bf16[1,8,512,512]{3,2,1,0:T(8,128)(2,1)}) fusion(bf16[8,512,256]{2,1,0:T(8,128)(2,1)S(1)} %bitcast.56, bf16[8,512,256]{2,1,0:T(8,128)(2,1)S(1)} %bitcast.58, bf16[8,512,256]{2,1,0:T(8,128)(2,1)S(1)} %neg.3), kind=kLoop, calls=%fused_computation.6 | loop fusion | flops 16777216 | bytes 14680064 | tf_op jit(solution)/shard_map/stack | solution.py:70
  106.0 7.4 %fusion.6 = f32[384,8,512]{2,0,1:T(8,128)S(1)} fusion(bf16[1,8,512,512]{3,2,1,0:T(8,128)(2,1)} %get-tuple-element.16, bf16[1,8,512,512]{3,2,1,0:T(8,128)(2,1)S(1)} %get-tuple-element.15, bf16[2,8,384,512]{3,2,1,0:T(8,128)(2,1)} %param.4, bf16[384,512]{1,0:T(8,128)(2,1)S(1)} %convert_element_type.7), kind=kOutput, calls=%fused_computation.9 | convolution fusion | flops 3228565504 | bytes 21364736 | tf_op jit(solution)/shard_map/dot_general | solution.py:73
  113.4 2.7 %fusion.16 = (f32[384,4,512]{2,0,1:T(8,128)}, f32[384,4,512]{2,0,1:T(8,128)S(1)}) fusion(f32[384,8,512]{2,0,1:T(8,128)S(1)} %fusion.6), kind=kLoop, calls=%fused_computation.39 | loop fusion | bytes 12582912 | tf_op jit(solution)/shard_map/slice | solution.py:78
  116.1 1.5 constant_dynamic-slice_fusion.1
  117.8 3.5 %collective-permute-done = f32[4,48,4,512]{3,1,2,0:T(8,128)} collective-permute-done((f32[4,48,4,512]{3,1,2,0:T(8,128)S(1)}, f32[4,48,4,512]{3,1,2,0:T(8,128)}, u32[]{:S(2)}, u32[]{:S(2)}) %collective-permute-start) | collective-permute-done | bytes 1572896 | tf_op jit(solution)/shard_map/ppermute | solution.py:46
  121.4 1.8 fusion.11
  123.3 2.6 %collective-permute-start.1 = (f32[24,4,512]{2,0,1:T(8,128)S(1)}, f32[24,4,512]{2,0,1:T(8,128)S(1)}, u32[]{:S(2)}, u32[]{:S(2)}) collective-permute-start(f32[24,4,512]{2,0,1:T(8,128)S(1)} %dynamic-slice_bitcast_fusion.1), channel_id=1, source_target_pairs={{0,2},{2,4},{4,6},{6,0},{1,3},{3,5},{5,7},{7,1},{8,10},{10,12},{12... | collective-permute-start | bytes 589832 | tf_op jit(solution)/shard_map/ppermute | solution.py:59
  125.9 1.8 collective-permute-start.4
  127.7 8.8 %collective-permute-done.1 = f32[24,4,512]{2,0,1:T(8,128)S(1)} collective-permute-done((f32[24,4,512]{2,0,1:T(8,128)S(1)}, f32[24,4,512]{2,0,1:T(8,128)S(1)}, u32[]{:S(2)}, u32[]{:S(2)}) %collective-permute-start.1) | collective-permute-done | bytes 196640 | tf_op jit(solution)/shard_map/ppermute | solution.py:59
  136.6 9.1 %collective-permute-start.2 = (f32[24,4,512]{2,0,1:T(8,128)S(1)}, f32[24,4,512]{2,0,1:T(8,128)S(1)}, u32[]{:S(2)}, u32[]{:S(2)}) collective-permute-start(f32[24,4,512]{2,0,1:T(8,128)S(1)} %bitcast_add_fusion.5), channel_id=1, source_target_pairs={{0,2},{2,4},{4,6},{6,0},{1,3},{3,5},{5,7},{7,1},{8,10},{10,12},{12... | collective-permute-start | bytes 589832 | tf_op jit(solution)/shard_map/ppermute | solution.py:59
  145.8 8.8 %collective-permute-done.2 = f32[24,4,512]{2,0,1:T(8,128)S(1)} collective-permute-done((f32[24,4,512]{2,0,1:T(8,128)S(1)}, f32[24,4,512]{2,0,1:T(8,128)S(1)}, u32[]{:S(2)}, u32[]{:S(2)}) %collective-permute-start.2) | collective-permute-done | bytes 196640 | tf_op jit(solution)/shard_map/ppermute | solution.py:59
  154.7 4.4 %collective-permute-start.3 = (f32[24,4,512]{2,0,1:T(8,128)S(1)}, f32[24,4,512]{2,0,1:T(8,128)S(1)}, u32[]{:S(2)}, u32[]{:S(2)}) collective-permute-start(f32[24,4,512]{2,0,1:T(8,128)S(1)} %bitcast_add_fusion.4), channel_id=1, source_target_pairs={{0,2},{2,4},{4,6},{6,0},{1,3},{3,5},{5,7},{7,1},{8,10},{10,12},{12... | collective-permute-start | bytes 589832 | tf_op jit(solution)/shard_map/ppermute | solution.py:59
  159.1 4.0 %collective-permute-done.5 = f32[24,4,512]{2,0,1:T(8,128)S(1)} collective-permute-done((f32[24,4,512]{2,0,1:T(8,128)S(1)}, f32[24,4,512]{2,0,1:T(8,128)S(1)}, u32[]{:S(2)}, u32[]{:S(2)}) %collective-permute-start.5) | collective-permute-done | bytes 196640 | tf_op jit(solution)/shard_map/ppermute | solution.py:60
  163.1 1.2 collective-permute-start.6
  164.2 11.0 %collective-permute-done.3 = f32[24,4,512]{2,0,1:T(8,128)S(1)} collective-permute-done((f32[24,4,512]{2,0,1:T(8,128)S(1)}, f32[24,4,512]{2,0,1:T(8,128)S(1)}, u32[]{:S(2)}, u32[]{:S(2)}) %collective-permute-start.3) | collective-permute-done | bytes 196640 | tf_op jit(solution)/shard_map/ppermute | solution.py:59
  175.3 5.8 %collective-permute-done.6 = f32[24,4,512]{2,0,1:T(8,128)S(1)} collective-permute-done((f32[24,4,512]{2,0,1:T(8,128)S(1)}, f32[24,4,512]{2,0,1:T(8,128)S(1)}, u32[]{:S(2)}, u32[]{:S(2)}) %collective-permute-start.6) | collective-permute-done | bytes 196640 | tf_op jit(solution)/shard_map/ppermute | solution.py:60
  181.1 8.7 %reduce-scatter.2.cloned.1.call-done = f32[48,4,512]{2,0,1:T(8,128)} async-done(((f32[384,4,512]{2,0,1:T(8,128)}), f32[48,4,512]{2,0,1:T(8,128)}) %reduce-scatter.2.cloned.1.call-update) | async-done | bytes 393232 | tf_op jit(solution)/shard_map/reduce_scatter | solution.py:78
  190.9 1.2 copy.28
  (36 shorter events, 5.4 us)
Async XLA Ops:
  6.5 14.9 %copy-start.2 = (s32[4,8]{1,0:T(4,128)S(1)}, s32[4,8]{1,0:T(4,128)}, u32[]{:S(2)}) copy-start(s32[4,8]{1,0:T(4,128)} %param.7) | copy-start | bytes 388
  6.5 36.9 %copy-start.1 = (s32[384,512]{1,0:T(8,128)S(1)}, s32[384,512]{1,0:T(8,128)}, u32[]{:S(2)}) copy-start(s32[384,512]{1,0:T(8,128)} %param.5) | copy-start | bytes 2359300
  12.4 24.6 %all-to-all-start = ((bf16[32,64,256]{2,1,0:T(8,128)(2,1)}), bf16[32,64,256]{2,1,0:T(8,128)(2,1)S(1)}, u32[]{:S(2)}, u32[]{:S(2)}) async-start(bf16[32,64,256]{2,1,0:T(8,128)(2,1)} %bitcast), calls=%async_computation | async-start | bytes 2097152 | tf_op jit(solution)/shard_map/all_to_all | solution.py:22
  21.4 78.8 %all-gather.3.cloned.1.call-start = ((), (), s32[]{:S(2)}) async-start(), calls=%async_computation.3 | async-start | bytes 4456448 | tf_op jit(solution)/shard_map/all_gather | solution.py:26
  43.4 146.4 %reduce-scatter.2.cloned.1.call-start = ((), (), s32[]{:S(2)}) async-start(), calls=%async_computation.2 | async-start | bytes 3538944 | tf_op jit(solution)/shard_map/reduce_scatter | solution.py:78
  117.6 3.8 %copy-start = (f32[4,1,48,4,512]{4,2,1,0,3:T(8,128)S(1)}, f32[4,1,48,4,512]{4,2,1,0,3:T(8,128)}, u32[]{:S(2)}) copy-start(f32[4,1,48,4,512]{4,2,1,0,3:T(8,128)} %get-tuple-element.13) | copy-start | bytes 4718596
  117.7 3.6 %collective-permute-start = (f32[4,48,4,512]{3,1,2,0:T(8,128)S(1)}, f32[4,48,4,512]{3,1,2,0:T(8,128)}, u32[]{:S(2)}, u32[]{:S(2)}) collective-permute-start(f32[4,48,4,512]{3,1,2,0:T(8,128)S(1)} %bitcast.60), channel_id=1, source_target_pairs={{0,1},{1,0},{2,3},{3,2},{4,5},{5,4},{6,7},{7,6},{8,9},{9,8},{10,11... | collective-permute-start | bytes 4718600 | tf_op jit(solution)/shard_map/ppermute | solution.py:46
  123.3 13.2 %collective-permute-start.1 = (f32[24,4,512]{2,0,1:T(8,128)S(1)}, f32[24,4,512]{2,0,1:T(8,128)S(1)}, u32[]{:S(2)}, u32[]{:S(2)}) collective-permute-start(f32[24,4,512]{2,0,1:T(8,128)S(1)} %dynamic-slice_bitcast_fusion.1), channel_id=1, source_target_pairs={{0,2},{2,4},{4,6},{6,0},{1,3},{3,5},{5,7},{7,1},{8,10},{10,12},{12... | collective-permute-start | bytes 589832 | tf_op jit(solution)/shard_map/ppermute | solution.py:59
  125.9 19.8 %collective-permute-start.4 = (f32[24,4,512]{2,0,1:T(8,128)S(1)}, f32[24,4,512]{2,0,1:T(8,128)S(1)}, u32[]{:S(2)}, u32[]{:S(2)}) collective-permute-start(f32[24,4,512]{2,0,1:T(8,128)S(1)} %dynamic-slice_bitcast_fusion), channel_id=1, source_target_pairs={{0,6},{2,0},{4,2},{6,4},{1,7},{3,1},{5,3},{7,5},{8,14},{10,8},{12,... | collective-permute-start | bytes 589832 | tf_op jit(solution)/shard_map/ppermute | solution.py:60
  136.6 18.1 %collective-permute-start.2 = (f32[24,4,512]{2,0,1:T(8,128)S(1)}, f32[24,4,512]{2,0,1:T(8,128)S(1)}, u32[]{:S(2)}, u32[]{:S(2)}) collective-permute-start(f32[24,4,512]{2,0,1:T(8,128)S(1)} %bitcast_add_fusion.5), channel_id=1, source_target_pairs={{0,2},{2,4},{4,6},{6,0},{1,3},{3,5},{5,7},{7,1},{8,10},{10,12},{12... | collective-permute-start | bytes 589832 | tf_op jit(solution)/shard_map/ppermute | solution.py:59
  145.7 17.3 %collective-permute-start.5 = (f32[24,4,512]{2,0,1:T(8,128)S(1)}, f32[24,4,512]{2,0,1:T(8,128)S(1)}, u32[]{:S(2)}, u32[]{:S(2)}) collective-permute-start(f32[24,4,512]{2,0,1:T(8,128)S(1)} %bitcast_add_fusion.2), channel_id=1, source_target_pairs={{0,6},{2,0},{4,2},{6,4},{1,7},{3,1},{5,3},{7,5},{8,14},{10,8},{12,... | collective-permute-start | bytes 589832 | tf_op jit(solution)/shard_map/ppermute | solution.py:60
  154.7 20.5 %collective-permute-start.3 = (f32[24,4,512]{2,0,1:T(8,128)S(1)}, f32[24,4,512]{2,0,1:T(8,128)S(1)}, u32[]{:S(2)}, u32[]{:S(2)}) collective-permute-start(f32[24,4,512]{2,0,1:T(8,128)S(1)} %bitcast_add_fusion.4), channel_id=1, source_target_pairs={{0,2},{2,4},{4,6},{6,0},{1,3},{3,5},{5,7},{7,1},{8,10},{10,12},{12... | collective-permute-start | bytes 589832 | tf_op jit(solution)/shard_map/ppermute | solution.py:59
  163.1 18.0 %collective-permute-start.6 = (f32[24,4,512]{2,0,1:T(8,128)S(1)}, f32[24,4,512]{2,0,1:T(8,128)S(1)}, u32[]{:S(2)}, u32[]{:S(2)}) collective-permute-start(f32[24,4,512]{2,0,1:T(8,128)S(1)} %bitcast_add_fusion.1), channel_id=1, source_target_pairs={{0,6},{2,0},{4,2},{6,4},{1,7},{3,1},{5,3},{7,5},{8,14},{10,8},{12,... | collective-permute-start | bytes 589832 | tf_op jit(solution)/shard_map/ppermute | solution.py:60
Sparse Core Ops, SparseCore 0:
  43.5 56.5 all-gather.2
  116.2 73.4 reduce-scatter.1

commit v9 on v8

--- a/solution.py
+++ b/solution.py
@@ -6,6 +6,22 @@
 STEPS = 4
 SHOT = ("x", "y", "zl")
 SP = ("zh", "c")
+
+
+def ring_gather(piece, axis):
+    n = lax.psum(1, axis)
+    me = lax.axis_index(axis)
+    fwd = [(i, (i + 1) % n) for i in range(n)]
+    bwd = [(i, (i - 1) % n) for i in range(n)]
+    from_left = lax.ppermute(piece, axis, fwd)
+    from_right = lax.ppermute(piece, axis, bwd)
+    half = piece.shape[0] // 2
+    far = jnp.concatenate(
+        [lax.ppermute(from_left[:half], axis, fwd), lax.ppermute(from_right[half:], axis, bwd)], axis=0
+    )
+    rel = jnp.stack([piece, from_right, far, from_left], axis=0)
+    doubled = jnp.concatenate([rel, rel], axis=0)
+    return lax.dynamic_slice_in_dim(doubled, (n - me) % n, n, axis=0)
 
 
 def gather_receivers(spectra, plan):
@@ -23,8 +39,9 @@
     chosen = jnp.take(got, column, axis=0)
     full = lax.all_gather(chosen, "zl", axis=0, tiled=False)
     n_y, n_x, n_zl = lax.psum(1, "y"), lax.psum(1, "x"), full.shape[0]
-    full = lax.all_gather(full, ("y", "x"), axis=0, tiled=False)
-    full = full.reshape(n_y, n_x, *full.shape[1:])
+    first = ring_gather(ring_gather(full[:, : STEPS // 2], "x"), "y")
+    second = ring_gather(ring_gather(full[:, STEPS // 2 :], "y"), "x")
+    full = jnp.concatenate([first, jnp.swapaxes(second, 0, 1)], axis=3)
     full = full.reshape(n_y, parts, n_x // parts, n_zl, STEPS, kb // split, recv)
 
     def part_of(p):

time: 200 us -> 183 us (0.915)
  waiting for transfers between devices: 123 us -> 93.9 us
  starting transfers between devices: 28.3 us -> 43.3 us
    all_gather x1 -> x0, waiting for transfers between devices: 56.6 us -> none  [gather_receivers(): full = lax.all_gather(full, ('y', 'x'), axis=0, tiled=False)]
    ppermute x0 -> x16, waiting for transfers between devices: none -> 23.2 us  [the longest x4 13.3 us: ring_gather(): from_left = lax.ppermute(piece, axis, fwd)]
    ppermute x0 -> x16, starting transfers between devices: none -> 21 us  [the longest x4 9.67 us: ring_gather(): lax.ppermute(from_right[half:], axis, bwd)]
    ppermute x3, starting transfers between devices: 16.1 us -> 7.54 us  [reduce_rows(): got_lo = lax.ppermute(acc_lo, 'zh', fwd)]
    reduce_scatter x1, waiting for transfers between devices: 8.66 us -> 12 us  [body(): lax.psum_scatter(out[:, :half], SP, scatter_dimension=0, tiled=True)]
    transpose x3 -> x1, local copies, waits for them, and re-layouts: 3.08 us -> 0.24 us  [gather_receivers(): full = jnp.concatenate([first, jnp.swapaxes(second, 0, 1)], axis=3)]
    ppermute x3, starting transfers between devices: 3 us -> 5.72 us  [reduce_rows(): got_hi = lax.ppermute(acc_hi, 'zh', bwd)]
  transfers between devices with their start and end apart: 10 -> 25, of which waited for: 9 -> 15; matrix products, arithmetic and copies ran while one was open for 2% -> 2% of each run, Pallas kernels for 0% -> 0%
where the time goes in v9:
time: 183 us; the launch traced here: 181 us
  waiting for transfers between devices  93.9 us (51%)
  starting transfers between devices  43.3 us (24%)
  between operations  15.6 us (9%)
  local copies, waits for them, and re-layouts  9.97 us (5%)
  other arithmetic  6.63 us (4%)
  matrix products  5.99 us (3%)
  blocking collectives  5.64 us (3%)
    ppermute x3, waiting for transfers between devices, reduce_rows(): got_lo = lax.ppermute(acc_lo, 'zh', fwd)  30.3 us
    all_to_all x1, waiting for transfers between devices, gather_receivers(): got = lax.all_to_all(pieces, SHOT, 0, 0, tiled=True)  15.3 us
    ppermute x4, waiting for transfers between devices, ring_gather(): from_left = lax.ppermute(piece, axis, fwd)  13.3 us
    reduce_scatter x1, waiting for transfers between devices, body(): lax.psum_scatter(out[:, :half], SP, scatter_dimension=0, tiled=True)  12 us
    ppermute x4, starting transfers between devices, ring_gather(): lax.ppermute(from_right[half:], axis, bwd)  9.67 us
    ppermute x3, waiting for transfers between devices, reduce_rows(): got_hi = lax.ppermute(acc_hi, 'zh', bwd)  9.46 us
    all_to_all x1, starting transfers between devices, gather_receivers(): got = lax.all_to_all(pieces, SHOT, 0, 0, tiled=True)  8.96 us
    ppermute x3, starting transfers between devices, reduce_rows(): got_lo = lax.ppermute(acc_lo, 'zh', fwd)  7.54 us
  transfers between devices with their start and end apart: 25, of which 15 were waited for; matrix products, arithmetic and copies ran while one was open for 2% of the time, Pallas kernels for 0%

profile of v9, /device:TPU:6, one launch (start us, length us, event | category | flops | bytes accessed | tf_op | source)
XLA Modules:
  0.0 181.0 jit_solution(9858352470680737947)
XLA Ops:
  9.8 2.3 %constant_dynamic-slice_fusion.5 = bf16[1,2,8,128,256]{4,3,2,1,0:T(8,128)(2,1)} fusion(bf16[4,2,8,128,256]{4,3,2,1,0:T(8,128)(2,1)} %param.6, s32[]{:T(128)S(6)} %select_n.115), kind=kLoop, calls=%fused_computation.70 | loop fusion | bytes 2097156 | tf_op jit(solution)/shard_map/jit(dynamic_index_in_dim)/dynamic_slice | solution.py:34
  12.2 9.0 %all-to-all-start = ((bf16[32,64,256]{2,1,0:T(8,128)(2,1)}), bf16[32,64,256]{2,1,0:T(8,128)(2,1)S(1)}, u32[]{:S(2)}, u32[]{:S(2)}) async-start(bf16[32,64,256]{2,1,0:T(8,128)(2,1)} %bitcast), calls=%async_computation | async-start | bytes 2097152 | tf_op jit(solution)/shard_map/all_to_all | solution.py:38
  21.4 15.3 %all-to-all-done = bf16[32,64,256]{2,1,0:T(8,128)(2,1)S(1)} async-done(((bf16[32,64,256]{2,1,0:T(8,128)(2,1)}), bf16[32,64,256]{2,1,0:T(8,128)(2,1)S(1)}, u32[]{:S(2)}, u32[]{:S(2)}) %all-to-all-start) | async-done | bytes 1048608 | tf_op jit(solution)/shard_map/all_to_all | solution.py:38
  37.4 5.6 %all_gather.4 = bf16[2,4,64,256]{3,2,0,1:T(8,128)(2,1)S(1)} all-gather(bf16[1,4,64,256]{3,2,0,1:T(8,128)(2,1)S(1)} %bitcast_select_fusion), channel_id=1, replica_groups=mesh['x'=4,'y'=4,'zl'=2,'zh'=4,'c'=2] {'zl'}, dimensions={0}, use_global_device_ids=true | all-gather | bytes 393216 | tf_op jit(solution)/shard_map/all_gather | solution.py:40
  45.7 2.6 %collective-permute-start.1 = (bf16[2,2,64,256]{3,2,0,1:T(8,128)(2,1)S(1)}, bf16[2,2,64,256]{3,2,0,1:T(8,128)(2,1)S(1)}, u32[]{:S(2)}, u32[]{:S(2)}) collective-permute-start(bf16[2,2,64,256]{3,2,0,1:T(8,128)(2,1)S(1)} %get-tuple-element.25), channel_id=1, source_target_pairs={{0,64},{64,128},{128,192},{192,0},{1,65},{65,129},{129,193},{193,1... | collective-permute-start | bytes 393224 | tf_op jit(solution)/shard_map/ppermute | solution.py:16
  48.4 2.4 %collective-permute-done.9 = bf16[2,2,64,256]{3,2,0,1:T(8,128)(2,1)S(1)} collective-permute-done((bf16[2,2,64,256]{3,2,0,1:T(8,128)(2,1)S(1)}, bf16[2,2,64,256]{3,2,0,1:T(8,128)(2,1)S(1)}, u32[]{:S(2)}, u32[]{:S(2)}) %collective-permute-start.9) | collective-permute-done | bytes 131104 | tf_op jit(solution)/shard_map/ppermute | solution.py:16
  50.8 3.3 %collective-permute-start.11 = (bf16[1,2,64,256]{3,2,0,1:T(8,128)(2,1)S(1)}, bf16[1,2,64,256]{3,2,0,1:T(8,128)(2,1)S(1)}, u32[]{:S(2)}, u32[]{:S(2)}) collective-permute-start(bf16[1,2,64,256]{3,2,0,1:T(8,128)(2,1)S(1)} %slice.73), channel_id=1, source_target_pairs={{0,48},{16,0},{32,16},{48,32},{1,49},{17,1},{33,17},{49,33},{2,50}... | collective-permute-start | bytes 196616 | tf_op jit(solution)/shard_map/ppermute | solution.py:20
  58.4 2.5 %collective-permute-done.3 = bf16[1,2,64,256]{3,2,0,1:T(8,128)(2,1)S(1)} collective-permute-done((bf16[1,2,64,256]{3,2,0,1:T(8,128)(2,1)S(1)}, bf16[1,2,64,256]{3,2,0,1:T(8,128)(2,1)S(1)}, u32[]{:S(2)}, u32[]{:S(2)}) %collective-permute-start.3) | collective-permute-done | bytes 65568 | tf_op jit(solution)/shard_map/ppermute | solution.py:20
  61.2 2.3 %collective-permute-start.4 = (bf16[4,2,2,64,256]{4,3,1,2,0:T(8,128)(2,1)S(1)}, bf16[4,2,2,64,256]{4,3,1,2,0:T(8,128)(2,1)S(1)}, u32[]{:S(2)}, u32[]{:S(2)}) collective-permute-start(bf16[4,2,2,64,256]{4,3,1,2,0:T(8,128)(2,1)S(1)} %get-tuple-element.10), channel_id=1, source_target_pairs={{0,48},{16,0},{32,16},{48,32},{1,49},{17,1},{33,17},{49,33},{2,50}... | collective-permute-start | bytes 1572872 | tf_op jit(solution)/shard_map/ppermute | solution.py:17
  65.8 10.9 %collective-permute-done.5 = bf16[4,2,2,64,256]{4,3,1,2,0:T(8,128)(2,1)S(1)} collective-permute-done((bf16[4,2,2,64,256]{4,3,1,2,0:T(8,128)(2,1)S(1)}, bf16[4,2,2,64,256]{4,3,1,2,0:T(8,128)(2,1)S(1)}, u32[]{:S(2)}, u32[]{:S(2)}) %collective-permute-start.5) | collective-permute-done | bytes 524320 | tf_op jit(solution)/shard_map/ppermute | solution.py:16
  76.9 3.5 %collective-permute-start.7 = (bf16[2,2,2,64,256]{4,3,1,2,0:T(8,128)(2,1)S(1)}, bf16[2,2,2,64,256]{4,3,1,2,0:T(8,128)(2,1)S(1)}, u32[]{:S(2)}, u32[]{:S(2)}) collective-permute-start(bf16[2,2,2,64,256]{4,3,1,2,0:T(8,128)(2,1)S(1)} %slice.70), channel_id=1, source_target_pairs={{0,48},{16,0},{32,16},{48,32},{1,49},{17,1},{33,17},{49,33},{2,50}... | collective-permute-start | bytes 786440 | tf_op jit(solution)/shard_map/ppermute | solution.py:20
  84.5 2.3 %collective-permute-done.14 = bf16[2,2,2,64,256]{4,3,1,2,0:T(8,128)(2,1)S(1)} collective-permute-done((bf16[2,2,2,64,256]{4,3,1,2,0:T(8,128)(2,1)S(1)}, bf16[2,2,2,64,256]{4,3,1,2,0:T(8,128)(2,1)S(1)}, u32[]{:S(2)}, u32[]{:S(2)}) %collective-permute-start.14) | collective-permute-done | bytes 262176 | tf_op jit(solution)/shard_map/ppermute | solution.py:20
  90.9 6.0 %fusion.4 = f32[384,8,512]{2,0,1:T(8,128)S(1)} fusion(bf16[2,8,384,512]{3,2,1,0:T(8,128)(2,1)} %param.4, bf16[384,512]{1,0:T(8,128)(2,1)S(1)} %convert_element_type.7, bf16[1,8,512,512]{3,2,0,1:T(8,128)(2,1)S(1)} %get-tuple-element.20, bf16[1,8,512,512]{3,2,0,1:T(8,128)(2,1)S(1)} %get-tuple-element.19), kind=kOutput, calls=%fused_computation.9 | convolution fusion | flops 3228565504 | bytes 21364736 | tf_op jit(solution)/shard_map/dot_general | solution.py:90
  96.9 2.4 %fusion.21 = (f32[384,4,512]{2,0,1:T(8,128)}, f32[384,4,512]{2,0,1:T(8,128)S(1)}) fusion(f32[384,8,512]{2,0,1:T(8,128)S(1)} %fusion.4), kind=kLoop, calls=%fused_computation.76 | loop fusion | bytes 12582912 | tf_op jit(solution)/shard_map/slice | solution.py:95
  101.1 3.5 %collective-permute-done.16 = f32[4,48,4,512]{3,1,2,0:T(8,128)} collective-permute-done((f32[4,48,4,512]{3,1,2,0:T(8,128)S(1)}, f32[4,48,4,512]{3,1,2,0:T(8,128)}, u32[]{:S(2)}, u32[]{:S(2)}) %collective-permute-start.16) | collective-permute-done | bytes 1572896 | tf_op jit(solution)/shard_map/ppermute | solution.py:63
  106.6 3.3 %collective-permute-start.17 = (f32[24,4,512]{2,0,1:T(8,128)S(1)}, f32[24,4,512]{2,0,1:T(8,128)S(1)}, u32[]{:S(2)}, u32[]{:S(2)}) collective-permute-start(f32[24,4,512]{2,0,1:T(8,128)S(1)} %dynamic-slice_bitcast_fusion.2), channel_id=1, source_target_pairs={{0,2},{2,4},{4,6},{6,0},{1,3},{3,5},{5,7},{7,1},{8,10},{10,12},{12... | collective-permute-start | bytes 589832 | tf_op jit(solution)/shard_map/ppermute | solution.py:76
  109.9 2.3 %collective-permute-start.20 = (f32[24,4,512]{2,0,1:T(8,128)S(1)}, f32[24,4,512]{2,0,1:T(8,128)S(1)}, u32[]{:S(2)}, u32[]{:S(2)}) collective-permute-start(f32[24,4,512]{2,0,1:T(8,128)S(1)} %dynamic-slice_bitcast_fusion.1), channel_id=1, source_target_pairs={{0,6},{2,0},{4,2},{6,4},{1,7},{3,1},{5,3},{7,5},{8,14},{10,8},{12,... | collective-permute-start | bytes 589832 | tf_op jit(solution)/shard_map/ppermute | solution.py:77
  112.2 9.6 %collective-permute-done.17 = f32[24,4,512]{2,0,1:T(8,128)S(1)} collective-permute-done((f32[24,4,512]{2,0,1:T(8,128)S(1)}, f32[24,4,512]{2,0,1:T(8,128)S(1)}, u32[]{:S(2)}, u32[]{:S(2)}) %collective-permute-start.17) | collective-permute-done | bytes 196640 | tf_op jit(solution)/shard_map/ppermute | solution.py:76
  121.9 2.4 %collective-permute-start.18 = (f32[24,4,512]{2,0,1:T(8,128)S(1)}, f32[24,4,512]{2,0,1:T(8,128)S(1)}, u32[]{:S(2)}, u32[]{:S(2)}) collective-permute-start(f32[24,4,512]{2,0,1:T(8,128)S(1)} %bitcast_add_fusion.5), channel_id=1, source_target_pairs={{0,2},{2,4},{4,6},{6,0},{1,3},{3,5},{5,7},{7,1},{8,10},{10,12},{12... | collective-permute-start | bytes 589832 | tf_op jit(solution)/shard_map/ppermute | solution.py:76
  124.3 3.9 %collective-permute-done.20 = f32[24,4,512]{2,0,1:T(8,128)S(1)} collective-permute-done((f32[24,4,512]{2,0,1:T(8,128)S(1)}, f32[24,4,512]{2,0,1:T(8,128)S(1)}, u32[]{:S(2)}, u32[]{:S(2)}) %collective-permute-start.20) | collective-permute-done | bytes 196640 | tf_op jit(solution)/shard_map/ppermute | solution.py:77
  129.8 9.7 %collective-permute-done.18 = f32[24,4,512]{2,0,1:T(8,128)S(1)} collective-permute-done((f32[24,4,512]{2,0,1:T(8,128)S(1)}, f32[24,4,512]{2,0,1:T(8,128)S(1)}, u32[]{:S(2)}, u32[]{:S(2)}) %collective-permute-start.18) | collective-permute-done | bytes 196640 | tf_op jit(solution)/shard_map/ppermute | solution.py:76
  141.3 5.5 %collective-permute-done.21 = f32[24,4,512]{2,0,1:T(8,128)S(1)} collective-permute-done((f32[24,4,512]{2,0,1:T(8,128)S(1)}, f32[24,4,512]{2,0,1:T(8,128)S(1)}, u32[]{:S(2)}, u32[]{:S(2)}) %collective-permute-start.21) | collective-permute-done | bytes 196640 | tf_op jit(solution)/shard_map/ppermute | solution.py:77
  148.7 11.0 %collective-permute-done.19 = f32[24,4,512]{2,0,1:T(8,128)S(1)} collective-permute-done((f32[24,4,512]{2,0,1:T(8,128)S(1)}, f32[24,4,512]{2,0,1:T(8,128)S(1)}, u32[]{:S(2)}, u32[]{:S(2)}) %collective-permute-start.19) | collective-permute-done | bytes 196640 | tf_op jit(solution)/shard_map/ppermute | solution.py:76
  159.8 12.0 %reduce-scatter.2.cloned.1.call-done = f32[48,4,512]{2,0,1:T(8,128)} async-done(((f32[384,4,512]{2,0,1:T(8,128)}), f32[48,4,512]{2,0,1:T(8,128)}) %reduce-scatter.2.cloned.1.call-update) | async-done | bytes 393232 | tf_op jit(solution)/shard_map/reduce_scatter | solution.py:95
  (103 shorter events, 31.7 us)
Async XLA Ops:
  12.2 24.6 %all-to-all-start = ((bf16[32,64,256]{2,1,0:T(8,128)(2,1)}), bf16[32,64,256]{2,1,0:T(8,128)(2,1)S(1)}, u32[]{:S(2)}, u32[]{:S(2)}) async-start(bf16[32,64,256]{2,1,0:T(8,128)(2,1)} %bitcast), calls=%async_computation | async-start | bytes 2097152 | tf_op jit(solution)/shard_map/all_to_all | solution.py:38
  21.1 150.7 %reduce-scatter.2.cloned.1.call-start = ((), (), s32[]{:S(2)}) async-start(), calls=%async_computation.2 | async-start | bytes 3538944 | tf_op jit(solution)/shard_map/reduce_scatter | solution.py:95
  43.0 7.8 %collective-permute-start.8 = (bf16[2,2,64,256]{3,2,0,1:T(8,128)(2,1)S(1)}, bf16[2,2,64,256]{3,2,0,1:T(8,128)(2,1)S(1)}, u32[]{:S(2)}, u32[]{:S(2)}) collective-permute-start(bf16[2,2,64,256]{3,2,0,1:T(8,128)(2,1)S(1)} %get-tuple-element.26), channel_id=1, source_target_pairs={{0,48},{16,0},{32,16},{48,32},{1,49},{17,1},{33,17},{49,33},{2,50}... | collective-permute-start | bytes 393224 | tf_op jit(solution)/shard_map/ppermute | solution.py:17
  44.3 6.5 %collective-permute-start.9 = (bf16[2,2,64,256]{3,2,0,1:T(8,128)(2,1)S(1)}, bf16[2,2,64,256]{3,2,0,1:T(8,128)(2,1)S(1)}, u32[]{:S(2)}, u32[]{:S(2)}) collective-permute-start(bf16[2,2,64,256]{3,2,0,1:T(8,128)(2,1)S(1)} %get-tuple-element.26), channel_id=1, source_target_pairs={{0,16},{16,32},{32,48},{48,0},{1,17},{17,33},{33,49},{49,1},{2,18}... | collective-permute-start | bytes 393224 | tf_op jit(solution)/shard_map/ppermute | solution.py:16
  45.1 10.3 %collective-permute-start = (bf16[2,2,64,256]{3,2,0,1:T(8,128)(2,1)S(1)}, bf16[2,2,64,256]{3,2,0,1:T(8,128)(2,1)S(1)}, u32[]{:S(2)}, u32[]{:S(2)}) collective-permute-start(bf16[2,2,64,256]{3,2,0,1:T(8,128)(2,1)S(1)} %get-tuple-element.25), channel_id=1, source_target_pairs={{0,192},{64,0},{128,64},{192,128},{1,193},{65,1},{129,65},{193,129... | collective-permute-start | bytes 393224 | tf_op jit(solution)/shard_map/ppermute | solution.py:17
  45.7 8.4 %collective-permute-start.1 = (bf16[2,2,64,256]{3,2,0,1:T(8,128)(2,1)S(1)}, bf16[2,2,64,256]{3,2,0,1:T(8,128)(2,1)S(1)}, u32[]{:S(2)}, u32[]{:S(2)}) collective-permute-start(bf16[2,2,64,256]{3,2,0,1:T(8,128)(2,1)S(1)} %get-tuple-element.25), channel_id=1, source_target_pairs={{0,64},{64,128},{128,192},{192,0},{1,65},{65,129},{129,193},{193,1... | collective-permute-start | bytes 393224 | tf_op jit(solution)/shard_map/ppermute | solution.py:16
  50.8 5.6 %collective-permute-start.10 = (bf16[1,2,64,256]{3,2,0,1:T(8,128)(2,1)S(1)}, bf16[1,2,64,256]{3,2,0,1:T(8,128)(2,1)S(1)}, u32[]{:S(2)}, u32[]{:S(2)}) collective-permute-start(bf16[1,2,64,256]{3,2,0,1:T(8,128)(2,1)S(1)} %slice.72), channel_id=1, source_target_pairs={{0,16},{16,32},{32,48},{48,0},{1,17},{17,33},{33,49},{49,1},{2,18}... | collective-permute-start | bytes 196616 | tf_op jit(solution)/shard_map/ppermute | solution.py:20
  50.8 5.5 %collective-permute-start.11 = (bf16[1,2,64,256]{3,2,0,1:T(8,128)(2,1)S(1)}, bf16[1,2,64,256]{3,2,0,1:T(8,128)(2,1)S(1)}, u32[]{:S(2)}, u32[]{:S(2)}) collective-permute-start(bf16[1,2,64,256]{3,2,0,1:T(8,128)(2,1)S(1)} %slice.73), channel_id=1, source_target_pairs={{0,48},{16,0},{32,16},{48,32},{1,49},{17,1},{33,17},{49,33},{2,50}... | collective-permute-start | bytes 196616 | tf_op jit(solution)/shard_map/ppermute | solution.py:20
  54.1 4.3 %collective-permute-start.2 = (bf16[1,2,64,256]{3,2,0,1:T(8,128)(2,1)S(1)}, bf16[1,2,64,256]{3,2,0,1:T(8,128)(2,1)S(1)}, u32[]{:S(2)}, u32[]{:S(2)}) collective-permute-start(bf16[1,2,64,256]{3,2,0,1:T(8,128)(2,1)S(1)} %slice.67), channel_id=1, source_target_pairs={{0,64},{64,128},{128,192},{192,0},{1,65},{65,129},{129,193},{193,1... | collective-permute-start | bytes 196616 | tf_op jit(solution)/shard_map/ppermute | solution.py:20
  55.4 5.6 %collective-permute-start.3 = (bf16[1,2,64,256]{3,2,0,1:T(8,128)(2,1)S(1)}, bf16[1,2,64,256]{3,2,0,1:T(8,128)(2,1)S(1)}, u32[]{:S(2)}, u32[]{:S(2)}) collective-permute-start(bf16[1,2,64,256]{3,2,0,1:T(8,128)(2,1)S(1)} %slice.68), channel_id=1, source_target_pairs={{0,192},{64,0},{128,64},{192,128},{1,193},{65,1},{129,65},{193,129... | collective-permute-start | bytes 196616 | tf_op jit(solution)/shard_map/ppermute | solution.py:20
  61.2 15.6 %collective-permute-start.4 = (bf16[4,2,2,64,256]{4,3,1,2,0:T(8,128)(2,1)S(1)}, bf16[4,2,2,64,256]{4,3,1,2,0:T(8,128)(2,1)S(1)}, u32[]{:S(2)}, u32[]{:S(2)}) collective-permute-start(bf16[4,2,2,64,256]{4,3,1,2,0:T(8,128)(2,1)S(1)} %get-tuple-element.10), channel_id=1, source_target_pairs={{0,48},{16,0},{32,16},{48,32},{1,49},{17,1},{33,17},{49,33},{2,50}... | collective-permute-start | bytes 1572872 | tf_op jit(solution)/shard_map/ppermute | solution.py:17
  63.5 13.2 %collective-permute-start.5 = (bf16[4,2,2,64,256]{4,3,1,2,0:T(8,128)(2,1)S(1)}, bf16[4,2,2,64,256]{4,3,1,2,0:T(8,128)(2,1)S(1)}, u32[]{:S(2)}, u32[]{:S(2)}) collective-permute-start(bf16[4,2,2,64,256]{4,3,1,2,0:T(8,128)(2,1)S(1)} %get-tuple-element.10), channel_id=1, source_target_pairs={{0,16},{16,32},{32,48},{48,0},{1,17},{17,33},{33,49},{49,1},{2,18}... | collective-permute-start | bytes 1572872 | tf_op jit(solution)/shard_map/ppermute | solution.py:16
  63.6 16.7 %collective-permute-start.13 = (bf16[4,2,2,64,256]{4,3,1,2,0:T(8,128)(2,1)S(1)}, bf16[4,2,2,64,256]{4,3,1,2,0:T(8,128)(2,1)S(1)}, u32[]{:S(2)}, u32[]{:S(2)}) collective-permute-start(bf16[4,2,2,64,256]{4,3,1,2,0:T(8,128)(2,1)S(1)} %get-tuple-element.12), channel_id=1, source_target_pairs={{0,64},{64,128},{128,192},{192,0},{1,65},{65,129},{129,193},{193,1... | collective-permute-start | bytes 1572872 | tf_op jit(solution)/shard_map/ppermute | solution.py:16
  63.7 16.7 %collective-permute-start.12 = (bf16[4,2,2,64,256]{4,3,1,2,0:T(8,128)(2,1)S(1)}, bf16[4,2,2,64,256]{4,3,1,2,0:T(8,128)(2,1)S(1)}, u32[]{:S(2)}, u32[]{:S(2)}) collective-permute-start(bf16[4,2,2,64,256]{4,3,1,2,0:T(8,128)(2,1)S(1)} %get-tuple-element.12), channel_id=1, source_target_pairs={{0,192},{64,0},{128,64},{192,128},{1,193},{65,1},{129,65},{193,129... | collective-permute-start | bytes 1572872 | tf_op jit(solution)/shard_map/ppermute | solution.py:17
  76.7 7.7 %collective-permute-start.6 = (bf16[2,2,2,64,256]{4,3,1,2,0:T(8,128)(2,1)S(1)}, bf16[2,2,2,64,256]{4,3,1,2,0:T(8,128)(2,1)S(1)}, u32[]{:S(2)}, u32[]{:S(2)}) collective-permute-start(bf16[2,2,2,64,256]{4,3,1,2,0:T(8,128)(2,1)S(1)} %slice.69), channel_id=1, source_target_pairs={{0,16},{16,32},{32,48},{48,0},{1,17},{17,33},{33,49},{49,1},{2,18}... | collective-permute-start | bytes 786440 | tf_op jit(solution)/shard_map/ppermute | solution.py:20
  76.9 7.5 %collective-permute-start.7 = (bf16[2,2,2,64,256]{4,3,1,2,0:T(8,128)(2,1)S(1)}, bf16[2,2,2,64,256]{4,3,1,2,0:T(8,128)(2,1)S(1)}, u32[]{:S(2)}, u32[]{:S(2)}) collective-permute-start(bf16[2,2,2,64,256]{4,3,1,2,0:T(8,128)(2,1)S(1)} %slice.70), channel_id=1, source_target_pairs={{0,48},{16,0},{32,16},{48,32},{1,49},{17,1},{33,17},{49,33},{2,50}... | collective-permute-start | bytes 786440 | tf_op jit(solution)/shard_map/ppermute | solution.py:20
  80.3 6.4 %collective-permute-start.14 = (bf16[2,2,2,64,256]{4,3,1,2,0:T(8,128)(2,1)S(1)}, bf16[2,2,2,64,256]{4,3,1,2,0:T(8,128)(2,1)S(1)}, u32[]{:S(2)}, u32[]{:S(2)}) collective-permute-start(bf16[2,2,2,64,256]{4,3,1,2,0:T(8,128)(2,1)S(1)} %slice.74), channel_id=1, source_target_pairs={{0,64},{64,128},{128,192},{192,0},{1,65},{65,129},{129,193},{193,1... | collective-permute-start | bytes 786440 | tf_op jit(solution)/shard_map/ppermute | solution.py:20
  80.5 7.7 %collective-permute-start.15 = (bf16[2,2,2,64,256]{4,3,1,2,0:T(8,128)(2,1)S(1)}, bf16[2,2,2,64,256]{4,3,1,2,0:T(8,128)(2,1)S(1)}, u32[]{:S(2)}, u32[]{:S(2)}) collective-permute-start(bf16[2,2,2,64,256]{4,3,1,2,0:T(8,128)(2,1)S(1)} %slice.75), channel_id=1, source_target_pairs={{0,192},{64,0},{128,64},{192,128},{1,193},{65,1},{129,65},{193,129... | collective-permute-start | bytes 786440 | tf_op jit(solution)/shard_map/ppermute | solution.py:20
  106.6 15.3 %collective-permute-start.17 = (f32[24,4,512]{2,0,1:T(8,128)S(1)}, f32[24,4,512]{2,0,1:T(8,128)S(1)}, u32[]{:S(2)}, u32[]{:S(2)}) collective-permute-start(f32[24,4,512]{2,0,1:T(8,128)S(1)} %dynamic-slice_bitcast_fusion.2), channel_id=1, source_target_pairs={{0,2},{2,4},{4,6},{6,0},{1,3},{3,5},{5,7},{7,1},{8,10},{10,12},{12... | collective-permute-start | bytes 589832 | tf_op jit(solution)/shard_map/ppermute | solution.py:76
  109.9 18.3 %collective-permute-start.20 = (f32[24,4,512]{2,0,1:T(8,128)S(1)}, f32[24,4,512]{2,0,1:T(8,128)S(1)}, u32[]{:S(2)}, u32[]{:S(2)}) collective-permute-start(f32[24,4,512]{2,0,1:T(8,128)S(1)} %dynamic-slice_bitcast_fusion.1), channel_id=1, source_target_pairs={{0,6},{2,0},{4,2},{6,4},{1,7},{3,1},{5,3},{7,5},{8,14},{10,8},{12,... | collective-permute-start | bytes 589832 | tf_op jit(solution)/shard_map/ppermute | solution.py:77
  121.9 17.6 %collective-permute-start.18 = (f32[24,4,512]{2,0,1:T(8,128)S(1)}, f32[24,4,512]{2,0,1:T(8,128)S(1)}, u32[]{:S(2)}, u32[]{:S(2)}) collective-permute-start(f32[24,4,512]{2,0,1:T(8,128)S(1)} %bitcast_add_fusion.5), channel_id=1, source_target_pairs={{0,2},{2,4},{4,6},{6,0},{1,3},{3,5},{5,7},{7,1},{8,10},{10,12},{12... | collective-permute-start | bytes 589832 | tf_op jit(solution)/shard_map/ppermute | solution.py:76
  128.2 18.6 %collective-permute-start.21 = (f32[24,4,512]{2,0,1:T(8,128)S(1)}, f32[24,4,512]{2,0,1:T(8,128)S(1)}, u32[]{:S(2)}, u32[]{:S(2)}) collective-permute-start(f32[24,4,512]{2,0,1:T(8,128)S(1)} %bitcast_add_fusion.2), channel_id=1, source_target_pairs={{0,6},{2,0},{4,2},{6,4},{1,7},{3,1},{5,3},{7,5},{8,14},{10,8},{12,... | collective-permute-start | bytes 589832 | tf_op jit(solution)/shard_map/ppermute | solution.py:77
  139.5 20.3 %collective-permute-start.19 = (f32[24,4,512]{2,0,1:T(8,128)S(1)}, f32[24,4,512]{2,0,1:T(8,128)S(1)}, u32[]{:S(2)}, u32[]{:S(2)}) collective-permute-start(f32[24,4,512]{2,0,1:T(8,128)S(1)} %bitcast_add_fusion.4), channel_id=1, source_target_pairs={{0,2},{2,4},{4,6},{6,0},{1,3},{3,5},{5,7},{7,1},{8,10},{10,12},{12... | collective-permute-start | bytes 589832 | tf_op jit(solution)/shard_map/ppermute | solution.py:76
  146.8 12.9 %collective-permute-start.22 = (f32[24,4,512]{2,0,1:T(8,128)S(1)}, f32[24,4,512]{2,0,1:T(8,128)S(1)}, u32[]{:S(2)}, u32[]{:S(2)}) collective-permute-start(f32[24,4,512]{2,0,1:T(8,128)S(1)} %bitcast_add_fusion.1), channel_id=1, source_target_pairs={{0,6},{2,0},{4,2},{6,4},{1,7},{3,1},{5,3},{7,5},{8,14},{10,8},{12,... | collective-permute-start | bytes 589832 | tf_op jit(solution)/shard_map/ppermute | solution.py:77
  (4 other events, 44.8 us)
Sparse Core Ops, SparseCore 0:
  99.5 72.3 reduce-scatter.1

commit v10 on v9

--- a/solution.py
+++ b/solution.py
@@ -37,7 +37,11 @@
     pieces = block.reshape(parts * freq * split, kb // split, recv)
     got = lax.all_to_all(pieces, SHOT, 0, 0, tiled=True)
     chosen = jnp.take(got, column, axis=0)
-    full = lax.all_gather(chosen, "zl", axis=0, tiled=False)
+    n_zl = lax.psum(1, "zl")
+    me_zl = lax.axis_index("zl")
+    other = lax.ppermute(chosen, "zl", [(i, n_zl - 1 - i) for i in range(n_zl)])
+    pair = jnp.stack([chosen, other, chosen], axis=0)
+    full = lax.dynamic_slice_in_dim(pair, (n_zl - me_zl) % n_zl, n_zl, axis=0)
     n_y, n_x, n_zl = lax.psum(1, "y"), lax.psum(1, "x"), full.shape[0]
     first = ring_gather(ring_gather(full[:, : STEPS // 2], "x"), "y")
     second = ring_gather(ring_gather(full[:, STEPS // 2 :], "y"), "x")

time: 183 us -> 183 us (level)
  blocking collectives: 5.64 us -> 0 us
  waiting for transfers between devices: 93.9 us -> 98 us
    all_gather x1 -> x0, blocking collectives: 5.64 us -> none  [gather_receivers(): full = lax.all_gather(chosen, 'zl', axis=0, tiled=False)]
    ppermute x0 -> x1, waiting for transfers between devices: none -> 4.04 us  [gather_receivers(): other = lax.ppermute(chosen, 'zl', [(i, n_zl - 1 - i) for i in range(n_zl)])]
  transfers between devices with their start and end apart: 25 -> 26, of which waited for: 15 -> 16; matrix products, arithmetic and copies ran while one was open for 2% -> 2% of each run, Pallas kernels for 0% -> 0%
where the time goes in v10:
time: 183 us; the launch traced here: 181 us
  waiting for transfers between devices  98 us (54%)
  starting transfers between devices  44.5 us (24%)
  between operations  15.9 us (9%)
  local copies, waits for them, and re-layouts  9.97 us (5%)
  other arithmetic  6.85 us (4%)
  matrix products  5.98 us (3%)
    ppermute x3, waiting for transfers between devices, reduce_rows(): got_lo = lax.ppermute(acc_lo, 'zh', fwd)  30.2 us
    all_to_all x1, waiting for transfers between devices, gather_receivers(): got = lax.all_to_all(pieces, SHOT, 0, 0, tiled=True)  15.3 us
    ppermute x4, waiting for transfers between devices, ring_gather(): from_left = lax.ppermute(piece, axis, fwd)  13.3 us
    reduce_scatter x1, waiting for transfers between devices, body(): lax.psum_scatter(out[:, :half], SP, scatter_dimension=0, tiled=True)  12.5 us
    ppermute x4, starting transfers between devices, ring_gather(): lax.ppermute(from_right[half:], axis, bwd)  9.49 us
    ppermute x3, waiting for transfers between devices, reduce_rows(): got_hi = lax.ppermute(acc_hi, 'zh', bwd)  9.19 us
    all_to_all x1, starting transfers between devices, gather_receivers(): got = lax.all_to_all(pieces, SHOT, 0, 0, tiled=True)  8.96 us
    ppermute x3, starting transfers between devices, reduce_rows(): got_lo = lax.ppermute(acc_lo, 'zh', fwd)  7.58 us
  transfers between devices with their start and end apart: 26, of which 16 were waited for; matrix products, arithmetic and copies ran while one was open for 2% of the time, Pallas kernels for 0%

profile of v10, /device:TPU:6, one launch (start us, length us, event | category | flops | bytes accessed | tf_op | source)
XLA Modules:
  0.0 181.2 jit_solution(8705473322169487539)
XLA Ops:
  10.1 2.3 %constant_dynamic-slice_fusion.5 = bf16[1,2,8,128,256]{4,3,2,1,0:T(8,128)(2,1)} fusion(bf16[4,2,8,128,256]{4,3,2,1,0:T(8,128)(2,1)} %param.6, s32[]{:T(128)S(6)} %select_n.124), kind=kLoop, calls=%fused_computation.75 | loop fusion | bytes 2097156 | tf_op jit(solution)/shard_map/jit(dynamic_index_in_dim)/dynamic_slice | solution.py:34
  12.4 9.0 %all-to-all-start = ((bf16[32,64,256]{2,1,0:T(8,128)(2,1)}), bf16[32,64,256]{2,1,0:T(8,128)(2,1)S(1)}, u32[]{:S(2)}, u32[]{:S(2)}) async-start(bf16[32,64,256]{2,1,0:T(8,128)(2,1)} %bitcast), calls=%async_computation | async-start | bytes 2097152 | tf_op jit(solution)/shard_map/all_to_all | solution.py:38
  21.6 15.3 %all-to-all-done = bf16[32,64,256]{2,1,0:T(8,128)(2,1)S(1)} async-done(((bf16[32,64,256]{2,1,0:T(8,128)(2,1)}), bf16[32,64,256]{2,1,0:T(8,128)(2,1)S(1)}, u32[]{:S(2)}, u32[]{:S(2)}) %all-to-all-start) | async-done | bytes 1048608 | tf_op jit(solution)/shard_map/all_to_all | solution.py:38
  38.6 4.0 %collective-permute-done = bf16[4,64,256]{2,1,0:T(8,128)(2,1)S(1)} collective-permute-done((bf16[4,64,256]{2,1,0:T(8,128)(2,1)S(1)}, bf16[4,64,256]{2,1,0:T(8,128)(2,1)S(1)}, u32[]{:S(2)}, u32[]{:S(2)}) %collective-permute-start) | collective-permute-done | bytes 131104 | tf_op jit(solution)/shard_map/ppermute | solution.py:42
  45.5 2.6 %collective-permute-start.2 = (bf16[2,2,64,256]{3,2,0,1:T(8,128)(2,1)S(1)}, bf16[2,2,64,256]{3,2,0,1:T(8,128)(2,1)S(1)}, u32[]{:S(2)}, u32[]{:S(2)}) collective-permute-start(bf16[2,2,64,256]{3,2,0,1:T(8,128)(2,1)S(1)} %get-tuple-element.25), channel_id=1, source_target_pairs={{0,64},{64,128},{128,192},{192,0},{1,65},{65,129},{129,193},{193,1... | collective-permute-start | bytes 393224 | tf_op jit(solution)/shard_map/ppermute | solution.py:16
  48.2 2.3 %collective-permute-done.10 = bf16[2,2,64,256]{3,2,0,1:T(8,128)(2,1)S(1)} collective-permute-done((bf16[2,2,64,256]{3,2,0,1:T(8,128)(2,1)S(1)}, bf16[2,2,64,256]{3,2,0,1:T(8,128)(2,1)S(1)}, u32[]{:S(2)}, u32[]{:S(2)}) %collective-permute-start.10) | collective-permute-done | bytes 131104 | tf_op jit(solution)/shard_map/ppermute | solution.py:16
  50.6 3.2 %collective-permute-start.12 = (bf16[1,2,64,256]{3,2,0,1:T(8,128)(2,1)S(1)}, bf16[1,2,64,256]{3,2,0,1:T(8,128)(2,1)S(1)}, u32[]{:S(2)}, u32[]{:S(2)}) collective-permute-start(bf16[1,2,64,256]{3,2,0,1:T(8,128)(2,1)S(1)} %slice.73), channel_id=1, source_target_pairs={{0,48},{16,0},{32,16},{48,32},{1,49},{17,1},{33,17},{49,33},{2,50}... | collective-permute-start | bytes 196616 | tf_op jit(solution)/shard_map/ppermute | solution.py:20
  58.2 2.5 %collective-permute-done.4 = bf16[1,2,64,256]{3,2,0,1:T(8,128)(2,1)S(1)} collective-permute-done((bf16[1,2,64,256]{3,2,0,1:T(8,128)(2,1)S(1)}, bf16[1,2,64,256]{3,2,0,1:T(8,128)(2,1)S(1)}, u32[]{:S(2)}, u32[]{:S(2)}) %collective-permute-start.4) | collective-permute-done | bytes 65568 | tf_op jit(solution)/shard_map/ppermute | solution.py:20
  60.9 2.3 %collective-permute-start.5 = (bf16[4,2,2,64,256]{4,3,1,2,0:T(8,128)(2,1)S(1)}, bf16[4,2,2,64,256]{4,3,1,2,0:T(8,128)(2,1)S(1)}, u32[]{:S(2)}, u32[]{:S(2)}) collective-permute-start(bf16[4,2,2,64,256]{4,3,1,2,0:T(8,128)(2,1)S(1)} %get-tuple-element.10), channel_id=1, source_target_pairs={{0,48},{16,0},{32,16},{48,32},{1,49},{17,1},{33,17},{49,33},{2,50}... | collective-permute-start | bytes 1572872 | tf_op jit(solution)/shard_map/ppermute | solution.py:17
  65.6 10.9 %collective-permute-done.6 = bf16[4,2,2,64,256]{4,3,1,2,0:T(8,128)(2,1)S(1)} collective-permute-done((bf16[4,2,2,64,256]{4,3,1,2,0:T(8,128)(2,1)S(1)}, bf16[4,2,2,64,256]{4,3,1,2,0:T(8,128)(2,1)S(1)}, u32[]{:S(2)}, u32[]{:S(2)}) %collective-permute-start.6) | collective-permute-done | bytes 524320 | tf_op jit(solution)/shard_map/ppermute | solution.py:16
  76.8 3.3 %collective-permute-start.8 = (bf16[2,2,2,64,256]{4,3,1,2,0:T(8,128)(2,1)S(1)}, bf16[2,2,2,64,256]{4,3,1,2,0:T(8,128)(2,1)S(1)}, u32[]{:S(2)}, u32[]{:S(2)}) collective-permute-start(bf16[2,2,2,64,256]{4,3,1,2,0:T(8,128)(2,1)S(1)} %slice.70), channel_id=1, source_target_pairs={{0,48},{16,0},{32,16},{48,32},{1,49},{17,1},{33,17},{49,33},{2,50}... | collective-permute-start | bytes 786440 | tf_op jit(solution)/shard_map/ppermute | solution.py:20
  84.5 2.1 %collective-permute-done.15 = bf16[2,2,2,64,256]{4,3,1,2,0:T(8,128)(2,1)S(1)} collective-permute-done((bf16[2,2,2,64,256]{4,3,1,2,0:T(8,128)(2,1)S(1)}, bf16[2,2,2,64,256]{4,3,1,2,0:T(8,128)(2,1)S(1)}, u32[]{:S(2)}, u32[]{:S(2)}) %collective-permute-start.15) | collective-permute-done | bytes 262176 | tf_op jit(solution)/shard_map/ppermute | solution.py:20
  90.7 6.0 %fusion.4 = f32[384,8,512]{2,0,1:T(8,128)S(1)} fusion(bf16[2,8,384,512]{3,2,1,0:T(8,128)(2,1)} %param.4, bf16[384,512]{1,0:T(8,128)(2,1)S(1)} %convert_element_type.7, bf16[1,8,512,512]{3,2,0,1:T(8,128)(2,1)S(1)} %get-tuple-element.20, bf16[1,8,512,512]{3,2,0,1:T(8,128)(2,1)S(1)} %get-tuple-element.19), kind=kOutput, calls=%fused_computation.9 | convolution fusion | flops 3228565504 | bytes 21364736 | tf_op jit(solution)/shard_map/dot_general | solution.py:94
  96.7 2.4 %fusion.23 = (f32[384,4,512]{2,0,1:T(8,128)}, f32[384,4,512]{2,0,1:T(8,128)S(1)}) fusion(f32[384,8,512]{2,0,1:T(8,128)S(1)} %fusion.4), kind=kLoop, calls=%fused_computation.82 | loop fusion | bytes 12582912 | tf_op jit(solution)/shard_map/slice | solution.py:99
  100.9 3.5 %collective-permute-done.17 = f32[4,48,4,512]{3,1,2,0:T(8,128)} collective-permute-done((f32[4,48,4,512]{3,1,2,0:T(8,128)S(1)}, f32[4,48,4,512]{3,1,2,0:T(8,128)}, u32[]{:S(2)}, u32[]{:S(2)}) %collective-permute-start.17) | collective-permute-done | bytes 1572896 | tf_op jit(solution)/shard_map/ppermute | solution.py:67
  106.3 3.3 %collective-permute-start.18 = (f32[24,4,512]{2,0,1:T(8,128)S(1)}, f32[24,4,512]{2,0,1:T(8,128)S(1)}, u32[]{:S(2)}, u32[]{:S(2)}) collective-permute-start(f32[24,4,512]{2,0,1:T(8,128)S(1)} %dynamic-slice_bitcast_fusion.2), channel_id=1, source_target_pairs={{0,2},{2,4},{4,6},{6,0},{1,3},{3,5},{5,7},{7,1},{8,10},{10,12},{12... | collective-permute-start | bytes 589832 | tf_op jit(solution)/shard_map/ppermute | solution.py:80
  109.7 2.3 %collective-permute-start.21 = (f32[24,4,512]{2,0,1:T(8,128)S(1)}, f32[24,4,512]{2,0,1:T(8,128)S(1)}, u32[]{:S(2)}, u32[]{:S(2)}) collective-permute-start(f32[24,4,512]{2,0,1:T(8,128)S(1)} %dynamic-slice_bitcast_fusion.1), channel_id=1, source_target_pairs={{0,6},{2,0},{4,2},{6,4},{1,7},{3,1},{5,3},{7,5},{8,14},{10,8},{12,... | collective-permute-start | bytes 589832 | tf_op jit(solution)/shard_map/ppermute | solution.py:81
  112.0 9.6 %collective-permute-done.18 = f32[24,4,512]{2,0,1:T(8,128)S(1)} collective-permute-done((f32[24,4,512]{2,0,1:T(8,128)S(1)}, f32[24,4,512]{2,0,1:T(8,128)S(1)}, u32[]{:S(2)}, u32[]{:S(2)}) %collective-permute-start.18) | collective-permute-done | bytes 196640 | tf_op jit(solution)/shard_map/ppermute | solution.py:80
  121.7 2.4 %collective-permute-start.19 = (f32[24,4,512]{2,0,1:T(8,128)S(1)}, f32[24,4,512]{2,0,1:T(8,128)S(1)}, u32[]{:S(2)}, u32[]{:S(2)}) collective-permute-start(f32[24,4,512]{2,0,1:T(8,128)S(1)} %bitcast_add_fusion.5), channel_id=1, source_target_pairs={{0,2},{2,4},{4,6},{6,0},{1,3},{3,5},{5,7},{7,1},{8,10},{10,12},{12... | collective-permute-start | bytes 589832 | tf_op jit(solution)/shard_map/ppermute | solution.py:80
  124.1 3.9 %collective-permute-done.21 = f32[24,4,512]{2,0,1:T(8,128)S(1)} collective-permute-done((f32[24,4,512]{2,0,1:T(8,128)S(1)}, f32[24,4,512]{2,0,1:T(8,128)S(1)}, u32[]{:S(2)}, u32[]{:S(2)}) %collective-permute-start.21) | collective-permute-done | bytes 196640 | tf_op jit(solution)/shard_map/ppermute | solution.py:81
  129.5 9.7 %collective-permute-done.19 = f32[24,4,512]{2,0,1:T(8,128)S(1)} collective-permute-done((f32[24,4,512]{2,0,1:T(8,128)S(1)}, f32[24,4,512]{2,0,1:T(8,128)S(1)}, u32[]{:S(2)}, u32[]{:S(2)}) %collective-permute-start.19) | collective-permute-done | bytes 196640 | tf_op jit(solution)/shard_map/ppermute | solution.py:80
  141.1 5.3 %collective-permute-done.22 = f32[24,4,512]{2,0,1:T(8,128)S(1)} collective-permute-done((f32[24,4,512]{2,0,1:T(8,128)S(1)}, f32[24,4,512]{2,0,1:T(8,128)S(1)}, u32[]{:S(2)}, u32[]{:S(2)}) %collective-permute-start.22) | collective-permute-done | bytes 196640 | tf_op jit(solution)/shard_map/ppermute | solution.py:81
  148.5 10.9 %collective-permute-done.20 = f32[24,4,512]{2,0,1:T(8,128)S(1)} collective-permute-done((f32[24,4,512]{2,0,1:T(8,128)S(1)}, f32[24,4,512]{2,0,1:T(8,128)S(1)}, u32[]{:S(2)}, u32[]{:S(2)}) %collective-permute-start.20) | collective-permute-done | bytes 196640 | tf_op jit(solution)/shard_map/ppermute | solution.py:80
  159.5 12.5 %reduce-scatter.2.cloned.1.call-done = f32[48,4,512]{2,0,1:T(8,128)} async-done(((f32[384,4,512]{2,0,1:T(8,128)}), f32[48,4,512]{2,0,1:T(8,128)}) %reduce-scatter.2.cloned.1.call-update) | async-done | bytes 393232 | tf_op jit(solution)/shard_map/reduce_scatter | solution.py:99
  (106 shorter events, 33.4 us)
Async XLA Ops:
  12.4 24.6 %all-to-all-start = ((bf16[32,64,256]{2,1,0:T(8,128)(2,1)}), bf16[32,64,256]{2,1,0:T(8,128)(2,1)S(1)}, u32[]{:S(2)}, u32[]{:S(2)}) async-start(bf16[32,64,256]{2,1,0:T(8,128)(2,1)} %bitcast), calls=%async_computation | async-start | bytes 2097152 | tf_op jit(solution)/shard_map/all_to_all | solution.py:38
  21.3 150.7 %reduce-scatter.2.cloned.1.call-start = ((), (), s32[]{:S(2)}) async-start(), calls=%async_computation.2 | async-start | bytes 3538944 | tf_op jit(solution)/shard_map/reduce_scatter | solution.py:99
  37.6 5.1 %collective-permute-start = (bf16[4,64,256]{2,1,0:T(8,128)(2,1)S(1)}, bf16[4,64,256]{2,1,0:T(8,128)(2,1)S(1)}, u32[]{:S(2)}, u32[]{:S(2)}) collective-permute-start(bf16[4,64,256]{2,1,0:T(8,128)(2,1)S(1)} %broadcast_select_fusion), channel_id=1, source_target_pairs={{0,8},{8,0},{1,9},{9,1},{2,10},{10,2},{3,11},{11,3},{4,12},{12,4},... | collective-permute-start | bytes 393224 | tf_op jit(solution)/shard_map/ppermute | solution.py:42
  42.8 7.8 %collective-permute-start.9 = (bf16[2,2,64,256]{3,2,0,1:T(8,128)(2,1)S(1)}, bf16[2,2,64,256]{3,2,0,1:T(8,128)(2,1)S(1)}, u32[]{:S(2)}, u32[]{:S(2)}) collective-permute-start(bf16[2,2,64,256]{3,2,0,1:T(8,128)(2,1)S(1)} %get-tuple-element.26), channel_id=1, source_target_pairs={{0,48},{16,0},{32,16},{48,32},{1,49},{17,1},{33,17},{49,33},{2,50}... | collective-permute-start | bytes 393224 | tf_op jit(solution)/shard_map/ppermute | solution.py:17
  44.1 6.5 %collective-permute-start.10 = (bf16[2,2,64,256]{3,2,0,1:T(8,128)(2,1)S(1)}, bf16[2,2,64,256]{3,2,0,1:T(8,128)(2,1)S(1)}, u32[]{:S(2)}, u32[]{:S(2)}) collective-permute-start(bf16[2,2,64,256]{3,2,0,1:T(8,128)(2,1)S(1)} %get-tuple-element.26), channel_id=1, source_target_pairs={{0,16},{16,32},{32,48},{48,0},{1,17},{17,33},{33,49},{49,1},{2,18}... | collective-permute-start | bytes 393224 | tf_op jit(solution)/shard_map/ppermute | solution.py:16
  44.9 10.3 %collective-permute-start.1 = (bf16[2,2,64,256]{3,2,0,1:T(8,128)(2,1)S(1)}, bf16[2,2,64,256]{3,2,0,1:T(8,128)(2,1)S(1)}, u32[]{:S(2)}, u32[]{:S(2)}) collective-permute-start(bf16[2,2,64,256]{3,2,0,1:T(8,128)(2,1)S(1)} %get-tuple-element.25), channel_id=1, source_target_pairs={{0,192},{64,0},{128,64},{192,128},{1,193},{65,1},{129,65},{193,129... | collective-permute-start | bytes 393224 | tf_op jit(solution)/shard_map/ppermute | solution.py:17
  45.5 8.4 %collective-permute-start.2 = (bf16[2,2,64,256]{3,2,0,1:T(8,128)(2,1)S(1)}, bf16[2,2,64,256]{3,2,0,1:T(8,128)(2,1)S(1)}, u32[]{:S(2)}, u32[]{:S(2)}) collective-permute-start(bf16[2,2,64,256]{3,2,0,1:T(8,128)(2,1)S(1)} %get-tuple-element.25), channel_id=1, source_target_pairs={{0,64},{64,128},{128,192},{192,0},{1,65},{65,129},{129,193},{193,1... | collective-permute-start | bytes 393224 | tf_op jit(solution)/shard_map/ppermute | solution.py:16
  50.5 5.6 %collective-permute-start.11 = (bf16[1,2,64,256]{3,2,0,1:T(8,128)(2,1)S(1)}, bf16[1,2,64,256]{3,2,0,1:T(8,128)(2,1)S(1)}, u32[]{:S(2)}, u32[]{:S(2)}) collective-permute-start(bf16[1,2,64,256]{3,2,0,1:T(8,128)(2,1)S(1)} %slice.72), channel_id=1, source_target_pairs={{0,16},{16,32},{32,48},{48,0},{1,17},{17,33},{33,49},{49,1},{2,18}... | collective-permute-start | bytes 196616 | tf_op jit(solution)/shard_map/ppermute | solution.py:20
  50.6 5.5 %collective-permute-start.12 = (bf16[1,2,64,256]{3,2,0,1:T(8,128)(2,1)S(1)}, bf16[1,2,64,256]{3,2,0,1:T(8,128)(2,1)S(1)}, u32[]{:S(2)}, u32[]{:S(2)}) collective-permute-start(bf16[1,2,64,256]{3,2,0,1:T(8,128)(2,1)S(1)} %slice.73), channel_id=1, source_target_pairs={{0,48},{16,0},{32,16},{48,32},{1,49},{17,1},{33,17},{49,33},{2,50}... | collective-permute-start | bytes 196616 | tf_op jit(solution)/shard_map/ppermute | solution.py:20
  55.2 5.6 %collective-permute-start.4 = (bf16[1,2,64,256]{3,2,0,1:T(8,128)(2,1)S(1)}, bf16[1,2,64,256]{3,2,0,1:T(8,128)(2,1)S(1)}, u32[]{:S(2)}, u32[]{:S(2)}) collective-permute-start(bf16[1,2,64,256]{3,2,0,1:T(8,128)(2,1)S(1)} %slice.68), channel_id=1, source_target_pairs={{0,192},{64,0},{128,64},{192,128},{1,193},{65,1},{129,65},{193,129... | collective-permute-start | bytes 196616 | tf_op jit(solution)/shard_map/ppermute | solution.py:20
  60.9 15.8 %collective-permute-start.5 = (bf16[4,2,2,64,256]{4,3,1,2,0:T(8,128)(2,1)S(1)}, bf16[4,2,2,64,256]{4,3,1,2,0:T(8,128)(2,1)S(1)}, u32[]{:S(2)}, u32[]{:S(2)}) collective-permute-start(bf16[4,2,2,64,256]{4,3,1,2,0:T(8,128)(2,1)S(1)} %get-tuple-element.10), channel_id=1, source_target_pairs={{0,48},{16,0},{32,16},{48,32},{1,49},{17,1},{33,17},{49,33},{2,50}... | collective-permute-start | bytes 1572872 | tf_op jit(solution)/shard_map/ppermute | solution.py:17
  63.3 13.2 %collective-permute-start.6 = (bf16[4,2,2,64,256]{4,3,1,2,0:T(8,128)(2,1)S(1)}, bf16[4,2,2,64,256]{4,3,1,2,0:T(8,128)(2,1)S(1)}, u32[]{:S(2)}, u32[]{:S(2)}) collective-permute-start(bf16[4,2,2,64,256]{4,3,1,2,0:T(8,128)(2,1)S(1)} %get-tuple-element.10), channel_id=1, source_target_pairs={{0,16},{16,32},{32,48},{48,0},{1,17},{17,33},{33,49},{49,1},{2,18}... | collective-permute-start | bytes 1572872 | tf_op jit(solution)/shard_map/ppermute | solution.py:16
  63.4 16.7 %collective-permute-start.14 = (bf16[4,2,2,64,256]{4,3,1,2,0:T(8,128)(2,1)S(1)}, bf16[4,2,2,64,256]{4,3,1,2,0:T(8,128)(2,1)S(1)}, u32[]{:S(2)}, u32[]{:S(2)}) collective-permute-start(bf16[4,2,2,64,256]{4,3,1,2,0:T(8,128)(2,1)S(1)} %get-tuple-element.12), channel_id=1, source_target_pairs={{0,64},{64,128},{128,192},{192,0},{1,65},{65,129},{129,193},{193,1... | collective-permute-start | bytes 1572872 | tf_op jit(solution)/shard_map/ppermute | solution.py:16
  63.5 16.7 %collective-permute-start.13 = (bf16[4,2,2,64,256]{4,3,1,2,0:T(8,128)(2,1)S(1)}, bf16[4,2,2,64,256]{4,3,1,2,0:T(8,128)(2,1)S(1)}, u32[]{:S(2)}, u32[]{:S(2)}) collective-permute-start(bf16[4,2,2,64,256]{4,3,1,2,0:T(8,128)(2,1)S(1)} %get-tuple-element.12), channel_id=1, source_target_pairs={{0,192},{64,0},{128,64},{192,128},{1,193},{65,1},{129,65},{193,129... | collective-permute-start | bytes 1572872 | tf_op jit(solution)/shard_map/ppermute | solution.py:17
  76.5 7.8 %collective-permute-start.7 = (bf16[2,2,2,64,256]{4,3,1,2,0:T(8,128)(2,1)S(1)}, bf16[2,2,2,64,256]{4,3,1,2,0:T(8,128)(2,1)S(1)}, u32[]{:S(2)}, u32[]{:S(2)}) collective-permute-start(bf16[2,2,2,64,256]{4,3,1,2,0:T(8,128)(2,1)S(1)} %slice.69), channel_id=1, source_target_pairs={{0,16},{16,32},{32,48},{48,0},{1,17},{17,33},{33,49},{49,1},{2,18}... | collective-permute-start | bytes 786440 | tf_op jit(solution)/shard_map/ppermute | solution.py:20
  76.8 7.5 %collective-permute-start.8 = (bf16[2,2,2,64,256]{4,3,1,2,0:T(8,128)(2,1)S(1)}, bf16[2,2,2,64,256]{4,3,1,2,0:T(8,128)(2,1)S(1)}, u32[]{:S(2)}, u32[]{:S(2)}) collective-permute-start(bf16[2,2,2,64,256]{4,3,1,2,0:T(8,128)(2,1)S(1)} %slice.70), channel_id=1, source_target_pairs={{0,48},{16,0},{32,16},{48,32},{1,49},{17,1},{33,17},{49,33},{2,50}... | collective-permute-start | bytes 786440 | tf_op jit(solution)/shard_map/ppermute | solution.py:20
  80.1 6.4 %collective-permute-start.15 = (bf16[2,2,2,64,256]{4,3,1,2,0:T(8,128)(2,1)S(1)}, bf16[2,2,2,64,256]{4,3,1,2,0:T(8,128)(2,1)S(1)}, u32[]{:S(2)}, u32[]{:S(2)}) collective-permute-start(bf16[2,2,2,64,256]{4,3,1,2,0:T(8,128)(2,1)S(1)} %slice.74), channel_id=1, source_target_pairs={{0,64},{64,128},{128,192},{192,0},{1,65},{65,129},{129,193},{193,1... | collective-permute-start | bytes 786440 | tf_op jit(solution)/shard_map/ppermute | solution.py:20
  80.2 7.7 %collective-permute-start.16 = (bf16[2,2,2,64,256]{4,3,1,2,0:T(8,128)(2,1)S(1)}, bf16[2,2,2,64,256]{4,3,1,2,0:T(8,128)(2,1)S(1)}, u32[]{:S(2)}, u32[]{:S(2)}) collective-permute-start(bf16[2,2,2,64,256]{4,3,1,2,0:T(8,128)(2,1)S(1)} %slice.75), channel_id=1, source_target_pairs={{0,192},{64,0},{128,64},{192,128},{1,193},{65,1},{129,65},{193,129... | collective-permute-start | bytes 786440 | tf_op jit(solution)/shard_map/ppermute | solution.py:20
  106.3 15.3 %collective-permute-start.18 = (f32[24,4,512]{2,0,1:T(8,128)S(1)}, f32[24,4,512]{2,0,1:T(8,128)S(1)}, u32[]{:S(2)}, u32[]{:S(2)}) collective-permute-start(f32[24,4,512]{2,0,1:T(8,128)S(1)} %dynamic-slice_bitcast_fusion.2), channel_id=1, source_target_pairs={{0,2},{2,4},{4,6},{6,0},{1,3},{3,5},{5,7},{7,1},{8,10},{10,12},{12... | collective-permute-start | bytes 589832 | tf_op jit(solution)/shard_map/ppermute | solution.py:80
  109.7 18.3 %collective-permute-start.21 = (f32[24,4,512]{2,0,1:T(8,128)S(1)}, f32[24,4,512]{2,0,1:T(8,128)S(1)}, u32[]{:S(2)}, u32[]{:S(2)}) collective-permute-start(f32[24,4,512]{2,0,1:T(8,128)S(1)} %dynamic-slice_bitcast_fusion.1), channel_id=1, source_target_pairs={{0,6},{2,0},{4,2},{6,4},{1,7},{3,1},{5,3},{7,5},{8,14},{10,8},{12,... | collective-permute-start | bytes 589832 | tf_op jit(solution)/shard_map/ppermute | solution.py:81
  121.7 17.5 %collective-permute-start.19 = (f32[24,4,512]{2,0,1:T(8,128)S(1)}, f32[24,4,512]{2,0,1:T(8,128)S(1)}, u32[]{:S(2)}, u32[]{:S(2)}) collective-permute-start(f32[24,4,512]{2,0,1:T(8,128)S(1)} %bitcast_add_fusion.5), channel_id=1, source_target_pairs={{0,2},{2,4},{4,6},{6,0},{1,3},{3,5},{5,7},{7,1},{8,10},{10,12},{12... | collective-permute-start | bytes 589832 | tf_op jit(solution)/shard_map/ppermute | solution.py:80
  128.0 18.4 %collective-permute-start.22 = (f32[24,4,512]{2,0,1:T(8,128)S(1)}, f32[24,4,512]{2,0,1:T(8,128)S(1)}, u32[]{:S(2)}, u32[]{:S(2)}) collective-permute-start(f32[24,4,512]{2,0,1:T(8,128)S(1)} %bitcast_add_fusion.2), channel_id=1, source_target_pairs={{0,6},{2,0},{4,2},{6,4},{1,7},{3,1},{5,3},{7,5},{8,14},{10,8},{12,... | collective-permute-start | bytes 589832 | tf_op jit(solution)/shard_map/ppermute | solution.py:81
  139.2 20.1 %collective-permute-start.20 = (f32[24,4,512]{2,0,1:T(8,128)S(1)}, f32[24,4,512]{2,0,1:T(8,128)S(1)}, u32[]{:S(2)}, u32[]{:S(2)}) collective-permute-start(f32[24,4,512]{2,0,1:T(8,128)S(1)} %bitcast_add_fusion.4), channel_id=1, source_target_pairs={{0,2},{2,4},{4,6},{6,0},{1,3},{3,5},{5,7},{7,1},{8,10},{10,12},{12... | collective-permute-start | bytes 589832 | tf_op jit(solution)/shard_map/ppermute | solution.py:80
  146.4 13.0 %collective-permute-start.23 = (f32[24,4,512]{2,0,1:T(8,128)S(1)}, f32[24,4,512]{2,0,1:T(8,128)S(1)}, u32[]{:S(2)}, u32[]{:S(2)}) collective-permute-start(f32[24,4,512]{2,0,1:T(8,128)S(1)} %bitcast_add_fusion.1), channel_id=1, source_target_pairs={{0,6},{2,0},{4,2},{6,4},{1,7},{3,1},{5,3},{7,5},{8,14},{10,8},{12,... | collective-permute-start | bytes 589832 | tf_op jit(solution)/shard_map/ppermute | solution.py:81
  (5 other events, 49.4 us)
Sparse Core Ops, SparseCore 0:
  99.2 72.7 reduce-scatter.1

commit v11 on v10

--- a/solution.py
+++ b/solution.py
@@ -91,13 +91,16 @@
     weights = jnp.stack(
         [jnp.concatenate([real_in, imag_in], axis=-1), jnp.concatenate([-imag_in, real_in], axis=-1)], axis=0
     )
-    out = lax.dot_general(
-        live, weights, (((0, 3), (0, 2)), ((1,), (1,))), preferred_element_type=jnp.float32
-    )
-    out = jnp.transpose(out, (1, 0, 2))
-    half = out.shape[1] // 2
-    by_scatter = lax.psum_scatter(out[:, :half], SP, scatter_dimension=0, tiled=True)
-    by_ring = reduce_rows(out[:, half:])
+    half = freq // 2
+
+    def product(lo, hi):
+        out = lax.dot_general(
+            live[:, lo:hi], weights[:, lo:hi], (((0, 3), (0, 2)), ((1,), (1,))), preferred_element_type=jnp.float32
+        )
+        return jnp.transpose(out, (1, 0, 2))
+
+    by_scatter = lax.psum_scatter(product(0, half), SP, scatter_dimension=0, tiled=True)
+    by_ring = reduce_rows(product(half, freq))
     out = jnp.concatenate([by_scatter, by_ring], axis=1)
     rows = out.shape[0]
     out = out.reshape(rows, freq, 2, recv).astype(jnp.bfloat16)

time: 183 us -> 181 us (0.989)
  waiting for transfers between devices: 98 us -> 93 us
  matrix products: 5.98 us -> 8.5 us
    reduce_scatter x1, waiting for transfers between devices: 12.5 us -> 4.89 us  [body(): lax.psum_scatter(product(0, half), SP, scatter_dimension=0, tiled=True)]
    ppermute x3, waiting for transfers between devices: 30.2 us -> 37.2 us  [reduce_rows(): got_lo = lax.ppermute(acc_lo, 'zh', fwd)]
    ppermute x3, starting transfers between devices: 5.91 us -> 10.6 us  [reduce_rows(): got_hi = lax.ppermute(acc_hi, 'zh', bwd)]
    ppermute x3, waiting for transfers between devices: 9.19 us -> 4.79 us  [reduce_rows(): got_hi = lax.ppermute(acc_hi, 'zh', bwd)]
    ppermute x3, starting transfers between devices: 7.58 us -> 3.72 us  [reduce_rows(): got_lo = lax.ppermute(acc_lo, 'zh', fwd)]
    unnamed x24 -> x29, local copies, waits for them, and re-layouts: 0.71 us -> 4.01 us
    dot_general x1 -> x2, matrix products: 5.98 us -> 8.5 us  [product(): lax.dot_general(live[:, lo:hi], weights[:, lo:hi], (((0, 3), (0, 2)), ((1...]
    slice x1 -> x0, local copies, waits for them, and re-layouts: 2.4 us -> none  [body(): out[:, :half]]
  transfers between devices with their start and end apart: 26 -> 26, of which waited for: 16 -> 15; matrix products, arithmetic and copies ran while one was open for 2% -> 5% of each run, Pallas kernels for 0% -> 0%
where the time goes in v11:
time: 181 us; the launch traced here: 180 us
  waiting for transfers between devices  93 us (51%)
  starting transfers between devices  45.3 us (25%)
  between operations  16.1 us (9%)
  local copies, waits for them, and re-layouts  9.83 us (5%)
  matrix products  8.5 us (5%)
  other arithmetic  6.93 us (4%)
    ppermute x3, waiting for transfers between devices, reduce_rows(): got_lo = lax.ppermute(acc_lo, 'zh', fwd)  37.2 us
    all_to_all x1, waiting for transfers between devices, gather_receivers(): got = lax.all_to_all(pieces, SHOT, 0, 0, tiled=True)  15.3 us
    ppermute x4, waiting for transfers between devices, ring_gather(): from_left = lax.ppermute(piece, axis, fwd)  13.3 us
    ppermute x3, starting transfers between devices, reduce_rows(): got_hi = lax.ppermute(acc_hi, 'zh', bwd)  10.6 us
    ppermute x4, starting transfers between devices, ring_gather(): lax.ppermute(from_right[half:], axis, bwd)  9.49 us
    all_to_all x1, starting transfers between devices, gather_receivers(): got = lax.all_to_all(pieces, SHOT, 0, 0, tiled=True)  8.96 us
    dot_general x2, matrix products, product(): lax.dot_general(live[:, lo:hi], weights[:, lo:hi], (((0, 3), (0, 2)), ((1...  8.5 us
    ppermute x4, starting transfers between devices, ring_gather(): from_right = lax.ppermute(piece, axis, bwd)  6.18 us
  transfers between devices with their start and end apart: 26, of which 15 were waited for; matrix products, arithmetic and copies ran while one was open for 5% of the time, Pallas kernels for 0%

profile of v11, /device:TPU:6, one launch (start us, length us, event | category | flops | bytes accessed | tf_op | source)
XLA Modules:
  0.0 179.7 jit_solution(15241496548702452098)
XLA Ops:
  10.3 2.3 %constant_dynamic-slice_fusion.5 = bf16[1,2,8,128,256]{4,3,2,1,0:T(8,128)(2,1)} fusion(bf16[4,2,8,128,256]{4,3,2,1,0:T(8,128)(2,1)} %param.6, s32[]{:T(128)S(6)} %select_n.124), kind=kLoop, calls=%fused_computation.79 | loop fusion | bytes 2097156 | tf_op jit(solution)/shard_map/jit(dynamic_index_in_dim)/dynamic_slice | solution.py:34
  12.6 9.0 %all-to-all-start = ((bf16[32,64,256]{2,1,0:T(8,128)(2,1)}), bf16[32,64,256]{2,1,0:T(8,128)(2,1)S(1)}, u32[]{:S(2)}, u32[]{:S(2)}) async-start(bf16[32,64,256]{2,1,0:T(8,128)(2,1)} %bitcast), calls=%async_computation | async-start | bytes 2097152 | tf_op jit(solution)/shard_map/all_to_all | solution.py:38
  21.9 15.3 %all-to-all-done = bf16[32,64,256]{2,1,0:T(8,128)(2,1)S(1)} async-done(((bf16[32,64,256]{2,1,0:T(8,128)(2,1)}), bf16[32,64,256]{2,1,0:T(8,128)(2,1)S(1)}, u32[]{:S(2)}, u32[]{:S(2)}) %all-to-all-start) | async-done | bytes 1048608 | tf_op jit(solution)/shard_map/all_to_all | solution.py:38
  38.9 4.0 %collective-permute-done = bf16[4,64,256]{2,1,0:T(8,128)(2,1)S(1)} collective-permute-done((bf16[4,64,256]{2,1,0:T(8,128)(2,1)S(1)}, bf16[4,64,256]{2,1,0:T(8,128)(2,1)S(1)}, u32[]{:S(2)}, u32[]{:S(2)}) %collective-permute-start) | collective-permute-done | bytes 131104 | tf_op jit(solution)/shard_map/ppermute | solution.py:42
  45.8 2.6 %collective-permute-start.2 = (bf16[2,2,64,256]{3,2,0,1:T(8,128)(2,1)S(1)}, bf16[2,2,64,256]{3,2,0,1:T(8,128)(2,1)S(1)}, u32[]{:S(2)}, u32[]{:S(2)}) collective-permute-start(bf16[2,2,64,256]{3,2,0,1:T(8,128)(2,1)S(1)} %get-tuple-element.23), channel_id=1, source_target_pairs={{0,64},{64,128},{128,192},{192,0},{1,65},{65,129},{129,193},{193,1... | collective-permute-start | bytes 393224 | tf_op jit(solution)/shard_map/ppermute | solution.py:16
  48.4 2.3 %collective-permute-done.10 = bf16[2,2,64,256]{3,2,0,1:T(8,128)(2,1)S(1)} collective-permute-done((bf16[2,2,64,256]{3,2,0,1:T(8,128)(2,1)S(1)}, bf16[2,2,64,256]{3,2,0,1:T(8,128)(2,1)S(1)}, u32[]{:S(2)}, u32[]{:S(2)}) %collective-permute-start.10) | collective-permute-done | bytes 131104 | tf_op jit(solution)/shard_map/ppermute | solution.py:16
  50.9 3.2 %collective-permute-start.12 = (bf16[1,2,64,256]{3,2,0,1:T(8,128)(2,1)S(1)}, bf16[1,2,64,256]{3,2,0,1:T(8,128)(2,1)S(1)}, u32[]{:S(2)}, u32[]{:S(2)}) collective-permute-start(bf16[1,2,64,256]{3,2,0,1:T(8,128)(2,1)S(1)} %slice.81), channel_id=1, source_target_pairs={{0,48},{16,0},{32,16},{48,32},{1,49},{17,1},{33,17},{49,33},{2,50}... | collective-permute-start | bytes 196616 | tf_op jit(solution)/shard_map/ppermute | solution.py:20
  58.5 2.5 %collective-permute-done.4 = bf16[1,2,64,256]{3,2,0,1:T(8,128)(2,1)S(1)} collective-permute-done((bf16[1,2,64,256]{3,2,0,1:T(8,128)(2,1)S(1)}, bf16[1,2,64,256]{3,2,0,1:T(8,128)(2,1)S(1)}, u32[]{:S(2)}, u32[]{:S(2)}) %collective-permute-start.4) | collective-permute-done | bytes 65568 | tf_op jit(solution)/shard_map/ppermute | solution.py:20
  61.2 2.3 %collective-permute-start.5 = (bf16[4,2,2,64,256]{4,3,1,2,0:T(8,128)(2,1)S(1)}, bf16[4,2,2,64,256]{4,3,1,2,0:T(8,128)(2,1)S(1)}, u32[]{:S(2)}, u32[]{:S(2)}) collective-permute-start(bf16[4,2,2,64,256]{4,3,1,2,0:T(8,128)(2,1)S(1)} %get-tuple-element.10), channel_id=1, source_target_pairs={{0,48},{16,0},{32,16},{48,32},{1,49},{17,1},{33,17},{49,33},{2,50}... | collective-permute-start | bytes 1572872 | tf_op jit(solution)/shard_map/ppermute | solution.py:17
  65.8 10.9 %collective-permute-done.6 = bf16[4,2,2,64,256]{4,3,1,2,0:T(8,128)(2,1)S(1)} collective-permute-done((bf16[4,2,2,64,256]{4,3,1,2,0:T(8,128)(2,1)S(1)}, bf16[4,2,2,64,256]{4,3,1,2,0:T(8,128)(2,1)S(1)}, u32[]{:S(2)}, u32[]{:S(2)}) %collective-permute-start.6) | collective-permute-done | bytes 524320 | tf_op jit(solution)/shard_map/ppermute | solution.py:16
  77.1 3.3 %collective-permute-start.8 = (bf16[2,2,2,64,256]{4,3,1,2,0:T(8,128)(2,1)S(1)}, bf16[2,2,2,64,256]{4,3,1,2,0:T(8,128)(2,1)S(1)}, u32[]{:S(2)}, u32[]{:S(2)}) collective-permute-start(bf16[2,2,2,64,256]{4,3,1,2,0:T(8,128)(2,1)S(1)} %slice.78), channel_id=1, source_target_pairs={{0,48},{16,0},{32,16},{48,32},{1,49},{17,1},{33,17},{49,33},{2,50}... | collective-permute-start | bytes 786440 | tf_op jit(solution)/shard_map/ppermute | solution.py:20
  91.0 2.1 %copy-done = bf16[1,8,512,512]{3,2,0,1:T(8,128)(2,1)} copy-done((bf16[1,8,512,512]{3,2,0,1:T(8,128)(2,1)}, bf16[1,8,512,512]{3,2,0,1:T(8,128)(2,1)S(1)}, u32[]{:S(2)}) %copy-start) | copy-done | bytes 4194328
  94.4 3.5 %fusion.7 = f32[384,4,512]{2,0,1:T(8,128)} fusion(bf16[1,8,512,512]{3,2,0,1:T(8,128)(2,1)S(1)} %get-tuple-element.17, bf16[1,8,512,512]{3,2,0,1:T(8,128)(2,1)S(1)} %get-tuple-element.18, bf16[2,8,384,512]{3,2,1,0:T(8,128)(2,1)S(1)} %bitcast.134, bf16[384,512]{1,0:T(8,128)(2,1)S(1)} %convert_element_type.7), kind=kOutput, calls=%fused_computation.15 | convolution fusion | flops 1631584256 | bytes 18219008 | tf_op jit(solution)/shard_map/dot_general | solution.py:97
  98.0 5.0 %fusion = f32[4,384,512,1]{2,1,3,0:T(8,128)S(1)} fusion(bf16[2,8,384,512]{3,2,1,0:T(8,128)(2,1)} %param.4, bf16[1,8,512,512]{3,2,0,1:T(8,128)(2,1)} %copy-done.1, bf16[1,8,512,512]{3,2,0,1:T(8,128)(2,1)} %copy-done, bf16[384,512]{1,0:T(8,128)(2,1)S(1)} %convert_element_type.7), kind=kOutput, calls=%fused_computation.4 | convolution fusion | flops 1631584256 | bytes 18219008 | tf_op jit(solution)/shard_map/dot_general | solution.py:97
  103.6 3.5 %collective-permute-done.17 = f32[4,48,4,512]{3,1,2,0:T(8,128)} collective-permute-done((f32[4,48,4,512]{3,1,2,0:T(8,128)S(1)}, f32[4,48,4,512]{3,1,2,0:T(8,128)}, u32[]{:S(2)}, u32[]{:S(2)}) %collective-permute-start.17) | collective-permute-done | bytes 1572896 | tf_op jit(solution)/shard_map/ppermute | solution.py:67
  109.0 3.6 %collective-permute-start.18 = (f32[24,4,512]{2,0,1:T(8,128)S(1)}, f32[24,4,512]{2,0,1:T(8,128)S(1)}, u32[]{:S(2)}, u32[]{:S(2)}) collective-permute-start(f32[24,4,512]{2,0,1:T(8,128)S(1)} %dynamic-slice_bitcast_fusion.2), channel_id=1, source_target_pairs={{0,2},{2,4},{4,6},{6,0},{1,3},{3,5},{5,7},{7,1},{8,10},{10,12},{12... | collective-permute-start | bytes 589832 | tf_op jit(solution)/shard_map/ppermute | solution.py:80
  112.6 2.2 %collective-permute-start.21 = (f32[24,4,512]{2,0,1:T(8,128)S(1)}, f32[24,4,512]{2,0,1:T(8,128)S(1)}, u32[]{:S(2)}, u32[]{:S(2)}) collective-permute-start(f32[24,4,512]{2,0,1:T(8,128)S(1)} %dynamic-slice_bitcast_fusion.1), channel_id=1, source_target_pairs={{0,6},{2,0},{4,2},{6,4},{1,7},{3,1},{5,3},{7,5},{8,14},{10,8},{12,... | collective-permute-start | bytes 589832 | tf_op jit(solution)/shard_map/ppermute | solution.py:81
  114.8 16.1 %collective-permute-done.18 = f32[24,4,512]{2,0,1:T(8,128)S(1)} collective-permute-done((f32[24,4,512]{2,0,1:T(8,128)S(1)}, f32[24,4,512]{2,0,1:T(8,128)S(1)}, u32[]{:S(2)}, u32[]{:S(2)}) %collective-permute-start.18) | collective-permute-done | bytes 196640 | tf_op jit(solution)/shard_map/ppermute | solution.py:80
  131.0 4.2 %collective-permute-start.22 = (f32[24,4,512]{2,0,1:T(8,128)S(1)}, f32[24,4,512]{2,0,1:T(8,128)S(1)}, u32[]{:S(2)}, u32[]{:S(2)}) collective-permute-start(f32[24,4,512]{2,0,1:T(8,128)S(1)} %bitcast_add_fusion.3), channel_id=1, source_target_pairs={{0,6},{2,0},{4,2},{6,4},{1,7},{3,1},{5,3},{7,5},{8,14},{10,8},{12,... | collective-permute-start | bytes 589832 | tf_op jit(solution)/shard_map/ppermute | solution.py:81
  135.2 11.6 %collective-permute-done.19 = f32[24,4,512]{2,0,1:T(8,128)S(1)} collective-permute-done((f32[24,4,512]{2,0,1:T(8,128)S(1)}, f32[24,4,512]{2,0,1:T(8,128)S(1)}, u32[]{:S(2)}, u32[]{:S(2)}) %collective-permute-start.19) | collective-permute-done | bytes 196640 | tf_op jit(solution)/shard_map/ppermute | solution.py:80
  147.0 4.2 %collective-permute-start.23 = (f32[24,4,512]{2,0,1:T(8,128)S(1)}, f32[24,4,512]{2,0,1:T(8,128)S(1)}, u32[]{:S(2)}, u32[]{:S(2)}) collective-permute-start(f32[24,4,512]{2,0,1:T(8,128)S(1)} %bitcast_add_fusion.2), channel_id=1, source_target_pairs={{0,6},{2,0},{4,2},{6,4},{1,7},{3,1},{5,3},{7,5},{8,14},{10,8},{12,... | collective-permute-start | bytes 589832 | tf_op jit(solution)/shard_map/ppermute | solution.py:81
  151.2 9.5 %collective-permute-done.20 = f32[24,4,512]{2,0,1:T(8,128)S(1)} collective-permute-done((f32[24,4,512]{2,0,1:T(8,128)S(1)}, f32[24,4,512]{2,0,1:T(8,128)S(1)}, u32[]{:S(2)}, u32[]{:S(2)}) %collective-permute-start.20) | collective-permute-done | bytes 196640 | tf_op jit(solution)/shard_map/ppermute | solution.py:80
  160.8 4.8 %collective-permute-done.23 = f32[24,4,512]{2,0,1:T(8,128)S(1)} collective-permute-done((f32[24,4,512]{2,0,1:T(8,128)S(1)}, f32[24,4,512]{2,0,1:T(8,128)S(1)}, u32[]{:S(2)}, u32[]{:S(2)}) %collective-permute-start.23) | collective-permute-done | bytes 196640 | tf_op jit(solution)/shard_map/ppermute | solution.py:81
  165.6 4.9 %reduce-scatter.2.cloned.1.call-done = f32[48,4,512]{2,0,1:T(8,128)} async-done(((f32[384,4,512]{2,0,1:T(8,128)}), f32[48,4,512]{2,0,1:T(8,128)}) %reduce-scatter.2.cloned.1.call-update) | async-done | bytes 393232 | tf_op jit(solution)/shard_map/reduce_scatter | solution.py:102
  (113 shorter events, 30.5 us)
Async XLA Ops:
  12.6 24.6 %all-to-all-start = ((bf16[32,64,256]{2,1,0:T(8,128)(2,1)}), bf16[32,64,256]{2,1,0:T(8,128)(2,1)S(1)}, u32[]{:S(2)}, u32[]{:S(2)}) async-start(bf16[32,64,256]{2,1,0:T(8,128)(2,1)} %bitcast), calls=%async_computation | async-start | bytes 2097152 | tf_op jit(solution)/shard_map/all_to_all | solution.py:38
  21.6 148.9 %reduce-scatter.2.cloned.1.call-start = ((), (), s32[]{:S(2)}) async-start(), calls=%async_computation.2 | async-start | bytes 3538944 | tf_op jit(solution)/shard_map/reduce_scatter | solution.py:102
  37.9 5.1 %collective-permute-start = (bf16[4,64,256]{2,1,0:T(8,128)(2,1)S(1)}, bf16[4,64,256]{2,1,0:T(8,128)(2,1)S(1)}, u32[]{:S(2)}, u32[]{:S(2)}) collective-permute-start(bf16[4,64,256]{2,1,0:T(8,128)(2,1)S(1)} %broadcast_select_fusion), channel_id=1, source_target_pairs={{0,8},{8,0},{1,9},{9,1},{2,10},{10,2},{3,11},{11,3},{4,12},{12,4},... | collective-permute-start | bytes 393224 | tf_op jit(solution)/shard_map/ppermute | solution.py:42
  43.1 7.8 %collective-permute-start.9 = (bf16[2,2,64,256]{3,2,0,1:T(8,128)(2,1)S(1)}, bf16[2,2,64,256]{3,2,0,1:T(8,128)(2,1)S(1)}, u32[]{:S(2)}, u32[]{:S(2)}) collective-permute-start(bf16[2,2,64,256]{3,2,0,1:T(8,128)(2,1)S(1)} %get-tuple-element.24), channel_id=1, source_target_pairs={{0,48},{16,0},{32,16},{48,32},{1,49},{17,1},{33,17},{49,33},{2,50}... | collective-permute-start | bytes 393224 | tf_op jit(solution)/shard_map/ppermute | solution.py:17
  44.3 6.5 %collective-permute-start.10 = (bf16[2,2,64,256]{3,2,0,1:T(8,128)(2,1)S(1)}, bf16[2,2,64,256]{3,2,0,1:T(8,128)(2,1)S(1)}, u32[]{:S(2)}, u32[]{:S(2)}) collective-permute-start(bf16[2,2,64,256]{3,2,0,1:T(8,128)(2,1)S(1)} %get-tuple-element.24), channel_id=1, source_target_pairs={{0,16},{16,32},{32,48},{48,0},{1,17},{17,33},{33,49},{49,1},{2,18}... | collective-permute-start | bytes 393224 | tf_op jit(solution)/shard_map/ppermute | solution.py:16
  45.2 10.3 %collective-permute-start.1 = (bf16[2,2,64,256]{3,2,0,1:T(8,128)(2,1)S(1)}, bf16[2,2,64,256]{3,2,0,1:T(8,128)(2,1)S(1)}, u32[]{:S(2)}, u32[]{:S(2)}) collective-permute-start(bf16[2,2,64,256]{3,2,0,1:T(8,128)(2,1)S(1)} %get-tuple-element.23), channel_id=1, source_target_pairs={{0,192},{64,0},{128,64},{192,128},{1,193},{65,1},{129,65},{193,129... | collective-permute-start | bytes 393224 | tf_op jit(solution)/shard_map/ppermute | solution.py:17
  45.8 8.4 %collective-permute-start.2 = (bf16[2,2,64,256]{3,2,0,1:T(8,128)(2,1)S(1)}, bf16[2,2,64,256]{3,2,0,1:T(8,128)(2,1)S(1)}, u32[]{:S(2)}, u32[]{:S(2)}) collective-permute-start(bf16[2,2,64,256]{3,2,0,1:T(8,128)(2,1)S(1)} %get-tuple-element.23), channel_id=1, source_target_pairs={{0,64},{64,128},{128,192},{192,0},{1,65},{65,129},{129,193},{193,1... | collective-permute-start | bytes 393224 | tf_op jit(solution)/shard_map/ppermute | solution.py:16
  50.8 5.6 %collective-permute-start.11 = (bf16[1,2,64,256]{3,2,0,1:T(8,128)(2,1)S(1)}, bf16[1,2,64,256]{3,2,0,1:T(8,128)(2,1)S(1)}, u32[]{:S(2)}, u32[]{:S(2)}) collective-permute-start(bf16[1,2,64,256]{3,2,0,1:T(8,128)(2,1)S(1)} %slice.80), channel_id=1, source_target_pairs={{0,16},{16,32},{32,48},{48,0},{1,17},{17,33},{33,49},{49,1},{2,18}... | collective-permute-start | bytes 196616 | tf_op jit(solution)/shard_map/ppermute | solution.py:20
  50.9 5.5 %collective-permute-start.12 = (bf16[1,2,64,256]{3,2,0,1:T(8,128)(2,1)S(1)}, bf16[1,2,64,256]{3,2,0,1:T(8,128)(2,1)S(1)}, u32[]{:S(2)}, u32[]{:S(2)}) collective-permute-start(bf16[1,2,64,256]{3,2,0,1:T(8,128)(2,1)S(1)} %slice.81), channel_id=1, source_target_pairs={{0,48},{16,0},{32,16},{48,32},{1,49},{17,1},{33,17},{49,33},{2,50}... | collective-permute-start | bytes 196616 | tf_op jit(solution)/shard_map/ppermute | solution.py:20
  55.5 5.6 %collective-permute-start.4 = (bf16[1,2,64,256]{3,2,0,1:T(8,128)(2,1)S(1)}, bf16[1,2,64,256]{3,2,0,1:T(8,128)(2,1)S(1)}, u32[]{:S(2)}, u32[]{:S(2)}) collective-permute-start(bf16[1,2,64,256]{3,2,0,1:T(8,128)(2,1)S(1)} %slice.76), channel_id=1, source_target_pairs={{0,192},{64,0},{128,64},{192,128},{1,193},{65,1},{129,65},{193,129... | collective-permute-start | bytes 196616 | tf_op jit(solution)/shard_map/ppermute | solution.py:20
  61.2 15.8 %collective-permute-start.5 = (bf16[4,2,2,64,256]{4,3,1,2,0:T(8,128)(2,1)S(1)}, bf16[4,2,2,64,256]{4,3,1,2,0:T(8,128)(2,1)S(1)}, u32[]{:S(2)}, u32[]{:S(2)}) collective-permute-start(bf16[4,2,2,64,256]{4,3,1,2,0:T(8,128)(2,1)S(1)} %get-tuple-element.10), channel_id=1, source_target_pairs={{0,48},{16,0},{32,16},{48,32},{1,49},{17,1},{33,17},{49,33},{2,50}... | collective-permute-start | bytes 1572872 | tf_op jit(solution)/shard_map/ppermute | solution.py:17
  63.5 13.2 %collective-permute-start.6 = (bf16[4,2,2,64,256]{4,3,1,2,0:T(8,128)(2,1)S(1)}, bf16[4,2,2,64,256]{4,3,1,2,0:T(8,128)(2,1)S(1)}, u32[]{:S(2)}, u32[]{:S(2)}) collective-permute-start(bf16[4,2,2,64,256]{4,3,1,2,0:T(8,128)(2,1)S(1)} %get-tuple-element.10), channel_id=1, source_target_pairs={{0,16},{16,32},{32,48},{48,0},{1,17},{17,33},{33,49},{49,1},{2,18}... | collective-permute-start | bytes 1572872 | tf_op jit(solution)/shard_map/ppermute | solution.py:16
  63.7 16.7 %collective-permute-start.14 = (bf16[4,2,2,64,256]{4,3,1,2,0:T(8,128)(2,1)S(1)}, bf16[4,2,2,64,256]{4,3,1,2,0:T(8,128)(2,1)S(1)}, u32[]{:S(2)}, u32[]{:S(2)}) collective-permute-start(bf16[4,2,2,64,256]{4,3,1,2,0:T(8,128)(2,1)S(1)} %get-tuple-element.12), channel_id=1, source_target_pairs={{0,64},{64,128},{128,192},{192,0},{1,65},{65,129},{129,193},{193,1... | collective-permute-start | bytes 1572872 | tf_op jit(solution)/shard_map/ppermute | solution.py:16
  63.8 16.7 %collective-permute-start.13 = (bf16[4,2,2,64,256]{4,3,1,2,0:T(8,128)(2,1)S(1)}, bf16[4,2,2,64,256]{4,3,1,2,0:T(8,128)(2,1)S(1)}, u32[]{:S(2)}, u32[]{:S(2)}) collective-permute-start(bf16[4,2,2,64,256]{4,3,1,2,0:T(8,128)(2,1)S(1)} %get-tuple-element.12), channel_id=1, source_target_pairs={{0,192},{64,0},{128,64},{192,128},{1,193},{65,1},{129,65},{193,129... | collective-permute-start | bytes 1572872 | tf_op jit(solution)/shard_map/ppermute | solution.py:17
  76.8 7.8 %collective-permute-start.7 = (bf16[2,2,2,64,256]{4,3,1,2,0:T(8,128)(2,1)S(1)}, bf16[2,2,2,64,256]{4,3,1,2,0:T(8,128)(2,1)S(1)}, u32[]{:S(2)}, u32[]{:S(2)}) collective-permute-start(bf16[2,2,2,64,256]{4,3,1,2,0:T(8,128)(2,1)S(1)} %slice.77), channel_id=1, source_target_pairs={{0,16},{16,32},{32,48},{48,0},{1,17},{17,33},{33,49},{49,1},{2,18}... | collective-permute-start | bytes 786440 | tf_op jit(solution)/shard_map/ppermute | solution.py:20
  77.1 7.5 %collective-permute-start.8 = (bf16[2,2,2,64,256]{4,3,1,2,0:T(8,128)(2,1)S(1)}, bf16[2,2,2,64,256]{4,3,1,2,0:T(8,128)(2,1)S(1)}, u32[]{:S(2)}, u32[]{:S(2)}) collective-permute-start(bf16[2,2,2,64,256]{4,3,1,2,0:T(8,128)(2,1)S(1)} %slice.78), channel_id=1, source_target_pairs={{0,48},{16,0},{32,16},{48,32},{1,49},{17,1},{33,17},{49,33},{2,50}... | collective-permute-start | bytes 786440 | tf_op jit(solution)/shard_map/ppermute | solution.py:20
  80.4 6.4 %collective-permute-start.15 = (bf16[2,2,2,64,256]{4,3,1,2,0:T(8,128)(2,1)S(1)}, bf16[2,2,2,64,256]{4,3,1,2,0:T(8,128)(2,1)S(1)}, u32[]{:S(2)}, u32[]{:S(2)}) collective-permute-start(bf16[2,2,2,64,256]{4,3,1,2,0:T(8,128)(2,1)S(1)} %slice.82), channel_id=1, source_target_pairs={{0,64},{64,128},{128,192},{192,0},{1,65},{65,129},{129,193},{193,1... | collective-permute-start | bytes 786440 | tf_op jit(solution)/shard_map/ppermute | solution.py:20
  80.5 7.7 %collective-permute-start.16 = (bf16[2,2,2,64,256]{4,3,1,2,0:T(8,128)(2,1)S(1)}, bf16[2,2,2,64,256]{4,3,1,2,0:T(8,128)(2,1)S(1)}, u32[]{:S(2)}, u32[]{:S(2)}) collective-permute-start(bf16[2,2,2,64,256]{4,3,1,2,0:T(8,128)(2,1)S(1)} %slice.83), channel_id=1, source_target_pairs={{0,192},{64,0},{128,64},{192,128},{1,193},{65,1},{129,65},{193,129... | collective-permute-start | bytes 786440 | tf_op jit(solution)/shard_map/ppermute | solution.py:20
  109.0 21.9 %collective-permute-start.18 = (f32[24,4,512]{2,0,1:T(8,128)S(1)}, f32[24,4,512]{2,0,1:T(8,128)S(1)}, u32[]{:S(2)}, u32[]{:S(2)}) collective-permute-start(f32[24,4,512]{2,0,1:T(8,128)S(1)} %dynamic-slice_bitcast_fusion.2), channel_id=1, source_target_pairs={{0,2},{2,4},{4,6},{6,0},{1,3},{3,5},{5,7},{7,1},{8,10},{10,12},{12... | collective-permute-start | bytes 589832 | tf_op jit(solution)/shard_map/ppermute | solution.py:80
  112.6 18.4 %collective-permute-start.21 = (f32[24,4,512]{2,0,1:T(8,128)S(1)}, f32[24,4,512]{2,0,1:T(8,128)S(1)}, u32[]{:S(2)}, u32[]{:S(2)}) collective-permute-start(f32[24,4,512]{2,0,1:T(8,128)S(1)} %dynamic-slice_bitcast_fusion.1), channel_id=1, source_target_pairs={{0,6},{2,0},{4,2},{6,4},{1,7},{3,1},{5,3},{7,5},{8,14},{10,8},{12,... | collective-permute-start | bytes 589832 | tf_op jit(solution)/shard_map/ppermute | solution.py:81
  130.9 15.9 %collective-permute-start.19 = (f32[24,4,512]{2,0,1:T(8,128)S(1)}, f32[24,4,512]{2,0,1:T(8,128)S(1)}, u32[]{:S(2)}, u32[]{:S(2)}) collective-permute-start(f32[24,4,512]{2,0,1:T(8,128)S(1)} %bitcast_add_fusion.6), channel_id=1, source_target_pairs={{0,2},{2,4},{4,6},{6,0},{1,3},{3,5},{5,7},{7,1},{8,10},{10,12},{12... | collective-permute-start | bytes 589832 | tf_op jit(solution)/shard_map/ppermute | solution.py:80
  131.0 15.9 %collective-permute-start.22 = (f32[24,4,512]{2,0,1:T(8,128)S(1)}, f32[24,4,512]{2,0,1:T(8,128)S(1)}, u32[]{:S(2)}, u32[]{:S(2)}) collective-permute-start(f32[24,4,512]{2,0,1:T(8,128)S(1)} %bitcast_add_fusion.3), channel_id=1, source_target_pairs={{0,6},{2,0},{4,2},{6,4},{1,7},{3,1},{5,3},{7,5},{8,14},{10,8},{12,... | collective-permute-start | bytes 589832 | tf_op jit(solution)/shard_map/ppermute | solution.py:81
  146.9 13.9 %collective-permute-start.20 = (f32[24,4,512]{2,0,1:T(8,128)S(1)}, f32[24,4,512]{2,0,1:T(8,128)S(1)}, u32[]{:S(2)}, u32[]{:S(2)}) collective-permute-start(f32[24,4,512]{2,0,1:T(8,128)S(1)} %bitcast_add_fusion.5), channel_id=1, source_target_pairs={{0,2},{2,4},{4,6},{6,0},{1,3},{3,5},{5,7},{7,1},{8,10},{10,12},{12... | collective-permute-start | bytes 589832 | tf_op jit(solution)/shard_map/ppermute | solution.py:80
  147.0 18.6 %collective-permute-start.23 = (f32[24,4,512]{2,0,1:T(8,128)S(1)}, f32[24,4,512]{2,0,1:T(8,128)S(1)}, u32[]{:S(2)}, u32[]{:S(2)}) collective-permute-start(f32[24,4,512]{2,0,1:T(8,128)S(1)} %bitcast_add_fusion.2), channel_id=1, source_target_pairs={{0,6},{2,0},{4,2},{6,4},{1,7},{3,1},{5,3},{7,5},{8,14},{10,8},{12,... | collective-permute-start | bytes 589832 | tf_op jit(solution)/shard_map/ppermute | solution.py:81
  (8 other events, 60.3 us)
Sparse Core Ops, SparseCore 0:
  98.1 72.3 reduce-scatter.1

commit v12 on v11

--- a/solution.py
+++ b/solution.py
@@ -91,7 +91,7 @@
     weights = jnp.stack(
         [jnp.concatenate([real_in, imag_in], axis=-1), jnp.concatenate([-imag_in, real_in], axis=-1)], axis=0
     )
-    half = freq // 2
+    half = (3 * freq) // 8
 
     def product(lo, hi):
         out = lax.dot_general(

time: 181 us -> 188 us (1.039)
  local copies, waits for them, and re-layouts: 9.83 us -> 21.1 us
  waiting for transfers between devices: 93 us -> 84.8 us
  other arithmetic: 6.93 us -> 10.7 us
    unnamed x29 -> x30, local copies, waits for them, and re-layouts: 4.01 us -> 12.8 us
    ppermute x3, waiting for transfers between devices: 37.2 us -> 42.3 us  [reduce_rows(): got_lo = lax.ppermute(acc_lo, 'zh', fwd)]
    reduce_scatter x1, waiting for transfers between devices: 4.89 us -> 0.02 us  [body(): lax.psum_scatter(product(0, half), SP, scatter_dimension=0, tiled=True)]
    ppermute x4, waiting for transfers between devices: 6.07 us -> 2.4 us  [ring_gather(): lax.ppermute(from_left[:half], axis, fwd)]
    ppermute x3, waiting for transfers between devices: 4.79 us -> 1.41 us  [reduce_rows(): got_hi = lax.ppermute(acc_hi, 'zh', bwd)]
    unnamed x9, other arithmetic: 0.2 us -> 2.57 us
    ppermute x4, waiting for transfers between devices: 13.3 us -> 11.4 us  [ring_gather(): from_left = lax.ppermute(piece, axis, fwd)]
  transfers between devices with their start and end apart: 26 -> 26, of which waited for: 15 -> 13; matrix products, arithmetic and copies ran while one was open for 5% -> 9% of each run, Pallas kernels for 0% -> 0%
where the time goes in v12:
time: 188 us; the launch traced here: 187 us
  waiting for transfers between devices  84.8 us (45%)
  starting transfers between devices  45.3 us (24%)
  local copies, waits for them, and re-layouts  21.1 us (11%)
  between operations  16 us (9%)
  other arithmetic  10.7 us (6%)
  matrix products  8.83 us (5%)
    ppermute x3, waiting for transfers between devices, reduce_rows(): got_lo = lax.ppermute(acc_lo, 'zh', fwd)  42.3 us
    all_to_all x1, waiting for transfers between devices, gather_receivers(): got = lax.all_to_all(pieces, SHOT, 0, 0, tiled=True)  15.3 us
    unnamed x30, local copies, waits for them, and re-layouts  12.8 us
    ppermute x4, waiting for transfers between devices, ring_gather(): from_left = lax.ppermute(piece, axis, fwd)  11.4 us
    ppermute x3, starting transfers between devices, reduce_rows(): got_hi = lax.ppermute(acc_hi, 'zh', bwd)  10.8 us
    ppermute x4, starting transfers between devices, ring_gather(): lax.ppermute(from_right[half:], axis, bwd)  9.49 us
    all_to_all x1, starting transfers between devices, gather_receivers(): got = lax.all_to_all(pieces, SHOT, 0, 0, tiled=True)  8.96 us
    dot_general x2, matrix products, product(): lax.dot_general(live[:, lo:hi], weights[:, lo:hi], (((0, 3), (0, 2)), ((1...  8.83 us
  transfers between devices with their start and end apart: 26, of which 13 were waited for; matrix products, arithmetic and copies ran while one was open for 9% of the time, Pallas kernels for 0%

profile of v12, /device:TPU:6, one launch (start us, length us, event | category | flops | bytes accessed | tf_op | source)
XLA Modules:
  0.0 186.6 jit_solution(3780461138825672523)
XLA Ops:
  10.3 2.3 %constant_dynamic-slice_fusion.5 = bf16[1,2,8,128,256]{4,3,2,1,0:T(8,128)(2,1)} fusion(bf16[4,2,8,128,256]{4,3,2,1,0:T(8,128)(2,1)} %param.6, s32[]{:T(128)S(6)} %select_n.124), kind=kLoop, calls=%fused_computation.79 | loop fusion | bytes 2097156 | tf_op jit(solution)/shard_map/jit(dynamic_index_in_dim)/dynamic_slice | solution.py:34
  12.6 9.0 %all-to-all-start = ((bf16[32,64,256]{2,1,0:T(8,128)(2,1)}), bf16[32,64,256]{2,1,0:T(8,128)(2,1)S(1)}, u32[]{:S(2)}, u32[]{:S(2)}) async-start(bf16[32,64,256]{2,1,0:T(8,128)(2,1)} %bitcast), calls=%async_computation | async-start | bytes 2097152 | tf_op jit(solution)/shard_map/all_to_all | solution.py:38
  21.9 15.3 %all-to-all-done = bf16[32,64,256]{2,1,0:T(8,128)(2,1)S(1)} async-done(((bf16[32,64,256]{2,1,0:T(8,128)(2,1)}), bf16[32,64,256]{2,1,0:T(8,128)(2,1)S(1)}, u32[]{:S(2)}, u32[]{:S(2)}) %all-to-all-start) | async-done | bytes 1048608 | tf_op jit(solution)/shard_map/all_to_all | solution.py:38
  38.9 4.0 %collective-permute-done = bf16[4,64,256]{2,1,0:T(8,128)(2,1)S(1)} collective-permute-done((bf16[4,64,256]{2,1,0:T(8,128)(2,1)S(1)}, bf16[4,64,256]{2,1,0:T(8,128)(2,1)S(1)}, u32[]{:S(2)}, u32[]{:S(2)}) %collective-permute-start) | collective-permute-done | bytes 131104 | tf_op jit(solution)/shard_map/ppermute | solution.py:42
  45.8 2.6 %collective-permute-start.2 = (bf16[2,2,64,256]{3,2,0,1:T(8,128)(2,1)S(1)}, bf16[2,2,64,256]{3,2,0,1:T(8,128)(2,1)S(1)}, u32[]{:S(2)}, u32[]{:S(2)}) collective-permute-start(bf16[2,2,64,256]{3,2,0,1:T(8,128)(2,1)S(1)} %get-tuple-element.23), channel_id=1, source_target_pairs={{0,64},{64,128},{128,192},{192,0},{1,65},{65,129},{129,193},{193,1... | collective-permute-start | bytes 393224 | tf_op jit(solution)/shard_map/ppermute | solution.py:16
  48.4 2.3 %collective-permute-done.10 = bf16[2,2,64,256]{3,2,0,1:T(8,128)(2,1)S(1)} collective-permute-done((bf16[2,2,64,256]{3,2,0,1:T(8,128)(2,1)S(1)}, bf16[2,2,64,256]{3,2,0,1:T(8,128)(2,1)S(1)}, u32[]{:S(2)}, u32[]{:S(2)}) %collective-permute-start.10) | collective-permute-done | bytes 131104 | tf_op jit(solution)/shard_map/ppermute | solution.py:16
  50.9 3.2 %collective-permute-start.12 = (bf16[1,2,64,256]{3,2,0,1:T(8,128)(2,1)S(1)}, bf16[1,2,64,256]{3,2,0,1:T(8,128)(2,1)S(1)}, u32[]{:S(2)}, u32[]{:S(2)}) collective-permute-start(bf16[1,2,64,256]{3,2,0,1:T(8,128)(2,1)S(1)} %slice.81), channel_id=1, source_target_pairs={{0,48},{16,0},{32,16},{48,32},{1,49},{17,1},{33,17},{49,33},{2,50}... | collective-permute-start | bytes 196616 | tf_op jit(solution)/shard_map/ppermute | solution.py:20
  56.4 2.1 %collective-permute-done.3 = bf16[1,2,64,256]{3,2,0,1:T(8,128)(2,1)S(1)} collective-permute-done((bf16[1,2,64,256]{3,2,0,1:T(8,128)(2,1)S(1)}, bf16[1,2,64,256]{3,2,0,1:T(8,128)(2,1)S(1)}, u32[]{:S(2)}, u32[]{:S(2)}) %collective-permute-start.3) | collective-permute-done | bytes 65568 | tf_op jit(solution)/shard_map/ppermute | solution.py:20
  58.5 2.5 %collective-permute-done.4 = bf16[1,2,64,256]{3,2,0,1:T(8,128)(2,1)S(1)} collective-permute-done((bf16[1,2,64,256]{3,2,0,1:T(8,128)(2,1)S(1)}, bf16[1,2,64,256]{3,2,0,1:T(8,128)(2,1)S(1)}, u32[]{:S(2)}, u32[]{:S(2)}) %collective-permute-start.4) | collective-permute-done | bytes 65568 | tf_op jit(solution)/shard_map/ppermute | solution.py:20
  62.1 2.2 %collective-permute-start.5 = (bf16[4,2,2,64,256]{4,3,1,2,0:T(8,128)(2,1)S(1)}, bf16[4,2,2,64,256]{4,3,1,2,0:T(8,128)(2,1)S(1)}, u32[]{:S(2)}, u32[]{:S(2)}) collective-permute-start(bf16[4,2,2,64,256]{4,3,1,2,0:T(8,128)(2,1)S(1)} %get-tuple-element.10), channel_id=1, source_target_pairs={{0,48},{16,0},{32,16},{48,32},{1,49},{17,1},{33,17},{49,33},{2,50}... | collective-permute-start | bytes 1572872 | tf_op jit(solution)/shard_map/ppermute | solution.py:17
  68.5 9.0 %collective-permute-done.6 = bf16[4,2,2,64,256]{4,3,1,2,0:T(8,128)(2,1)S(1)} collective-permute-done((bf16[4,2,2,64,256]{4,3,1,2,0:T(8,128)(2,1)S(1)}, bf16[4,2,2,64,256]{4,3,1,2,0:T(8,128)(2,1)S(1)}, u32[]{:S(2)}, u32[]{:S(2)}) %collective-permute-start.6) | collective-permute-done | bytes 524320 | tf_op jit(solution)/shard_map/ppermute | solution.py:16
  77.8 3.3 %collective-permute-start.8 = (bf16[2,2,2,64,256]{4,3,1,2,0:T(8,128)(2,1)S(1)}, bf16[2,2,2,64,256]{4,3,1,2,0:T(8,128)(2,1)S(1)}, u32[]{:S(2)}, u32[]{:S(2)}) collective-permute-start(bf16[2,2,2,64,256]{4,3,1,2,0:T(8,128)(2,1)S(1)} %slice.78), channel_id=1, source_target_pairs={{0,48},{16,0},{32,16},{48,32},{1,49},{17,1},{33,17},{49,33},{2,50}... | collective-permute-start | bytes 786440 | tf_op jit(solution)/shard_map/ppermute | solution.py:20
  81.3 2.1 %collective-permute-start.16 = (bf16[2,2,2,64,256]{4,3,1,2,0:T(8,128)(2,1)S(1)}, bf16[2,2,2,64,256]{4,3,1,2,0:T(8,128)(2,1)S(1)}, u32[]{:S(2)}, u32[]{:S(2)}) collective-permute-start(bf16[2,2,2,64,256]{4,3,1,2,0:T(8,128)(2,1)S(1)} %slice.83), channel_id=1, source_target_pairs={{0,192},{64,0},{128,64},{192,128},{1,193},{65,1},{129,65},{193,129... | collective-permute-start | bytes 786440 | tf_op jit(solution)/shard_map/ppermute | solution.py:20
  98.0 2.1 %copy-done = bf16[1,8,512,512]{3,2,0,1:T(8,128)(2,1)} copy-done((bf16[1,8,512,512]{3,2,0,1:T(8,128)(2,1)}, bf16[1,8,512,512]{3,2,0,1:T(8,128)(2,1)S(1)}, u32[]{:S(2)}) %copy-start) | copy-done | bytes 4194328
  101.5 2.9 %fusion.9 = f32[384,3,512]{2,0,1:T(8,128)} fusion(bf16[1,8,512,512]{3,2,0,1:T(8,128)(2,1)S(1)} %get-tuple-element.18, bf16[1,8,512,512]{3,2,0,1:T(8,128)(2,1)S(1)} %get-tuple-element.17, bf16[2,8,384,512]{3,2,1,0:T(8,128)(2,1)S(1)} %bitcast.135, bf16[384,512]{1,0:T(8,128)(2,1)S(1)} %convert_element_type.7), kind=kOutput, calls=%fused_computation.18 | convolution fusion | flops 1226833920 | bytes 17432576 | tf_op jit(solution)/shard_map/dot_general | solution.py:97
  104.4 5.9 %fusion = f32[5,384,512,1]{2,1,3,0:T(8,128)S(1)} fusion(bf16[1,8,512,512]{3,2,0,1:T(8,128)(2,1)} %copy-done.1, bf16[1,8,512,512]{3,2,0,1:T(8,128)(2,1)} %copy-done, bf16[2,8,384,512]{3,2,1,0:T(8,128)(2,1)} %param.4, bf16[384,512]{1,0:T(8,128)(2,1)S(1)} %convert_element_type.7), kind=kOutput, calls=%fused_computation.3 | convolution fusion | flops 2036334592 | bytes 19005440 | tf_op jit(solution)/shard_map/dot_general | solution.py:97
  112.4 4.3 %collective-permute-done.17 = f32[4,48,5,512]{3,1,2,0:T(8,128)} collective-permute-done((f32[4,48,5,512]{3,1,2,0:T(8,128)}, f32[4,48,5,512]{3,1,2,0:T(8,128)}, u32[]{:S(2)}, u32[]{:S(2)}) %collective-permute-start.17) | collective-permute-done | bytes 1966112 | tf_op jit(solution)/shard_map/ppermute | solution.py:67
  118.9 3.5 %collective-permute-start.18 = (f32[24,5,512]{2,0,1:T(8,128)S(1)}, f32[24,5,512]{2,0,1:T(8,128)S(1)}, u32[]{:S(2)}, u32[]{:S(2)}) collective-permute-start(f32[24,5,512]{2,0,1:T(8,128)S(1)} %dynamic-slice_bitcast_fusion.2), channel_id=1, source_target_pairs={{0,2},{2,4},{4,6},{6,0},{1,3},{3,5},{5,7},{7,1},{8,10},{10,12},{12... | collective-permute-start | bytes 737288 | tf_op jit(solution)/shard_map/ppermute | solution.py:80
  122.5 2.2 %collective-permute-start.21 = (f32[24,5,512]{2,0,1:T(8,128)S(1)}, f32[24,5,512]{2,0,1:T(8,128)S(1)}, u32[]{:S(2)}, u32[]{:S(2)}) collective-permute-start(f32[24,5,512]{2,0,1:T(8,128)S(1)} %dynamic-slice_bitcast_fusion.1), channel_id=1, source_target_pairs={{0,6},{2,0},{4,2},{6,4},{1,7},{3,1},{5,3},{7,5},{8,14},{10,8},{12,... | collective-permute-start | bytes 737288 | tf_op jit(solution)/shard_map/ppermute | solution.py:81
  124.7 20.6 %collective-permute-done.18 = f32[24,5,512]{2,0,1:T(8,128)S(1)} collective-permute-done((f32[24,5,512]{2,0,1:T(8,128)S(1)}, f32[24,5,512]{2,0,1:T(8,128)S(1)}, u32[]{:S(2)}, u32[]{:S(2)}) %collective-permute-start.18) | collective-permute-done | bytes 245792 | tf_op jit(solution)/shard_map/ppermute | solution.py:80
  145.5 4.4 %collective-permute-start.22 = (f32[24,5,512]{2,0,1:T(8,128)S(1)}, f32[24,5,512]{2,0,1:T(8,128)S(1)}, u32[]{:S(2)}, u32[]{:S(2)}) collective-permute-start(f32[24,5,512]{2,0,1:T(8,128)S(1)} %bitcast_add_fusion.2), channel_id=1, source_target_pairs={{0,6},{2,0},{4,2},{6,4},{1,7},{3,1},{5,3},{7,5},{8,14},{10,8},{12,... | collective-permute-start | bytes 737288 | tf_op jit(solution)/shard_map/ppermute | solution.py:81
  149.9 15.5 %collective-permute-done.19 = f32[24,5,512]{2,0,1:T(8,128)S(1)} collective-permute-done((f32[24,5,512]{2,0,1:T(8,128)S(1)}, f32[24,5,512]{2,0,1:T(8,128)S(1)}, u32[]{:S(2)}, u32[]{:S(2)}) %collective-permute-start.19) | collective-permute-done | bytes 245792 | tf_op jit(solution)/shard_map/ppermute | solution.py:80
  165.6 4.2 %collective-permute-start.23 = (f32[24,5,512]{2,0,1:T(8,128)S(1)}, f32[24,5,512]{2,0,1:T(8,128)S(1)}, u32[]{:S(2)}, u32[]{:S(2)}) collective-permute-start(f32[24,5,512]{2,0,1:T(8,128)S(1)} %bitcast_add_fusion.1), channel_id=1, source_target_pairs={{0,6},{2,0},{4,2},{6,4},{1,7},{3,1},{5,3},{7,5},{8,14},{10,8},{12,... | collective-permute-start | bytes 737288 | tf_op jit(solution)/shard_map/ppermute | solution.py:81
  169.8 6.2 %collective-permute-done.20 = f32[24,5,512]{2,0,1:T(8,128)S(1)} collective-permute-done((f32[24,5,512]{2,0,1:T(8,128)S(1)}, f32[24,5,512]{2,0,1:T(8,128)S(1)}, u32[]{:S(2)}, u32[]{:S(2)}) %collective-permute-start.20) | collective-permute-done | bytes 245792 | tf_op jit(solution)/shard_map/ppermute | solution.py:80
  (113 shorter events, 38.6 us)
Async XLA Ops:
  12.6 24.6 %all-to-all-start = ((bf16[32,64,256]{2,1,0:T(8,128)(2,1)}), bf16[32,64,256]{2,1,0:T(8,128)(2,1)S(1)}, u32[]{:S(2)}, u32[]{:S(2)}) async-start(bf16[32,64,256]{2,1,0:T(8,128)(2,1)} %bitcast), calls=%async_computation | async-start | bytes 2097152 | tf_op jit(solution)/shard_map/all_to_all | solution.py:38
  21.6 155.8 %reduce-scatter.2.cloned.1.call-start = ((), (), s32[]{:S(2)}) async-start(), calls=%async_computation.2 | async-start | bytes 2654208 | tf_op jit(solution)/shard_map/reduce_scatter | solution.py:102
  37.9 5.1 %collective-permute-start = (bf16[4,64,256]{2,1,0:T(8,128)(2,1)S(1)}, bf16[4,64,256]{2,1,0:T(8,128)(2,1)S(1)}, u32[]{:S(2)}, u32[]{:S(2)}) collective-permute-start(bf16[4,64,256]{2,1,0:T(8,128)(2,1)S(1)} %broadcast_select_fusion), channel_id=1, source_target_pairs={{0,8},{8,0},{1,9},{9,1},{2,10},{10,2},{3,11},{11,3},{4,12},{12,4},... | collective-permute-start | bytes 393224 | tf_op jit(solution)/shard_map/ppermute | solution.py:42
  43.1 7.8 %collective-permute-start.9 = (bf16[2,2,64,256]{3,2,0,1:T(8,128)(2,1)S(1)}, bf16[2,2,64,256]{3,2,0,1:T(8,128)(2,1)S(1)}, u32[]{:S(2)}, u32[]{:S(2)}) collective-permute-start(bf16[2,2,64,256]{3,2,0,1:T(8,128)(2,1)S(1)} %get-tuple-element.24), channel_id=1, source_target_pairs={{0,48},{16,0},{32,16},{48,32},{1,49},{17,1},{33,17},{49,33},{2,50}... | collective-permute-start | bytes 393224 | tf_op jit(solution)/shard_map/ppermute | solution.py:17
  44.3 6.5 %collective-permute-start.10 = (bf16[2,2,64,256]{3,2,0,1:T(8,128)(2,1)S(1)}, bf16[2,2,64,256]{3,2,0,1:T(8,128)(2,1)S(1)}, u32[]{:S(2)}, u32[]{:S(2)}) collective-permute-start(bf16[2,2,64,256]{3,2,0,1:T(8,128)(2,1)S(1)} %get-tuple-element.24), channel_id=1, source_target_pairs={{0,16},{16,32},{32,48},{48,0},{1,17},{17,33},{33,49},{49,1},{2,18}... | collective-permute-start | bytes 393224 | tf_op jit(solution)/shard_map/ppermute | solution.py:16
  45.2 10.3 %collective-permute-start.1 = (bf16[2,2,64,256]{3,2,0,1:T(8,128)(2,1)S(1)}, bf16[2,2,64,256]{3,2,0,1:T(8,128)(2,1)S(1)}, u32[]{:S(2)}, u32[]{:S(2)}) collective-permute-start(bf16[2,2,64,256]{3,2,0,1:T(8,128)(2,1)S(1)} %get-tuple-element.23), channel_id=1, source_target_pairs={{0,192},{64,0},{128,64},{192,128},{1,193},{65,1},{129,65},{193,129... | collective-permute-start | bytes 393224 | tf_op jit(solution)/shard_map/ppermute | solution.py:17
  45.8 8.4 %collective-permute-start.2 = (bf16[2,2,64,256]{3,2,0,1:T(8,128)(2,1)S(1)}, bf16[2,2,64,256]{3,2,0,1:T(8,128)(2,1)S(1)}, u32[]{:S(2)}, u32[]{:S(2)}) collective-permute-start(bf16[2,2,64,256]{3,2,0,1:T(8,128)(2,1)S(1)} %get-tuple-element.23), channel_id=1, source_target_pairs={{0,64},{64,128},{128,192},{192,0},{1,65},{65,129},{129,193},{193,1... | collective-permute-start | bytes 393224 | tf_op jit(solution)/shard_map/ppermute | solution.py:16
  50.8 5.6 %collective-permute-start.11 = (bf16[1,2,64,256]{3,2,0,1:T(8,128)(2,1)S(1)}, bf16[1,2,64,256]{3,2,0,1:T(8,128)(2,1)S(1)}, u32[]{:S(2)}, u32[]{:S(2)}) collective-permute-start(bf16[1,2,64,256]{3,2,0,1:T(8,128)(2,1)S(1)} %slice.80), channel_id=1, source_target_pairs={{0,16},{16,32},{32,48},{48,0},{1,17},{17,33},{33,49},{49,1},{2,18}... | collective-permute-start | bytes 196616 | tf_op jit(solution)/shard_map/ppermute | solution.py:20
  50.9 5.5 %collective-permute-start.12 = (bf16[1,2,64,256]{3,2,0,1:T(8,128)(2,1)S(1)}, bf16[1,2,64,256]{3,2,0,1:T(8,128)(2,1)S(1)}, u32[]{:S(2)}, u32[]{:S(2)}) collective-permute-start(bf16[1,2,64,256]{3,2,0,1:T(8,128)(2,1)S(1)} %slice.81), channel_id=1, source_target_pairs={{0,48},{16,0},{32,16},{48,32},{1,49},{17,1},{33,17},{49,33},{2,50}... | collective-permute-start | bytes 196616 | tf_op jit(solution)/shard_map/ppermute | solution.py:20
  55.4 5.6 %collective-permute-start.4 = (bf16[1,2,64,256]{3,2,0,1:T(8,128)(2,1)S(1)}, bf16[1,2,64,256]{3,2,0,1:T(8,128)(2,1)S(1)}, u32[]{:S(2)}, u32[]{:S(2)}) collective-permute-start(bf16[1,2,64,256]{3,2,0,1:T(8,128)(2,1)S(1)} %slice.76), channel_id=1, source_target_pairs={{0,192},{64,0},{128,64},{192,128},{1,193},{65,1},{129,65},{193,129... | collective-permute-start | bytes 196616 | tf_op jit(solution)/shard_map/ppermute | solution.py:20
  62.1 15.7 %collective-permute-start.5 = (bf16[4,2,2,64,256]{4,3,1,2,0:T(8,128)(2,1)S(1)}, bf16[4,2,2,64,256]{4,3,1,2,0:T(8,128)(2,1)S(1)}, u32[]{:S(2)}, u32[]{:S(2)}) collective-permute-start(bf16[4,2,2,64,256]{4,3,1,2,0:T(8,128)(2,1)S(1)} %get-tuple-element.10), channel_id=1, source_target_pairs={{0,48},{16,0},{32,16},{48,32},{1,49},{17,1},{33,17},{49,33},{2,50}... | collective-permute-start | bytes 1572872 | tf_op jit(solution)/shard_map/ppermute | solution.py:17
  64.3 13.2 %collective-permute-start.6 = (bf16[4,2,2,64,256]{4,3,1,2,0:T(8,128)(2,1)S(1)}, bf16[4,2,2,64,256]{4,3,1,2,0:T(8,128)(2,1)S(1)}, u32[]{:S(2)}, u32[]{:S(2)}) collective-permute-start(bf16[4,2,2,64,256]{4,3,1,2,0:T(8,128)(2,1)S(1)} %get-tuple-element.10), channel_id=1, source_target_pairs={{0,16},{16,32},{32,48},{48,0},{1,17},{17,33},{33,49},{49,1},{2,18}... | collective-permute-start | bytes 1572872 | tf_op jit(solution)/shard_map/ppermute | solution.py:16
  65.3 15.9 %collective-permute-start.14 = (bf16[4,2,2,64,256]{4,3,1,2,0:T(8,128)(2,1)S(1)}, bf16[4,2,2,64,256]{4,3,1,2,0:T(8,128)(2,1)S(1)}, u32[]{:S(2)}, u32[]{:S(2)}) collective-permute-start(bf16[4,2,2,64,256]{4,3,1,2,0:T(8,128)(2,1)S(1)} %get-tuple-element.12), channel_id=1, source_target_pairs={{0,64},{64,128},{128,192},{192,0},{1,65},{65,129},{129,193},{193,1... | collective-permute-start | bytes 1572872 | tf_op jit(solution)/shard_map/ppermute | solution.py:16
  65.3 16.0 %collective-permute-start.13 = (bf16[4,2,2,64,256]{4,3,1,2,0:T(8,128)(2,1)S(1)}, bf16[4,2,2,64,256]{4,3,1,2,0:T(8,128)(2,1)S(1)}, u32[]{:S(2)}, u32[]{:S(2)}) collective-permute-start(bf16[4,2,2,64,256]{4,3,1,2,0:T(8,128)(2,1)S(1)} %get-tuple-element.12), channel_id=1, source_target_pairs={{0,192},{64,0},{128,64},{192,128},{1,193},{65,1},{129,65},{193,129... | collective-permute-start | bytes 1572872 | tf_op jit(solution)/shard_map/ppermute | solution.py:17
  77.5 7.8 %collective-permute-start.7 = (bf16[2,2,2,64,256]{4,3,1,2,0:T(8,128)(2,1)S(1)}, bf16[2,2,2,64,256]{4,3,1,2,0:T(8,128)(2,1)S(1)}, u32[]{:S(2)}, u32[]{:S(2)}) collective-permute-start(bf16[2,2,2,64,256]{4,3,1,2,0:T(8,128)(2,1)S(1)} %slice.77), channel_id=1, source_target_pairs={{0,16},{16,32},{32,48},{48,0},{1,17},{17,33},{33,49},{49,1},{2,18}... | collective-permute-start | bytes 786440 | tf_op jit(solution)/shard_map/ppermute | solution.py:20
  77.8 7.5 %collective-permute-start.8 = (bf16[2,2,2,64,256]{4,3,1,2,0:T(8,128)(2,1)S(1)}, bf16[2,2,2,64,256]{4,3,1,2,0:T(8,128)(2,1)S(1)}, u32[]{:S(2)}, u32[]{:S(2)}) collective-permute-start(bf16[2,2,2,64,256]{4,3,1,2,0:T(8,128)(2,1)S(1)} %slice.78), channel_id=1, source_target_pairs={{0,48},{16,0},{32,16},{48,32},{1,49},{17,1},{33,17},{49,33},{2,50}... | collective-permute-start | bytes 786440 | tf_op jit(solution)/shard_map/ppermute | solution.py:20
  81.1 6.7 %collective-permute-start.15 = (bf16[2,2,2,64,256]{4,3,1,2,0:T(8,128)(2,1)S(1)}, bf16[2,2,2,64,256]{4,3,1,2,0:T(8,128)(2,1)S(1)}, u32[]{:S(2)}, u32[]{:S(2)}) collective-permute-start(bf16[2,2,2,64,256]{4,3,1,2,0:T(8,128)(2,1)S(1)} %slice.82), channel_id=1, source_target_pairs={{0,64},{64,128},{128,192},{192,0},{1,65},{65,129},{129,193},{193,1... | collective-permute-start | bytes 786440 | tf_op jit(solution)/shard_map/ppermute | solution.py:20
  81.3 7.7 %collective-permute-start.16 = (bf16[2,2,2,64,256]{4,3,1,2,0:T(8,128)(2,1)S(1)}, bf16[2,2,2,64,256]{4,3,1,2,0:T(8,128)(2,1)S(1)}, u32[]{:S(2)}, u32[]{:S(2)}) collective-permute-start(bf16[2,2,2,64,256]{4,3,1,2,0:T(8,128)(2,1)S(1)} %slice.83), channel_id=1, source_target_pairs={{0,192},{64,0},{128,64},{192,128},{1,193},{65,1},{129,65},{193,129... | collective-permute-start | bytes 786440 | tf_op jit(solution)/shard_map/ppermute | solution.py:20
  118.9 26.4 %collective-permute-start.18 = (f32[24,5,512]{2,0,1:T(8,128)S(1)}, f32[24,5,512]{2,0,1:T(8,128)S(1)}, u32[]{:S(2)}, u32[]{:S(2)}) collective-permute-start(f32[24,5,512]{2,0,1:T(8,128)S(1)} %dynamic-slice_bitcast_fusion.2), channel_id=1, source_target_pairs={{0,2},{2,4},{4,6},{6,0},{1,3},{3,5},{5,7},{7,1},{8,10},{10,12},{12... | collective-permute-start | bytes 737288 | tf_op jit(solution)/shard_map/ppermute | solution.py:80
  122.5 23.0 %collective-permute-start.21 = (f32[24,5,512]{2,0,1:T(8,128)S(1)}, f32[24,5,512]{2,0,1:T(8,128)S(1)}, u32[]{:S(2)}, u32[]{:S(2)}) collective-permute-start(f32[24,5,512]{2,0,1:T(8,128)S(1)} %dynamic-slice_bitcast_fusion.1), channel_id=1, source_target_pairs={{0,6},{2,0},{4,2},{6,4},{1,7},{3,1},{5,3},{7,5},{8,14},{10,8},{12,... | collective-permute-start | bytes 737288 | tf_op jit(solution)/shard_map/ppermute | solution.py:81
  145.4 20.0 %collective-permute-start.19 = (f32[24,5,512]{2,0,1:T(8,128)S(1)}, f32[24,5,512]{2,0,1:T(8,128)S(1)}, u32[]{:S(2)}, u32[]{:S(2)}) collective-permute-start(f32[24,5,512]{2,0,1:T(8,128)S(1)} %bitcast_add_fusion.5), channel_id=1, source_target_pairs={{0,2},{2,4},{4,6},{6,0},{1,3},{3,5},{5,7},{7,1},{8,10},{10,12},{12... | collective-permute-start | bytes 737288 | tf_op jit(solution)/shard_map/ppermute | solution.py:80
  145.5 20.0 %collective-permute-start.22 = (f32[24,5,512]{2,0,1:T(8,128)S(1)}, f32[24,5,512]{2,0,1:T(8,128)S(1)}, u32[]{:S(2)}, u32[]{:S(2)}) collective-permute-start(f32[24,5,512]{2,0,1:T(8,128)S(1)} %bitcast_add_fusion.2), channel_id=1, source_target_pairs={{0,6},{2,0},{4,2},{6,4},{1,7},{3,1},{5,3},{7,5},{8,14},{10,8},{12,... | collective-permute-start | bytes 737288 | tf_op jit(solution)/shard_map/ppermute | solution.py:81
  165.5 10.5 %collective-permute-start.20 = (f32[24,5,512]{2,0,1:T(8,128)S(1)}, f32[24,5,512]{2,0,1:T(8,128)S(1)}, u32[]{:S(2)}, u32[]{:S(2)}) collective-permute-start(f32[24,5,512]{2,0,1:T(8,128)S(1)} %bitcast_add_fusion.4), channel_id=1, source_target_pairs={{0,2},{2,4},{4,6},{6,0},{1,3},{3,5},{5,7},{7,1},{8,10},{10,12},{12... | collective-permute-start | bytes 737288 | tf_op jit(solution)/shard_map/ppermute | solution.py:80
  165.6 11.8 %collective-permute-start.23 = (f32[24,5,512]{2,0,1:T(8,128)S(1)}, f32[24,5,512]{2,0,1:T(8,128)S(1)}, u32[]{:S(2)}, u32[]{:S(2)}) collective-permute-start(f32[24,5,512]{2,0,1:T(8,128)S(1)} %bitcast_add_fusion.1), channel_id=1, source_target_pairs={{0,6},{2,0},{4,2},{6,4},{1,7},{3,1},{5,3},{7,5},{8,14},{10,8},{12,... | collective-permute-start | bytes 737288 | tf_op jit(solution)/shard_map/ppermute | solution.py:81
  (8 other events, 43.4 us)
Sparse Core Ops, SparseCore 0:
  104.5 64.2 reduce-scatter.1

commit v13 on v12

--- a/solution.py
+++ b/solution.py
@@ -91,7 +91,7 @@
     weights = jnp.stack(
         [jnp.concatenate([real_in, imag_in], axis=-1), jnp.concatenate([-imag_in, real_in], axis=-1)], axis=0
     )
-    half = (3 * freq) // 8
+    half = (5 * freq) // 8
 
     def product(lo, hi):
         out = lax.dot_general(

time: 188 us -> 180 us (0.957)
  local copies, waits for them, and re-layouts: 21.1 us -> 9.61 us
  waiting for transfers between devices: 84.8 us -> 93.3 us
  other arithmetic: 10.7 us -> 5.42 us
    ppermute x3, waiting for transfers between devices: 42.3 us -> 5.92 us  [reduce_rows(): got_lo = lax.ppermute(acc_lo, 'zh', fwd)]
    reduce_scatter x1, waiting for transfers between devices: 0.02 us -> 23.8 us  [body(): lax.psum_scatter(product(0, half), SP, scatter_dimension=0, tiled=True)]
    ppermute x3, waiting for transfers between devices: 1.41 us -> 23.2 us  [reduce_rows(): got_hi = lax.ppermute(acc_hi, 'zh', bwd)]
    ppermute x4, waiting for transfers between devices: 11.4 us -> 0.01 us  [ring_gather(): from_left = lax.ppermute(piece, axis, fwd)]
    unnamed x30 -> x29, local copies, waits for them, and re-layouts: 12.8 us -> 4.01 us
    ppermute x4, waiting for transfers between devices: 0.01 us -> 8.17 us  [ring_gather(): from_right = lax.ppermute(piece, axis, bwd)]
    ppermute x4, starting transfers between devices: 1.72 us -> 9.06 us  [ring_gather(): lax.ppermute(from_left[:half], axis, fwd)]
    ppermute x4, starting transfers between devices: 9.49 us -> 2.2 us  [ring_gather(): lax.ppermute(from_right[half:], axis, bwd)]
  transfers between devices with their start and end apart: 26 -> 26, of which waited for: 13 -> 16; matrix products, arithmetic and copies ran while one was open for 9% -> 3% of each run, Pallas kernels for 0% -> 0%
where the time goes in v13:
time: 180 us
  waiting for transfers between devices  93.3 us (52%)
  starting transfers between devices  46.9 us (26%)
  between operations  16.1 us (9%)
  local copies, waits for them, and re-layouts  9.61 us (5%)
  matrix products  8.26 us (5%)
  other arithmetic  5.42 us (3%)
    reduce_scatter x1, waiting for transfers between devices, body(): lax.psum_scatter(product(0, half), SP, scatter_dimension=0, tiled=True)  23.8 us
    ppermute x3, waiting for transfers between devices, reduce_rows(): got_hi = lax.ppermute(acc_hi, 'zh', bwd)  23.2 us
    all_to_all x1, waiting for transfers between devices, gather_receivers(): got = lax.all_to_all(pieces, SHOT, 0, 0, tiled=True)  15.3 us
    ppermute x3, starting transfers between devices, reduce_rows(): got_hi = lax.ppermute(acc_hi, 'zh', bwd)  14.6 us
    ppermute x4, starting transfers between devices, ring_gather(): lax.ppermute(from_left[:half], axis, fwd)  9.06 us
    all_to_all x1, starting transfers between devices, gather_receivers(): got = lax.all_to_all(pieces, SHOT, 0, 0, tiled=True)  8.96 us
    ppermute x4, starting transfers between devices, ring_gather(): from_left = lax.ppermute(piece, axis, fwd)  8.74 us
    dot_general x2, matrix products, product(): lax.dot_general(live[:, lo:hi], weights[:, lo:hi], (((0, 3), (0, 2)), ((1...  8.26 us
  transfers between devices with their start and end apart: 26, of which 16 were waited for; matrix products, arithmetic and copies ran while one was open for 3% of the time, Pallas kernels for 0%

profile of v13, /device:TPU:6, one launch (start us, length us, event | category | flops | bytes accessed | tf_op | source)
XLA Modules:
  0.0 179.6 jit_solution(14570160236214180946)
XLA Ops:
  10.3 2.3 %constant_dynamic-slice_fusion.5 = bf16[1,2,8,128,256]{4,3,2,1,0:T(8,128)(2,1)} fusion(bf16[4,2,8,128,256]{4,3,2,1,0:T(8,128)(2,1)} %param.6, s32[]{:T(128)S(6)} %select_n.124), kind=kLoop, calls=%fused_computation.79 | loop fusion | bytes 2097156 | tf_op jit(solution)/shard_map/jit(dynamic_index_in_dim)/dynamic_slice | solution.py:34
  12.6 9.0 %all-to-all-start = ((bf16[32,64,256]{2,1,0:T(8,128)(2,1)}), bf16[32,64,256]{2,1,0:T(8,128)(2,1)S(1)}, u32[]{:S(2)}, u32[]{:S(2)}) async-start(bf16[32,64,256]{2,1,0:T(8,128)(2,1)} %bitcast), calls=%async_computation | async-start | bytes 2097152 | tf_op jit(solution)/shard_map/all_to_all | solution.py:38
  21.9 15.3 %all-to-all-done = bf16[32,64,256]{2,1,0:T(8,128)(2,1)S(1)} async-done(((bf16[32,64,256]{2,1,0:T(8,128)(2,1)}), bf16[32,64,256]{2,1,0:T(8,128)(2,1)S(1)}, u32[]{:S(2)}, u32[]{:S(2)}) %all-to-all-start) | async-done | bytes 1048608 | tf_op jit(solution)/shard_map/all_to_all | solution.py:38
  38.9 4.0 %collective-permute-done = bf16[4,64,256]{2,1,0:T(8,128)(2,1)S(1)} collective-permute-done((bf16[4,64,256]{2,1,0:T(8,128)(2,1)S(1)}, bf16[4,64,256]{2,1,0:T(8,128)(2,1)S(1)}, u32[]{:S(2)}, u32[]{:S(2)}) %collective-permute-start) | collective-permute-done | bytes 131104 | tf_op jit(solution)/shard_map/ppermute | solution.py:42
  43.7 2.6 %collective-permute-start.2 = (bf16[2,2,64,256]{3,2,0,1:T(8,128)(2,1)S(1)}, bf16[2,2,64,256]{3,2,0,1:T(8,128)(2,1)S(1)}, u32[]{:S(2)}, u32[]{:S(2)}) collective-permute-start(bf16[2,2,64,256]{3,2,0,1:T(8,128)(2,1)S(1)} %get-tuple-element.23), channel_id=1, source_target_pairs={{0,64},{64,128},{128,192},{192,0},{1,65},{65,129},{129,193},{193,1... | collective-permute-start | bytes 393224 | tf_op jit(solution)/shard_map/ppermute | solution.py:16
  49.4 3.3 %collective-permute-start.3 = (bf16[1,2,64,256]{3,2,0,1:T(8,128)(2,1)S(1)}, bf16[1,2,64,256]{3,2,0,1:T(8,128)(2,1)S(1)}, u32[]{:S(2)}, u32[]{:S(2)}) collective-permute-start(bf16[1,2,64,256]{3,2,0,1:T(8,128)(2,1)S(1)} %slice.75), channel_id=1, source_target_pairs={{0,64},{64,128},{128,192},{192,0},{1,65},{65,129},{129,193},{193,1... | collective-permute-start | bytes 196616 | tf_op jit(solution)/shard_map/ppermute | solution.py:20
  55.0 2.1 %collective-permute-done.12 = bf16[1,2,64,256]{3,2,0,1:T(8,128)(2,1)S(1)} collective-permute-done((bf16[1,2,64,256]{3,2,0,1:T(8,128)(2,1)S(1)}, bf16[1,2,64,256]{3,2,0,1:T(8,128)(2,1)S(1)}, u32[]{:S(2)}, u32[]{:S(2)}) %collective-permute-start.12) | collective-permute-done | bytes 65568 | tf_op jit(solution)/shard_map/ppermute | solution.py:20
  57.1 2.8 %collective-permute-done.11 = bf16[1,2,64,256]{3,2,0,1:T(8,128)(2,1)S(1)} collective-permute-done((bf16[1,2,64,256]{3,2,0,1:T(8,128)(2,1)S(1)}, bf16[1,2,64,256]{3,2,0,1:T(8,128)(2,1)S(1)}, u32[]{:S(2)}, u32[]{:S(2)}) %collective-permute-start.11) | collective-permute-done | bytes 65568 | tf_op jit(solution)/shard_map/ppermute | solution.py:20
  60.2 3.2 %collective-permute-start.14 = (bf16[4,2,2,64,256]{4,3,1,2,0:T(8,128)(2,1)S(1)}, bf16[4,2,2,64,256]{4,3,1,2,0:T(8,128)(2,1)S(1)}, u32[]{:S(2)}, u32[]{:S(2)}) collective-permute-start(bf16[4,2,2,64,256]{4,3,1,2,0:T(8,128)(2,1)S(1)} %get-tuple-element.12), channel_id=1, source_target_pairs={{0,64},{64,128},{128,192},{192,0},{1,65},{65,129},{129,193},{193,1... | collective-permute-start | bytes 1572872 | tf_op jit(solution)/shard_map/ppermute | solution.py:16
  65.7 7.3 %collective-permute-done.13 = bf16[4,2,2,64,256]{4,3,1,2,0:T(8,128)(2,1)S(1)} collective-permute-done((bf16[4,2,2,64,256]{4,3,1,2,0:T(8,128)(2,1)S(1)}, bf16[4,2,2,64,256]{4,3,1,2,0:T(8,128)(2,1)S(1)}, u32[]{:S(2)}, u32[]{:S(2)}) %collective-permute-start.13) | collective-permute-done | bytes 524320 | tf_op jit(solution)/shard_map/ppermute | solution.py:17
  73.3 3.3 %collective-permute-start.15 = (bf16[2,2,2,64,256]{4,3,1,2,0:T(8,128)(2,1)S(1)}, bf16[2,2,2,64,256]{4,3,1,2,0:T(8,128)(2,1)S(1)}, u32[]{:S(2)}, u32[]{:S(2)}) collective-permute-start(bf16[2,2,2,64,256]{4,3,1,2,0:T(8,128)(2,1)S(1)} %slice.82), channel_id=1, source_target_pairs={{0,64},{64,128},{128,192},{192,0},{1,65},{65,129},{129,193},{193,1... | collective-permute-start | bytes 786440 | tf_op jit(solution)/shard_map/ppermute | solution.py:20
  87.1 2.1 %copy-done = bf16[1,8,512,512]{3,2,0,1:T(8,128)(2,1)} copy-done((bf16[1,8,512,512]{3,2,0,1:T(8,128)(2,1)}, bf16[1,8,512,512]{3,2,0,1:T(8,128)(2,1)S(1)}, u32[]{:S(2)}) %copy-start) | copy-done | bytes 4194328
  90.5 4.3 %fusion.7 = f32[384,5,512]{2,0,1:T(8,128)} fusion(bf16[1,8,512,512]{3,2,0,1:T(8,128)(2,1)S(1)} %get-tuple-element.17, bf16[1,8,512,512]{3,2,0,1:T(8,128)(2,1)S(1)} %get-tuple-element.18, bf16[2,8,384,512]{3,2,1,0:T(8,128)(2,1)S(1)} %bitcast.134, bf16[384,512]{1,0:T(8,128)(2,1)S(1)} %convert_element_type.7), kind=kOutput, calls=%fused_computation.15 | convolution fusion | flops 2036334592 | bytes 19005440 | tf_op jit(solution)/shard_map/dot_general | solution.py:97
  94.8 4.0 %fusion.3 = f32[3,384,512,1]{2,1,3,0:T(8,128)S(1)} fusion(bf16[2,8,384,512]{3,2,1,0:T(8,128)(2,1)} %param.4, bf16[1,8,512,512]{3,2,0,1:T(8,128)(2,1)} %copy-done.1, bf16[1,8,512,512]{3,2,0,1:T(8,128)(2,1)} %copy-done, bf16[384,512]{1,0:T(8,128)(2,1)S(1)} %convert_element_type.7), kind=kOutput, calls=%fused_computation.6 | convolution fusion | flops 1226833920 | bytes 17432576 | tf_op jit(solution)/shard_map/dot_general | solution.py:97
  99.2 2.8 %collective-permute-done.17 = f32[4,48,3,512]{3,1,2,0:T(8,128)S(1)} collective-permute-done((f32[4,48,3,512]{3,1,2,0:T(8,128)S(1)}, f32[4,48,3,512]{3,1,2,0:T(8,128)S(1)}, u32[]{:S(2)}, u32[]{:S(2)}) %collective-permute-start.17) | collective-permute-done | bytes 1179680 | tf_op jit(solution)/shard_map/ppermute | solution.py:67
  102.4 5.5 %collective-permute-start.21 = (f32[24,3,512]{2,0,1:T(8,128)S(1)}, f32[24,3,512]{2,0,1:T(8,128)S(1)}, u32[]{:S(2)}, u32[]{:S(2)}) collective-permute-start(f32[24,3,512]{2,0,1:T(8,128)S(1)} %dynamic-slice_bitcast_fusion.1), channel_id=1, source_target_pairs={{0,6},{2,0},{4,2},{6,4},{1,7},{3,1},{5,3},{7,5},{8,14},{10,8},{12,... | collective-permute-start | bytes 442376 | tf_op jit(solution)/shard_map/ppermute | solution.py:81
  108.0 10.0 %collective-permute-done.21 = f32[24,3,512]{2,0,1:T(8,128)S(1)} collective-permute-done((f32[24,3,512]{2,0,1:T(8,128)S(1)}, f32[24,3,512]{2,0,1:T(8,128)S(1)}, u32[]{:S(2)}, u32[]{:S(2)}) %collective-permute-start.21) | collective-permute-done | bytes 147488 | tf_op jit(solution)/shard_map/ppermute | solution.py:81
  118.0 4.2 %collective-permute-start.22 = (f32[24,3,512]{2,0,1:T(8,128)S(1)}, f32[24,3,512]{2,0,1:T(8,128)S(1)}, u32[]{:S(2)}, u32[]{:S(2)}) collective-permute-start(f32[24,3,512]{2,0,1:T(8,128)S(1)} %bitcast_add_fusion.3), channel_id=1, source_target_pairs={{0,6},{2,0},{4,2},{6,4},{1,7},{3,1},{5,3},{7,5},{8,14},{10,8},{12,... | collective-permute-start | bytes 442376 | tf_op jit(solution)/shard_map/ppermute | solution.py:81
  122.3 3.1 %collective-permute-done.18 = f32[24,3,512]{2,0,1:T(8,128)S(1)} collective-permute-done((f32[24,3,512]{2,0,1:T(8,128)S(1)}, f32[24,3,512]{2,0,1:T(8,128)S(1)}, u32[]{:S(2)}, u32[]{:S(2)}) %collective-permute-start.18) | collective-permute-done | bytes 147488 | tf_op jit(solution)/shard_map/ppermute | solution.py:80
  125.5 2.9 %collective-permute-done.22 = f32[24,3,512]{2,0,1:T(8,128)S(1)} collective-permute-done((f32[24,3,512]{2,0,1:T(8,128)S(1)}, f32[24,3,512]{2,0,1:T(8,128)S(1)}, u32[]{:S(2)}, u32[]{:S(2)}) %collective-permute-start.22) | collective-permute-done | bytes 147488 | tf_op jit(solution)/shard_map/ppermute | solution.py:81
  128.5 4.9 %collective-permute-start.23 = (f32[24,3,512]{2,0,1:T(8,128)S(1)}, f32[24,3,512]{2,0,1:T(8,128)S(1)}, u32[]{:S(2)}, u32[]{:S(2)}) collective-permute-start(f32[24,3,512]{2,0,1:T(8,128)S(1)} %bitcast_add_fusion.2), channel_id=1, source_target_pairs={{0,6},{2,0},{4,2},{6,4},{1,7},{3,1},{5,3},{7,5},{8,14},{10,8},{12,... | collective-permute-start | bytes 442376 | tf_op jit(solution)/shard_map/ppermute | solution.py:81
  133.5 10.3 %collective-permute-done.23 = f32[24,3,512]{2,0,1:T(8,128)S(1)} collective-permute-done((f32[24,3,512]{2,0,1:T(8,128)S(1)}, f32[24,3,512]{2,0,1:T(8,128)S(1)}, u32[]{:S(2)}, u32[]{:S(2)}) %collective-permute-start.23) | collective-permute-done | bytes 147488 | tf_op jit(solution)/shard_map/ppermute | solution.py:81
  143.8 2.8 %collective-permute-done.20 = f32[24,3,512]{2,0,1:T(8,128)S(1)} collective-permute-done((f32[24,3,512]{2,0,1:T(8,128)S(1)}, f32[24,3,512]{2,0,1:T(8,128)S(1)}, u32[]{:S(2)}, u32[]{:S(2)}) %collective-permute-start.20) | collective-permute-done | bytes 147488 | tf_op jit(solution)/shard_map/ppermute | solution.py:80
  146.6 23.8 %reduce-scatter.2.cloned.1.call-done = f32[48,5,512]{2,0,1:T(8,128)} async-done(((f32[384,5,512]{2,0,1:T(8,128)}), f32[48,5,512]{2,0,1:T(8,128)}) %reduce-scatter.2.cloned.1.call-update) | async-done | bytes 491536 | tf_op jit(solution)/shard_map/reduce_scatter | solution.py:102
  (113 shorter events, 27.5 us)
Async XLA Ops:
  12.6 24.6 %all-to-all-start = ((bf16[32,64,256]{2,1,0:T(8,128)(2,1)}), bf16[32,64,256]{2,1,0:T(8,128)(2,1)S(1)}, u32[]{:S(2)}, u32[]{:S(2)}) async-start(bf16[32,64,256]{2,1,0:T(8,128)(2,1)} %bitcast), calls=%async_computation | async-start | bytes 2097152 | tf_op jit(solution)/shard_map/all_to_all | solution.py:38
  21.6 148.8 %reduce-scatter.2.cloned.1.call-start = ((), (), s32[]{:S(2)}) async-start(), calls=%async_computation.2 | async-start | bytes 4423680 | tf_op jit(solution)/shard_map/reduce_scatter | solution.py:102
  37.9 5.1 %collective-permute-start = (bf16[4,64,256]{2,1,0:T(8,128)(2,1)S(1)}, bf16[4,64,256]{2,1,0:T(8,128)(2,1)S(1)}, u32[]{:S(2)}, u32[]{:S(2)}) collective-permute-start(bf16[4,64,256]{2,1,0:T(8,128)(2,1)S(1)} %broadcast_select_fusion), channel_id=1, source_target_pairs={{0,8},{8,0},{1,9},{9,1},{2,10},{10,2},{3,11},{11,3},{4,12},{12,4},... | collective-permute-start | bytes 393224 | tf_op jit(solution)/shard_map/ppermute | solution.py:42
  43.1 6.3 %collective-permute-start.1 = (bf16[2,2,64,256]{3,2,0,1:T(8,128)(2,1)S(1)}, bf16[2,2,64,256]{3,2,0,1:T(8,128)(2,1)S(1)}, u32[]{:S(2)}, u32[]{:S(2)}) collective-permute-start(bf16[2,2,64,256]{3,2,0,1:T(8,128)(2,1)S(1)} %get-tuple-element.23), channel_id=1, source_target_pairs={{0,192},{64,0},{128,64},{192,128},{1,193},{65,1},{129,65},{193,129... | collective-permute-start | bytes 393224 | tf_op jit(solution)/shard_map/ppermute | solution.py:17
  43.7 5.6 %collective-permute-start.2 = (bf16[2,2,64,256]{3,2,0,1:T(8,128)(2,1)S(1)}, bf16[2,2,64,256]{3,2,0,1:T(8,128)(2,1)S(1)}, u32[]{:S(2)}, u32[]{:S(2)}) collective-permute-start(bf16[2,2,64,256]{3,2,0,1:T(8,128)(2,1)S(1)} %get-tuple-element.23), channel_id=1, source_target_pairs={{0,64},{64,128},{128,192},{192,0},{1,65},{65,129},{129,193},{193,1... | collective-permute-start | bytes 393224 | tf_op jit(solution)/shard_map/ppermute | solution.py:16
  46.4 6.3 %collective-permute-start.9 = (bf16[2,2,64,256]{3,2,0,1:T(8,128)(2,1)S(1)}, bf16[2,2,64,256]{3,2,0,1:T(8,128)(2,1)S(1)}, u32[]{:S(2)}, u32[]{:S(2)}) collective-permute-start(bf16[2,2,64,256]{3,2,0,1:T(8,128)(2,1)S(1)} %get-tuple-element.24), channel_id=1, source_target_pairs={{0,48},{16,0},{32,16},{48,32},{1,49},{17,1},{33,17},{49,33},{2,50}... | collective-permute-start | bytes 393224 | tf_op jit(solution)/shard_map/ppermute | solution.py:17
  47.6 6.8 %collective-permute-start.10 = (bf16[2,2,64,256]{3,2,0,1:T(8,128)(2,1)S(1)}, bf16[2,2,64,256]{3,2,0,1:T(8,128)(2,1)S(1)}, u32[]{:S(2)}, u32[]{:S(2)}) collective-permute-start(bf16[2,2,64,256]{3,2,0,1:T(8,128)(2,1)S(1)} %get-tuple-element.24), channel_id=1, source_target_pairs={{0,16},{16,32},{32,48},{48,0},{1,17},{17,33},{33,49},{49,1},{2,18}... | collective-permute-start | bytes 393224 | tf_op jit(solution)/shard_map/ppermute | solution.py:16
  49.3 5.6 %collective-permute-start.4 = (bf16[1,2,64,256]{3,2,0,1:T(8,128)(2,1)S(1)}, bf16[1,2,64,256]{3,2,0,1:T(8,128)(2,1)S(1)}, u32[]{:S(2)}, u32[]{:S(2)}) collective-permute-start(bf16[1,2,64,256]{3,2,0,1:T(8,128)(2,1)S(1)} %slice.76), channel_id=1, source_target_pairs={{0,192},{64,0},{128,64},{192,128},{1,193},{65,1},{129,65},{193,129... | collective-permute-start | bytes 196616 | tf_op jit(solution)/shard_map/ppermute | solution.py:20
  49.4 5.6 %collective-permute-start.3 = (bf16[1,2,64,256]{3,2,0,1:T(8,128)(2,1)S(1)}, bf16[1,2,64,256]{3,2,0,1:T(8,128)(2,1)S(1)}, u32[]{:S(2)}, u32[]{:S(2)}) collective-permute-start(bf16[1,2,64,256]{3,2,0,1:T(8,128)(2,1)S(1)} %slice.75), channel_id=1, source_target_pairs={{0,64},{64,128},{128,192},{192,0},{1,65},{65,129},{129,193},{193,1... | collective-permute-start | bytes 196616 | tf_op jit(solution)/shard_map/ppermute | solution.py:20
  54.4 5.6 %collective-permute-start.11 = (bf16[1,2,64,256]{3,2,0,1:T(8,128)(2,1)S(1)}, bf16[1,2,64,256]{3,2,0,1:T(8,128)(2,1)S(1)}, u32[]{:S(2)}, u32[]{:S(2)}) collective-permute-start(bf16[1,2,64,256]{3,2,0,1:T(8,128)(2,1)S(1)} %slice.80), channel_id=1, source_target_pairs={{0,16},{16,32},{32,48},{48,0},{1,17},{17,33},{33,49},{49,1},{2,18}... | collective-permute-start | bytes 196616 | tf_op jit(solution)/shard_map/ppermute | solution.py:20
  60.1 12.9 %collective-permute-start.13 = (bf16[4,2,2,64,256]{4,3,1,2,0:T(8,128)(2,1)S(1)}, bf16[4,2,2,64,256]{4,3,1,2,0:T(8,128)(2,1)S(1)}, u32[]{:S(2)}, u32[]{:S(2)}) collective-permute-start(bf16[4,2,2,64,256]{4,3,1,2,0:T(8,128)(2,1)S(1)} %get-tuple-element.12), channel_id=1, source_target_pairs={{0,192},{64,0},{128,64},{192,128},{1,193},{65,1},{129,65},{193,129... | collective-permute-start | bytes 1572872 | tf_op jit(solution)/shard_map/ppermute | solution.py:17
  60.2 13.1 %collective-permute-start.14 = (bf16[4,2,2,64,256]{4,3,1,2,0:T(8,128)(2,1)S(1)}, bf16[4,2,2,64,256]{4,3,1,2,0:T(8,128)(2,1)S(1)}, u32[]{:S(2)}, u32[]{:S(2)}) collective-permute-start(bf16[4,2,2,64,256]{4,3,1,2,0:T(8,128)(2,1)S(1)} %get-tuple-element.12), channel_id=1, source_target_pairs={{0,64},{64,128},{128,192},{192,0},{1,65},{65,129},{129,193},{193,1... | collective-permute-start | bytes 1572872 | tf_op jit(solution)/shard_map/ppermute | solution.py:16
  63.6 13.1 %collective-permute-start.5 = (bf16[4,2,2,64,256]{4,3,1,2,0:T(8,128)(2,1)S(1)}, bf16[4,2,2,64,256]{4,3,1,2,0:T(8,128)(2,1)S(1)}, u32[]{:S(2)}, u32[]{:S(2)}) collective-permute-start(bf16[4,2,2,64,256]{4,3,1,2,0:T(8,128)(2,1)S(1)} %get-tuple-element.10), channel_id=1, source_target_pairs={{0,48},{16,0},{32,16},{48,32},{1,49},{17,1},{33,17},{49,33},{2,50}... | collective-permute-start | bytes 1572872 | tf_op jit(solution)/shard_map/ppermute | solution.py:17
  63.7 13.3 %collective-permute-start.6 = (bf16[4,2,2,64,256]{4,3,1,2,0:T(8,128)(2,1)S(1)}, bf16[4,2,2,64,256]{4,3,1,2,0:T(8,128)(2,1)S(1)}, u32[]{:S(2)}, u32[]{:S(2)}) collective-permute-start(bf16[4,2,2,64,256]{4,3,1,2,0:T(8,128)(2,1)S(1)} %get-tuple-element.10), channel_id=1, source_target_pairs={{0,16},{16,32},{32,48},{48,0},{1,17},{17,33},{33,49},{49,1},{2,18}... | collective-permute-start | bytes 1572872 | tf_op jit(solution)/shard_map/ppermute | solution.py:16
  73.0 7.8 %collective-permute-start.16 = (bf16[2,2,2,64,256]{4,3,1,2,0:T(8,128)(2,1)S(1)}, bf16[2,2,2,64,256]{4,3,1,2,0:T(8,128)(2,1)S(1)}, u32[]{:S(2)}, u32[]{:S(2)}) collective-permute-start(bf16[2,2,2,64,256]{4,3,1,2,0:T(8,128)(2,1)S(1)} %slice.83), channel_id=1, source_target_pairs={{0,192},{64,0},{128,64},{192,128},{1,193},{65,1},{129,65},{193,129... | collective-permute-start | bytes 786440 | tf_op jit(solution)/shard_map/ppermute | solution.py:20
  73.3 7.5 %collective-permute-start.15 = (bf16[2,2,2,64,256]{4,3,1,2,0:T(8,128)(2,1)S(1)}, bf16[2,2,2,64,256]{4,3,1,2,0:T(8,128)(2,1)S(1)}, u32[]{:S(2)}, u32[]{:S(2)}) collective-permute-start(bf16[2,2,2,64,256]{4,3,1,2,0:T(8,128)(2,1)S(1)} %slice.82), channel_id=1, source_target_pairs={{0,64},{64,128},{128,192},{192,0},{1,65},{65,129},{129,193},{193,1... | collective-permute-start | bytes 786440 | tf_op jit(solution)/shard_map/ppermute | solution.py:20
  76.6 6.4 %collective-permute-start.8 = (bf16[2,2,2,64,256]{4,3,1,2,0:T(8,128)(2,1)S(1)}, bf16[2,2,2,64,256]{4,3,1,2,0:T(8,128)(2,1)S(1)}, u32[]{:S(2)}, u32[]{:S(2)}) collective-permute-start(bf16[2,2,2,64,256]{4,3,1,2,0:T(8,128)(2,1)S(1)} %slice.78), channel_id=1, source_target_pairs={{0,48},{16,0},{32,16},{48,32},{1,49},{17,1},{33,17},{49,33},{2,50}... | collective-permute-start | bytes 786440 | tf_op jit(solution)/shard_map/ppermute | solution.py:20
  77.0 7.7 %collective-permute-start.7 = (bf16[2,2,2,64,256]{4,3,1,2,0:T(8,128)(2,1)S(1)}, bf16[2,2,2,64,256]{4,3,1,2,0:T(8,128)(2,1)S(1)}, u32[]{:S(2)}, u32[]{:S(2)}) collective-permute-start(bf16[2,2,2,64,256]{4,3,1,2,0:T(8,128)(2,1)S(1)} %slice.77), channel_id=1, source_target_pairs={{0,16},{16,32},{32,48},{48,0},{1,17},{17,33},{33,49},{49,1},{2,18}... | collective-permute-start | bytes 786440 | tf_op jit(solution)/shard_map/ppermute | solution.py:20
  102.4 15.6 %collective-permute-start.21 = (f32[24,3,512]{2,0,1:T(8,128)S(1)}, f32[24,3,512]{2,0,1:T(8,128)S(1)}, u32[]{:S(2)}, u32[]{:S(2)}) collective-permute-start(f32[24,3,512]{2,0,1:T(8,128)S(1)} %dynamic-slice_bitcast_fusion.1), channel_id=1, source_target_pairs={{0,6},{2,0},{4,2},{6,4},{1,7},{3,1},{5,3},{7,5},{8,14},{10,8},{12,... | collective-permute-start | bytes 442376 | tf_op jit(solution)/shard_map/ppermute | solution.py:81
  107.9 17.5 %collective-permute-start.18 = (f32[24,3,512]{2,0,1:T(8,128)S(1)}, f32[24,3,512]{2,0,1:T(8,128)S(1)}, u32[]{:S(2)}, u32[]{:S(2)}) collective-permute-start(f32[24,3,512]{2,0,1:T(8,128)S(1)} %dynamic-slice_bitcast_fusion.2), channel_id=1, source_target_pairs={{0,2},{2,4},{4,6},{6,0},{1,3},{3,5},{5,7},{7,1},{8,10},{10,12},{12... | collective-permute-start | bytes 442376 | tf_op jit(solution)/shard_map/ppermute | solution.py:80
  118.0 10.4 %collective-permute-start.22 = (f32[24,3,512]{2,0,1:T(8,128)S(1)}, f32[24,3,512]{2,0,1:T(8,128)S(1)}, u32[]{:S(2)}, u32[]{:S(2)}) collective-permute-start(f32[24,3,512]{2,0,1:T(8,128)S(1)} %bitcast_add_fusion.3), channel_id=1, source_target_pairs={{0,6},{2,0},{4,2},{6,4},{1,7},{3,1},{5,3},{7,5},{8,14},{10,8},{12,... | collective-permute-start | bytes 442376 | tf_op jit(solution)/shard_map/ppermute | solution.py:81
  125.4 8.0 %collective-permute-start.19 = (f32[24,3,512]{2,0,1:T(8,128)S(1)}, f32[24,3,512]{2,0,1:T(8,128)S(1)}, u32[]{:S(2)}, u32[]{:S(2)}) collective-permute-start(f32[24,3,512]{2,0,1:T(8,128)S(1)} %bitcast_add_fusion.6), channel_id=1, source_target_pairs={{0,2},{2,4},{4,6},{6,0},{1,3},{3,5},{5,7},{7,1},{8,10},{10,12},{12... | collective-permute-start | bytes 442376 | tf_op jit(solution)/shard_map/ppermute | solution.py:80
  128.5 15.3 %collective-permute-start.23 = (f32[24,3,512]{2,0,1:T(8,128)S(1)}, f32[24,3,512]{2,0,1:T(8,128)S(1)}, u32[]{:S(2)}, u32[]{:S(2)}) collective-permute-start(f32[24,3,512]{2,0,1:T(8,128)S(1)} %bitcast_add_fusion.2), channel_id=1, source_target_pairs={{0,6},{2,0},{4,2},{6,4},{1,7},{3,1},{5,3},{7,5},{8,14},{10,8},{12,... | collective-permute-start | bytes 442376 | tf_op jit(solution)/shard_map/ppermute | solution.py:81
  133.4 13.2 %collective-permute-start.20 = (f32[24,3,512]{2,0,1:T(8,128)S(1)}, f32[24,3,512]{2,0,1:T(8,128)S(1)}, u32[]{:S(2)}, u32[]{:S(2)}) collective-permute-start(f32[24,3,512]{2,0,1:T(8,128)S(1)} %bitcast_add_fusion.5), channel_id=1, source_target_pairs={{0,2},{2,4},{4,6},{6,0},{1,3},{3,5},{5,7},{7,1},{8,10},{10,12},{12... | collective-permute-start | bytes 442376 | tf_op jit(solution)/shard_map/ppermute | solution.py:80
  (8 other events, 59.5 us)
Sparse Core Ops, SparseCore 0:
  94.9 75.3 reduce-scatter.1
